TPU v7x, 512 devices: a whole 4x4x16 slice. The times are simulated.
512 devices in a mesh: req: 32 (over x, y, core), ctx: 16 (over z).
Axes of the slice: x: 4, y: 4, z: 16, core: 2. Of those that a mesh axis runs over, the one named last changes fastest.
Arguments:
- queries: bfloat16 [64, 48, 8192], P('req', None, 'ctx'), parts along dimension 0, may hold values from -120 to 120
- key_cache: bfloat16 [64, 2048, 1024], P('req', 'ctx'), parts along dimension 0, may hold values from -5 to 5
- value_cache: bfloat16 [64, 2048, 1024], P('req', 'ctx'), parts along dimension 0, may hold values from -6 to 6
- draft_keys: bfloat16 [64, 48, 1024], P('req', None, 'ctx'), parts along dimension 0, may hold values from -12 to 12
- draft_values: bfloat16 [64, 48, 1024], P('req', None, 'ctx'), parts along dimension 0, may hold values from -6 to 6
- ancestors: int32 [64, 24, 24], P('req'), parts along dimension 0, may hold values from 0 to 1, as said below
- context_length: int32 [32], P('req'), parts along dimension 0, may hold values from 1025 to 2048
Outputs:
- attention: float32 [64, 48, 8192], P('req', None, 'ctx'), parts along dimension 0
There are 32 independent parts, one for each index of `req`. A program takes and returns all parts, laid end to end along the dimension named above; each array names one. Nothing has to cross between parts.
Inputs may be any that keep to these rules, and one draw needn't show every extreme that they name: ancestors[t, n, j] is 1 exactly where node j of tree t is node n itself or one of its ancestors; node 0 is the root of every tree and every other node's parent has a lower number.
All inputs are finite; a program needn't handle non-finite values.
Results may differ from a plain program's by a relative error of at most 0.005.
Values may be sent and summed in bfloat16 or wider, within the bound.
No kernel may reach another device: no remote copies, remote signals or barrier semaphores. Data moves between devices by JAX's collectives and lax.ppermute only.
A program may use at most 64 MiB of HBM per device.

v0:
```python
import math

import jax
import jax.numpy as jnp
from jax import lax
from jax.sharding import PartitionSpec as P

H = 64
KVH = 8
DH = 128


masked_score = -1e30


def sent_together(arrays, axis, dim, along):
    ends, at = ([], 0)
    for a in arrays[:-1]:
        at += a.shape[along]
        ends.append(at)
    both = jnp.concatenate(arrays, axis=along)
    return tuple(jnp.split(lax.all_gather(both, axis, axis=dim, tiled=True), ends, axis=along))


def block_partial(
    query_heads, block_keys, block_values, draft_k, draft_v, cache_keep, draft_keep, score_scale
):
    scores = (
        jnp.einsum("qkjd,pkd->kqjp", query_heads, block_keys, preferred_element_type=jnp.float32)
        * score_scale
    )
    draft_scores = (
        jnp.einsum("qkjd,tkd->kqjt", query_heads, draft_k, preferred_element_type=jnp.float32)
        * score_scale
    )
    scores = jnp.where(cache_keep[None, None, None, :], scores, masked_score)
    draft_scores = jnp.where(draft_keep[None, :, None, :], draft_scores, masked_score)
    top_score = jnp.maximum(jnp.max(scores, -1), jnp.max(draft_scores, -1))
    shift_by = jnp.where(top_score > -1e29, top_score, 0.0)
    cache_weight = jnp.exp(scores - shift_by[..., None])
    draft_weight = jnp.exp(draft_scores - shift_by[..., None])
    total = jnp.sum(cache_weight, -1) + jnp.sum(draft_weight, -1)
    weighted = jnp.einsum(
        "kqjp,pkd->qkjd",
        cache_weight.astype(jnp.bfloat16),
        block_values,
        preferred_element_type=jnp.float32,
    )
    weighted = weighted + jnp.einsum(
        "kqjt,tkd->qkjd",
        draft_weight.astype(jnp.bfloat16),
        draft_v,
        preferred_element_type=jnp.float32,
    )
    top_score = jnp.transpose(top_score, (1, 0, 2))
    total = jnp.transpose(total, (1, 0, 2))
    alive = total > 0.0
    safe_total = jnp.where(alive, total, 1.0)
    output = jnp.where(alive[..., None], weighted / safe_total[..., None], 0.0).astype(jnp.bfloat16)
    lse = jnp.where(alive, top_score + jnp.log(safe_total), masked_score)
    return (lse, output)


def body(queries, key_cache, value_cache, draft_keys, draft_values, ancestors, context_length):
    devices = lax.axis_size("ctx")
    device_index = lax.axis_index("ctx")
    gathered_q, gathered_k, gathered_v = (
        lax.all_gather(queries, "ctx", axis=2, tiled=True),
        *sent_together((draft_keys, draft_values), "ctx", 2, 0),
    )
    layers = gathered_q.shape[0]
    rows = gathered_q.shape[1]
    local_len = key_cache.shape[1]
    trees = ancestors.shape[0]
    group_size = H // KVH
    score_scale = 1.0 / math.sqrt(DH)
    heads_here = H // devices
    tree_keep = (
        jnp.eye(trees, dtype=jnp.int32)[:, None, :, None] * ancestors[:, :, None, :]
    ).reshape(rows, rows) > 0
    draft_keep = jnp.logical_and(tree_keep, device_index == 0)
    cache_keep = (
        device_index * local_len + jnp.arange(local_len, dtype=jnp.int32) < context_length[0]
    )
    results = []
    for layer_index in range(layers):
        query_heads = gathered_q[layer_index].reshape(rows, KVH, group_size, DH)
        lse, output = block_partial(
            query_heads,
            key_cache[layer_index].reshape(local_len, KVH, DH),
            value_cache[layer_index].reshape(local_len, KVH, DH),
            gathered_k[layer_index].reshape(rows, KVH, DH),
            gathered_v[layer_index].reshape(rows, KVH, DH),
            cache_keep,
            draft_keep,
            score_scale,
        )
        lse = lse.reshape(rows, H)
        output = output.reshape(rows, H, DH).astype(jnp.float32)
        lses, outputs = (
            lax.all_to_all(lse[None], "ctx", split_axis=2, concat_axis=0, tiled=True),
            lax.all_to_all(output[None], "ctx", split_axis=2, concat_axis=0, tiled=True),
        )
        overall = jnp.max(lses, 0)
        factor = jnp.exp(lses - overall)
        total_mine = jnp.sum(factor, 0)
        weighted_mine = jnp.sum(factor[..., None] * outputs, 0)
        mine = weighted_mine / total_mine[..., None]
        results.append(mine.reshape(rows, heads_here * DH))
    return jnp.stack(results)


def solution(mesh):
    placed = (
        P("req", None, "ctx"),
        P("req", "ctx", None),
        P("req", "ctx", None),
        P("req", None, "ctx"),
        P("req", None, "ctx"),
        P("req", None, None),
        P("req"),
    )
    return jax.shard_map(
        body, mesh=mesh, in_specs=placed, out_specs=P("req", None, "ctx"), check_vma=False
    )
```

profile of v0, /device:TPU:6, one launch (start us, length us, event | category | flops | bytes accessed | tf_op | source)
XLA Modules:
  0.0 295.3 jit_solution(13309664191307874075)
XLA Ops:
  15.1 43.3 %all_gather.7 = bf16[4,48,1024]{1,0,2:T(4,128)(2,1)S(1)} all-gather(bf16[4,48,64]{1,0,2:T(4,128)(2,1)S(1)} %pad_maximum_fusion.1), channel_id=1, replica_groups=mesh['req'=32,'ctx'=16] {'ctx'}, dimensions={2}, use_global_device_ids=true | all-gather | bytes 417792 | tf_op jit(solution)/shard_map/all_gather | solution.py:22
  58.4 2.2 fusion.34
  62.9 23.9 %all-gather.2.cloned.1.call-done = bf16[2,48,8192]{2,1,0:T(8,128)(2,1)} async-done(((bf16[2,48,512]{2,1,0:T(8,128)(2,1)}), bf16[2,48,8192]{2,1,0:T(8,128)(2,1)}) %all-gather.2.cloned.1.call-update) | async-done | bytes 1572880 | tf_op jit(solution)/shard_map/all_gather | solution.py:68
  88.6 2.2 fusion.40
  91.0 1.6 fusion.39
  92.7 2.7 fusion.11
  96.4 1.8 fusion.18
  101.1 7.8 %all-to-all-start = ((f32[16,1,192]{2,1,0:T(1,128)}), f32[16,1,192]{2,1,0:T(1,128)S(1)}, u32[]{:S(2)}, u32[]{:S(2)}) async-start(f32[16,1,192]{2,1,0:T(1,128)} %reshape.145), calls=%async_computation | async-start | bytes 32768 | tf_op jit(solution)/shard_map/all_to_all | solution.py:101
  109.0 2.2 fusion.38
  112.1 2.7 fusion.15
  119.4 2.0 all-to-all-done
  121.5 10.0 %all-to-all-start.2 = ((f32[16,1,192]{2,1,0:T(1,128)}), f32[16,1,192]{2,1,0:T(1,128)S(1)}, u32[]{:S(2)}, u32[]{:S(2)}) async-start(f32[16,1,192]{2,1,0:T(1,128)} %reshape.143), calls=%async_computation.2 | async-start | bytes 32768 | tf_op jit(solution)/shard_map/all_to_all | solution.py:101
  131.5 2.3 fusion.6
  134.0 2.1 copy.142
  136.1 8.0 %all-to-all-done.2 = f32[16,1,192]{2,1,0:T(1,128)S(1)} async-done(((f32[16,1,192]{2,1,0:T(1,128)}), f32[16,1,192]{2,1,0:T(1,128)S(1)}, u32[]{:S(2)}, u32[]{:S(2)}) %all-to-all-start.2) | async-done | bytes 12320 | tf_op jit(solution)/shard_map/all_to_all | solution.py:101
  144.7 4.0 %all-to-all-start.1 = ((f32[1,48,64,128]{3,1,0,2:T(8,128)}), f32[1,48,64,128]{3,1,0,2:T(8,128)S(1)}, u32[]{:S(2)}, u32[]{:S(2)}) async-start(f32[1,48,64,128]{3,1,0,2:T(8,128)} %copy.142), calls=%async_computation.1 | async-start | bytes 3145728 | tf_op jit(solution)/shard_map/all_to_all | solution.py:102
  148.7 1.8 copy.190
  151.7 2.4 copy.159
  154.1 1.6 fusion.16
  155.8 1.5 fusion.7
  157.5 2.1 copy.161
  159.6 51.4 %all-to-all-done.1 = f32[1,48,64,128]{3,1,0,2:T(8,128)S(1)} async-done(((f32[1,48,64,128]{3,1,0,2:T(8,128)}), f32[1,48,64,128]{3,1,0,2:T(8,128)S(1)}, u32[]{:S(2)}, u32[]{:S(2)}) %all-to-all-start.1) | async-done | bytes 1572896 | tf_op jit(solution)/shard_map/all_to_all | solution.py:102
  211.1 7.6 %all-to-all-start.3 = ((f32[1,48,64,128]{3,1,0,2:T(8,128)}), f32[1,48,64,128]{3,1,0,2:T(8,128)S(1)}, u32[]{:S(2)}, u32[]{:S(2)}) async-start(f32[1,48,64,128]{3,1,0,2:T(8,128)} %copy.161), calls=%async_computation.3 | async-start | bytes 3145728 | tf_op jit(solution)/shard_map/all_to_all | solution.py:102
  221.2 65.9 %all-to-all-done.3 = f32[1,48,64,128]{3,1,0,2:T(8,128)S(1)} async-done(((f32[1,48,64,128]{3,1,0,2:T(8,128)}), f32[1,48,64,128]{3,1,0,2:T(8,128)S(1)}, u32[]{:S(2)}, u32[]{:S(2)}) %all-to-all-start.3) | async-done | bytes 1572896 | tf_op jit(solution)/shard_map/all_to_all | solution.py:102
  (100 shorter events, 27.6 us)
Async XLA Ops:
  6.5 6.9 %copy-start.4 = (bf16[2,128,1024]{2,1,0:T(8,128)(2,1)S(1)}, bf16[2,128,1024]{2,1,0:T(8,128)(2,1)}, u32[]{:S(2)}) copy-start(bf16[2,128,1024]{2,1,0:T(8,128)(2,1)} %param.9) | copy-start | bytes 1572868
  6.5 80.2 %all-gather.2.cloned.1.call-start = ((), (), s32[]{:S(2)}) async-start(), calls=%async_computation.4 | async-start | bytes 1671168 | tf_op jit(solution)/shard_map/all_gather | solution.py:68
  9.0 79.6 %copy-start.11 = (pred[48,48]{0,1:T(8,128)(4,1)}, pred[48,48]{0,1:T(8,128)(4,1)S(1)}, u32[]{:S(2)}) copy-start(pred[48,48]{0,1:T(8,128)(4,1)S(1)} %copy.125) | copy-start | bytes 6916
  62.9 28.1 %copy-start.15 = (pred[128]{0:T(512)(128)(4,1)}, pred[128]{0:T(512)(128)(4,1)S(1)}, u32[]{:S(2)}) copy-start(pred[128]{0:T(512)(128)(4,1)S(1)} %add_compare_fusion) | copy-start | bytes 388
  95.4 1.1 copy-start.2
  98.2 10.8 %copy-start.5 = (bf16[6,8,8,128]{3,2,1,0:T(8,128)(2,1)S(1)}, bf16[6,8,8,128]{3,2,1,0:T(8,128)(2,1)}, u32[]{:S(2)}) copy-start(bf16[6,8,8,128]{3,2,1,0:T(8,128)(2,1)} %copy.195) | copy-start | bytes 294916
  98.2 10.8 %copy-start.12 = (pred[48,48]{0,1:T(8,128)(4,1)S(1)}, pred[48,48]{0,1:T(8,128)(4,1)}, u32[]{:S(2)}) copy-start(pred[48,48]{0,1:T(8,128)(4,1)} %copy-done.11) | copy-start | bytes 6916
  99.0 12.3 %copy-start.1 = (bf16[1,128,1024]{1,2,0:T(8,128)(2,1)S(1)}, bf16[1,128,1024]{1,2,0:T(8,128)(2,1)}, u32[]{:S(2)}) copy-start(bf16[1,128,1024]{1,2,0:T(8,128)(2,1)} %copy.189) | copy-start | bytes 786436
  99.0 12.3 %copy-start.16 = (pred[128]{0:T(512)(128)(4,1)S(1)}, pred[128]{0:T(512)(128)(4,1)}, u32[]{:S(2)}) copy-start(pred[128]{0:T(512)(128)(4,1)} %copy-done.15) | copy-start | bytes 388
  101.1 20.3 %all-to-all-start = ((f32[16,1,192]{2,1,0:T(1,128)}), f32[16,1,192]{2,1,0:T(1,128)S(1)}, u32[]{:S(2)}, u32[]{:S(2)}) async-start(f32[16,1,192]{2,1,0:T(1,128)} %reshape.145), calls=%async_computation | async-start | bytes 32768 | tf_op jit(solution)/shard_map/all_to_all | solution.py:101
  114.9 1.7 copy-start
  115.8 15.7 %copy-start.6 = (f32[48,8,8]{2,0,1:T(8,128)S(1)}, f32[48,8,8]{2,0,1:T(8,128)}, u32[]{:S(2)}) copy-start(f32[48,8,8]{2,0,1:T(8,128)} %get-tuple-element.8) | copy-start | bytes 36868
  116.6 14.9 %copy-start.8 = (bf16[6,8,8,128]{3,2,1,0:T(8,128)(2,1)S(1)}, bf16[6,8,8,128]{3,2,1,0:T(8,128)(2,1)}, u32[]{:S(2)}) copy-start(bf16[6,8,8,128]{3,2,1,0:T(8,128)(2,1)} %copy.193) | copy-start | bytes 294916
  116.6 14.9 %copy-start.13 = (pred[48,8,8]{2,0,1:T(8,128)(4,1)S(1)}, pred[48,8,8]{2,0,1:T(8,128)(4,1)}, u32[]{:S(2)}) copy-start(pred[48,8,8]{2,0,1:T(8,128)(4,1)} %get-tuple-element.9) | copy-start | bytes 9220
  121.5 22.7 %all-to-all-start.2 = ((f32[16,1,192]{2,1,0:T(1,128)}), f32[16,1,192]{2,1,0:T(1,128)S(1)}, u32[]{:S(2)}, u32[]{:S(2)}) async-start(f32[16,1,192]{2,1,0:T(1,128)} %reshape.143), calls=%async_computation.2 | async-start | bytes 32768 | tf_op jit(solution)/shard_map/all_to_all | solution.py:101
  144.1 0.6 copy-start.9
  144.7 66.3 %all-to-all-start.1 = ((f32[1,48,64,128]{3,1,0,2:T(8,128)}), f32[1,48,64,128]{3,1,0,2:T(8,128)S(1)}, u32[]{:S(2)}, u32[]{:S(2)}) async-start(f32[1,48,64,128]{3,1,0,2:T(8,128)} %copy.142), calls=%async_computation.1 | async-start | bytes 3145728 | tf_op jit(solution)/shard_map/all_to_all | solution.py:102
  154.1 1.6 copy-start.3
  154.1 1.6 copy-start.7
  154.1 1.7 copy-start.14
  159.6 59.9 %copy-start.10 = (f32[16,1,192]{2,1,0:T(1,128)S(1)}, f32[16,1,192]{2,1,0:T(1,128)}, u32[]{:S(2)}) copy-start(f32[16,1,192]{2,1,0:T(1,128)} %copy-done.9) | copy-start | bytes 36868
  211.1 76.1 %all-to-all-start.3 = ((f32[1,48,64,128]{3,1,0,2:T(8,128)}), f32[1,48,64,128]{3,1,0,2:T(8,128)S(1)}, u32[]{:S(2)}, u32[]{:S(2)}) async-start(f32[1,48,64,128]{3,1,0,2:T(8,128)} %copy.161), calls=%async_computation.3 | async-start | bytes 3145728 | tf_op jit(solution)/shard_map/all_to_all | solution.py:102
Sparse Core Ops, SparseCore 0:
  9.4 77.2 all-gather.1
where the time goes:
time: 299 us; the launch traced here: 295 us
  waiting for transfers between devices  152 us (51%)
  blocking collectives  43.3 us (14%)
  starting transfers between devices  29.4 us (10%)
  local copies, waits for them, and re-layouts  27.5 us (9%)
  other arithmetic  14.7 us (5%)
  between operations  14.6 us (5%)
  matrix products  13.9 us (5%)
    all_to_all x2, waiting for transfers between devices, body(): lax.all_to_all(output[None], 'ctx', split_axis=2, concat_axis=0, tiled=True)  117 us
    all_gather x1, blocking collectives, sent_together(): lax.all_gather(both, axis, axis=dim, tiled=True)  43.3 us
    all_gather x1, waiting for transfers between devices, body(): lax.all_gather(queries, 'ctx', axis=2, tiled=True)  23.9 us
    all_to_all x2, starting transfers between devices, body(): lax.all_to_all(lse[None], 'ctx', split_axis=2, concat_axis=0, tiled=True)  17.8 us
    unnamed x52, local copies, waits for them, and re-layouts  12 us
    all_to_all x2, starting transfers between devices, body(): lax.all_to_all(output[None], 'ctx', split_axis=2, concat_axis=0, tiled=True)  11.6 us
    all_to_all x2, waiting for transfers between devices, body(): lax.all_to_all(lse[None], 'ctx', split_axis=2, concat_axis=0, tiled=True)  10.1 us
    reduce_sum x4, other arithmetic, block_partial(): total = jnp.sum(cache_weight, -1) + jnp.sum(draft_weight, -1)  7.23 us
  transfers between devices with their start and end apart: 5, of which 5 were waited for; matrix products, arithmetic and copies ran while one was open for 13% of the time, Pallas kernels for 0%

commit v1 on v0

v1 whole, which is shorter than its diff:
```python
import math

import jax
import jax.numpy as jnp
from jax import lax
from jax.sharding import PartitionSpec as P

H = 64
KVH = 8
DH = 128


masked_score = -1e30


def block_partial(query_heads, block_keys, block_values, draft_k, draft_v, cache_keep, draft_keep, score_scale):
    scores = (
        jnp.einsum("kaqid,pkd->kaqip", query_heads, block_keys, preferred_element_type=jnp.float32)
        * score_scale
    )
    draft_scores = (
        jnp.einsum("kaqid,tkd->kaqit", query_heads, draft_k, preferred_element_type=jnp.float32)
        * score_scale
    )
    scores = jnp.where(cache_keep[None, None, None, None, :], scores, masked_score)
    draft_scores = jnp.where(draft_keep[None, None, :, None, :], draft_scores, masked_score)
    top_score = jnp.maximum(jnp.max(scores, -1), jnp.max(draft_scores, -1))
    shift_by = jnp.where(top_score > -1e29, top_score, 0.0)
    cache_weight = jnp.exp(scores - shift_by[..., None])
    draft_weight = jnp.exp(draft_scores - shift_by[..., None])
    total = jnp.sum(cache_weight, -1) + jnp.sum(draft_weight, -1)
    weighted = jnp.einsum(
        "kaqip,pkd->kaiqd",
        cache_weight.astype(jnp.bfloat16),
        block_values,
        preferred_element_type=jnp.float32,
    )
    weighted = weighted + jnp.einsum(
        "kaqit,tkd->kaiqd",
        draft_weight.astype(jnp.bfloat16),
        draft_v,
        preferred_element_type=jnp.float32,
    )
    top_score = jnp.transpose(top_score, (0, 1, 3, 2))
    total = jnp.transpose(total, (0, 1, 3, 2))
    alive = total > 0.0
    safe_total = jnp.where(alive, total, 1.0)
    output = jnp.where(alive[..., None], weighted / safe_total[..., None], 0.0).astype(jnp.bfloat16)
    lse = jnp.where(alive, top_score + jnp.log(safe_total), masked_score)
    return (lse, output)


def body(queries, key_cache, value_cache, draft_keys, draft_values, ancestors, context_length):
    devices = lax.axis_size("ctx")
    device_index = lax.axis_index("ctx")
    layers, rows, q_cols = queries.shape
    kv_cols = draft_keys.shape[2]
    packed = jnp.concatenate([queries, draft_keys, draft_values], axis=2)
    gathered = lax.all_gather(packed, "ctx", axis=0)
    local_len = key_cache.shape[1]
    trees = ancestors.shape[0]
    group_size = H // KVH
    split = devices // KVH
    heads_here = H // devices
    score_scale = 1.0 / math.sqrt(DH)
    tree_keep = (
        jnp.eye(trees, dtype=jnp.int32)[:, None, :, None] * ancestors[:, :, None, :]
    ).reshape(rows, rows) > 0
    draft_keep = jnp.logical_and(tree_keep, device_index == 0)
    cache_keep = (
        device_index * local_len + jnp.arange(local_len, dtype=jnp.int32) < context_length[0]
    )
    results = []
    for layer_index in range(layers):
        g = gathered[:, layer_index]
        query_heads = g[:, :, :q_cols].reshape(KVH, split, rows, heads_here, DH)
        draft_k = g[:, :, q_cols:q_cols + kv_cols].reshape(KVH, split, rows, kv_cols)
        draft_k = jnp.transpose(draft_k, (2, 0, 1, 3)).reshape(rows, KVH, DH)
        draft_v = g[:, :, q_cols + kv_cols:].reshape(KVH, split, rows, kv_cols)
        draft_v = jnp.transpose(draft_v, (2, 0, 1, 3)).reshape(rows, KVH, DH)
        lse, output = block_partial(
            query_heads,
            key_cache[layer_index].reshape(local_len, KVH, DH),
            value_cache[layer_index].reshape(local_len, KVH, DH),
            draft_k,
            draft_v,
            cache_keep,
            draft_keep,
            score_scale,
        )
        lse = lse.reshape(devices, heads_here, rows)
        output = output.reshape(devices, heads_here, rows, DH).astype(jnp.float32)
        overall = lax.pmax(lse, "ctx")
        factor = jnp.exp(lse - overall)
        weighted = factor[..., None] * output
        weighted_mine = lax.psum_scatter(weighted, "ctx", scatter_dimension=0, tiled=True)[0]
        total_mine = lax.psum_scatter(factor, "ctx", scatter_dimension=0, tiled=True)[0]
        mine = weighted_mine / total_mine[..., None]
        results.append(jnp.transpose(mine, (1, 0, 2)).reshape(rows, heads_here * DH))
    return jnp.stack(results)


def solution(mesh):
    placed = (
        P("req", None, "ctx"),
        P("req", "ctx", None),
        P("req", "ctx", None),
        P("req", None, "ctx"),
        P("req", None, "ctx"),
        P("req", None, None),
        P("req"),
    )
    return jax.shard_map(
        body, mesh=mesh, in_specs=placed, out_specs=P("req", None, "ctx"), check_vma=False
    )
```

time: 299 us -> 314 us (1.050); the launches traced: 295 us -> 314 us
  blocking collectives: 43.3 us -> 108 us
  starting transfers between devices: 29.4 us -> 0.09 us
  local copies, waits for them, and re-layouts: 27.5 us -> 15.3 us
    all_to_all x4 -> x0, waiting for transfers between devices: 127 us -> none  [the longest x2 117 us: body(): lax.all_to_all(output[None], 'ctx', split_axis=2, concat_axis=0, tiled=True)]
    reduce_scatter x0 -> x2, waiting for transfers between devices: none -> 75.9 us  [body(): lax.psum_scatter(weighted, 'ctx', scatter_dimension=0, tiled=True)[0]]
    pmax x0 -> x1, blocking collectives: none -> 55.7 us  [body(): overall = lax.pmax(lse, 'ctx')]
    unnamed x0 -> x1, blocking collectives: none -> 52.7 us
    all_gather x1, waiting for transfers between devices: 23.9 us -> 74.7 us  [body(): gathered = lax.all_gather(packed, 'ctx', axis=0)]
    all_gather x1 -> x0, blocking collectives: 43.3 us -> none  [sent_together(): lax.all_gather(both, axis, axis=dim, tiled=True)]
    all_to_all x4 -> x0, starting transfers between devices: 29.4 us -> none  [the longest x2 17.8 us: body(): lax.all_to_all(lse[None], 'ctx', split_axis=2, concat_axis=0, tiled=True)]
    convert_element_type x6 -> x0, local copies, waits for them, and re-layouts: 8.22 us -> none  [the longest x4 4.53 us: body(): output = output.reshape(rows, H, DH).astype(jnp.float32)]
  transfers between devices with their start and end apart: 5 -> 3, of which waited for: 5 -> 3; matrix products, arithmetic and copies ran while one was open for 13% -> 5% of each run, Pallas kernels for 0% -> 0%
where the time goes in v1:
time: 314 us
  waiting for transfers between devices  151 us (48%)
  blocking collectives  108 us (34%)
  local copies, waits for them, and re-layouts  15.3 us (5%)
  other arithmetic  14.1 us (4%)
  between operations  14 us (4%)
  matrix products  10.9 us (3%)
    reduce_scatter x2, waiting for transfers between devices, body(): lax.psum_scatter(weighted, 'ctx', scatter_dimension=0, tiled=True)[0]  75.9 us
    all_gather x1, waiting for transfers between devices, body(): gathered = lax.all_gather(packed, 'ctx', axis=0)  74.7 us
    pmax x1, blocking collectives, body(): overall = lax.pmax(lse, 'ctx')  55.7 us
    unnamed x1, blocking collectives  52.7 us
  transfers between devices with their start and end apart: 3, of which 3 were waited for; matrix products, arithmetic and copies ran while one was open for 5% of the time, Pallas kernels for 0%

profile of v1, /device:TPU:6, one launch (start us, length us, event | category | flops | bytes accessed | tf_op | source)
XLA Modules:
  0.0 313.6 jit_solution(359991566802228348)
XLA Ops:
  6.5 1.7 pad_maximum_fusion.1
  10.0 1.1 fusion.39
  12.4 74.7 %all-gather.3.cloned.1.call-done = bf16[32,48,640]{2,1,0:T(8,128)(2,1)} async-done(((bf16[2,48,640]{2,1,0:T(8,128)(2,1)}), bf16[32,48,640]{2,1,0:T(8,128)(2,1)}) %all-gather.3.cloned.1.call-update) | async-done | bytes 1966096 | tf_op jit(solution)/shard_map/all_gather | solution.py:59
  87.0 1.7 slice_bitcast_fusion.1
  89.7 1.1 reshape.103
  93.8 1.0 fusion.43
  94.9 1.1 copy-done
  96.4 1.0 fusion.7
  97.4 1.8 fusion.18
  100.0 1.0 fusion.41
  101.5 1.0 fusion.11
  103.7 55.7 %all-reduce.3 = (f32[16,4,48]{2,1,0:T(4,128)}, f32[16,4,48]{2,1,0:T(4,128)}) all-reduce(f32[16,4,48]{2,1,0:T(4,128)S(1)} %bitcast.139, f32[16,4,48]{2,1,0:T(4,128)S(1)} %bitcast.140), channel_id=1, replica_groups=mesh['req'=32,'ctx'=16] {'ctx'}, use_global_device_ids=true, to_apply=%region_11.12 | all-reduce | flops 6144 | bytes 49152 | tf_op jit(solution)/shard_map/pmax | solution.py:93
  160.2 2.7 fusion.5
  163.0 1.6 convert_multiply_fusion.1
  165.5 1.1 copy.73
  168.2 1.6 fusion.15
  169.8 1.5 fusion.2
  171.3 1.6 convert_multiply_fusion
  172.9 1.3 dynamic-slice
  174.2 52.7 %all-reduce.2 = (f32[16,4,48]{2,1,0:T(4,128)S(1)}, f32[16,4,48]{2,1,0:T(4,128)S(1)}) all-reduce(f32[16,4,48]{2,1,0:T(4,128)S(1)} %subtract_exponential_fusion.4, f32[16,4,48]{2,1,0:T(4,128)S(1)} %subtract_exponential_fusion.5), channel_id=6, replica_groups=mesh['req'=32,'ctx'=16] {'ctx'}, use_global_device_ids=true, to_apply=%region_13.14.clone | all-reduce | flops 6144 | bytes 49152
  228.2 4.4 %reduce-scatter.3.cloned.1.call-done = f32[1,4,48,128]{3,2,1,0:T(8,128)} async-done(((f32[16,4,48,128]{3,2,1,0:T(8,128)}), f32[1,4,48,128]{3,2,1,0:T(8,128)}) %reduce-scatter.3.cloned.1.call-update) | async-done | bytes 98320 | tf_op jit(solution)/shard_map/reduce_scatter | solution.py:96
  232.6 1.0 fusion.31
  233.7 71.5 %reduce-scatter.5.cloned.1.call-done = f32[1,4,48,128]{3,2,1,0:T(8,128)} async-done(((f32[16,4,48,128]{3,2,1,0:T(8,128)}), f32[1,4,48,128]{3,2,1,0:T(8,128)}) %reduce-scatter.5.cloned.1.call-update) | async-done | bytes 98320 | tf_op jit(solution)/shard_map/reduce_scatter | solution.py:96
  305.3 1.0 fusion.28
  (59 shorter events, 14.7 us)
Async XLA Ops:
  6.5 5.6 %copy-start.2 = (bf16[2,128,1024]{2,1,0:T(8,128)(2,1)S(1)}, bf16[2,128,1024]{2,1,0:T(8,128)(2,1)}, u32[]{:S(2)}) copy-start(bf16[2,128,1024]{2,1,0:T(8,128)(2,1)} %param.9) | copy-start | bytes 1572868
  6.5 80.5 %all-gather.3.cloned.1.call-start = ((), (), s32[]{:S(2)}) async-start(), calls=%async_computation.4 | async-start | bytes 2088960 | tf_op jit(solution)/shard_map/all_gather | solution.py:59
  8.3 224.4 %reduce-scatter.3.cloned.1.call-start = ((), (), s32[]{:S(2)}) async-start(), calls=%async_computation.2 | async-start | bytes 1671168 | tf_op jit(solution)/shard_map/reduce_scatter | solution.py:96
  94.9 1.1 copy-start
  97.4 1.8 copy-start.1
  97.4 1.8 copy-start.4
  99.1 0.9 copy-start.5
  103.1 56.3 %copy-start.3 = (f32[8,2,4,48]{3,2,1,0:T(4,128)}, f32[8,2,4,48]{3,2,1,0:T(4,128)S(1)}, u32[]{:S(2)}) copy-start(f32[8,2,4,48]{3,2,1,0:T(4,128)S(1)} %get-tuple-element.9) | copy-start | bytes 36868
  164.6 140.6 %reduce-scatter.5.cloned.1.call-start = ((), (), s32[]{:S(2)}) async-start(), calls=%async_computation.3 | async-start | bytes 1671168 | tf_op jit(solution)/shard_map/reduce_scatter | solution.py:96
  168.2 1.6 copy-start.6
  168.2 1.6 copy-start.7
Sparse Core Ops, SparseCore 0:
  9.4 77.5 all-gather.2
  164.7 67.8 reduce-scatter.2
  235.7 69.5 reduce-scatter.4

commit v2 on v1

v2 whole, which is shorter than its diff:
```python
import math

import jax
import jax.numpy as jnp
from jax import lax
from jax.sharding import PartitionSpec as P

H = 64
KVH = 8
DH = 128


masked_score = -1e30


def send_target(s, j, n):
    return (s + j) % n if (s + j) % 2 == 0 else (s - j) % n


def blocks_partial(query_heads, block_keys, block_values, draft_k, draft_v, cache_keep, draft_keep, score_scale):
    scores = (
        jnp.einsum("qhd,jpd->hqjp", query_heads, block_keys, preferred_element_type=jnp.float32)
        * score_scale
    )
    draft_scores = (
        jnp.einsum("qhd,td->hqt", query_heads, draft_k, preferred_element_type=jnp.float32)
        * score_scale
    )
    scores = jnp.where(cache_keep[None, None], scores, masked_score)
    draft_scores = jnp.where(draft_keep[None], draft_scores[:, :, None, :], masked_score)
    top_score = jnp.maximum(jnp.max(scores, -1), jnp.max(draft_scores, -1))
    shift_by = jnp.where(top_score > -1e29, top_score, 0.0)
    cache_weight = jnp.exp(scores - shift_by[..., None])
    draft_weight = jnp.exp(draft_scores - shift_by[..., None])
    total = jnp.sum(cache_weight, -1) + jnp.sum(draft_weight, -1)
    weighted = jnp.einsum(
        "hqjp,jpd->hqjd",
        cache_weight.astype(jnp.bfloat16),
        block_values,
        preferred_element_type=jnp.float32,
    )
    weighted = weighted + jnp.einsum(
        "hqjt,td->hqjd",
        draft_weight.astype(jnp.bfloat16),
        draft_v,
        preferred_element_type=jnp.float32,
    )
    alive = total > 0.0
    safe_total = jnp.where(alive, total, 1.0)
    output = lax.reduce_precision(
        jnp.where(alive[..., None], weighted / safe_total[..., None], 0.0), exponent_bits=8, mantissa_bits=7
    )
    lse = jnp.where(alive, top_score + jnp.log(safe_total), masked_score)
    top = jnp.max(lse, -1)
    factor = jnp.where(lse > -1e29, jnp.exp(lse - top[..., None]), 0.0)
    return top, jnp.sum(factor, -1), jnp.sum(factor[..., None] * output, 2)


def body(queries, key_cache, value_cache, draft_keys, draft_values, ancestors, context_length):
    n = lax.axis_size("ctx")
    d = lax.axis_index("ctx")
    assert n == 2 * KVH
    layers, rows, q_cols = queries.shape
    kv_cols = draft_keys.shape[2]
    local_len = key_cache.shape[1]
    trees = ancestors.shape[0]
    heads_here = H // n
    reach = n // 2
    score_scale = 1.0 / math.sqrt(DH)
    own = d % 2
    pair = d // 2
    swap = [(s, s ^ 1) for s in range(n)]

    packed = jnp.concatenate([queries, draft_keys, draft_values], axis=2)
    partner = lax.ppermute(packed, "ctx", swap)
    first = jnp.where(own == 0, packed, partner)
    second = jnp.where(own == 0, partner, packed)

    kv = jnp.stack(
        [key_cache.reshape(layers, local_len, KVH, DH), value_cache.reshape(layers, local_len, KVH, DH)], 1
    )
    kv = jnp.transpose(kv, (0, 3, 1, 2, 4))

    sources = jnp.where(own == 0, d - jnp.arange(reach), d + jnp.arange(reach)) % n
    tree_keep = (
        jnp.eye(trees, dtype=jnp.int32)[:, None, :, None] * ancestors[:, :, None, :]
    ).reshape(rows, rows) > 0
    cache_keep = sources[:, None] * local_len + jnp.arange(local_len)[None, :] < context_length[0]
    draft_keep = jnp.logical_and(tree_keep[:, None, :], (sources == 0)[None, :, None])

    results = []
    for layer_index in range(layers):
        here = kv[layer_index]
        blocks = [lax.dynamic_index_in_dim(here, pair, 0, keepdims=False)]
        for j in range(1, reach):
            target = jnp.where((d + j) % 2 == 0, (d + j) % n, (d - j) % n)
            msg = lax.dynamic_index_in_dim(here, target // 2, 0, keepdims=False)
            blocks.append(lax.ppermute(msg, "ctx", [(s, send_target(s, j, n)) for s in range(n)]))
        blocks = jnp.stack(blocks)
        f = first[layer_index]
        s2 = second[layer_index]
        query_heads = jnp.concatenate(
            [f[:, :q_cols].reshape(rows, heads_here, DH), s2[:, :q_cols].reshape(rows, heads_here, DH)], 1
        )
        draft_k = jnp.concatenate([f[:, q_cols:q_cols + kv_cols], s2[:, q_cols:q_cols + kv_cols]], 1)
        draft_v = jnp.concatenate([f[:, q_cols + kv_cols:], s2[:, q_cols + kv_cols:]], 1)
        top, total, acc = blocks_partial(
            query_heads, blocks[:, 0], blocks[:, 1], draft_k, draft_v, cache_keep, draft_keep, score_scale
        )
        top = top.reshape(2, heads_here, rows)
        total = total.reshape(2, heads_here, rows)
        acc = acc.reshape(2, heads_here, rows, DH)
        keep = (jnp.where(own == 0, top[0], top[1]), jnp.where(own == 0, total[0], total[1]),
                jnp.where(own == 0, acc[0], acc[1]))
        give = (jnp.where(own == 0, top[1], top[0]), jnp.where(own == 0, total[1], total[0]),
                jnp.where(own == 0, acc[1], acc[0]))
        got = lax.ppermute(give, "ctx", swap)
        overall = jnp.maximum(keep[0], got[0])
        f_keep = jnp.exp(keep[0] - overall)
        f_got = jnp.exp(got[0] - overall)
        mine = (keep[2] * f_keep[..., None] + got[2] * f_got[..., None]) / (
            keep[1] * f_keep + got[1] * f_got
        )[..., None]
        results.append(jnp.transpose(mine, (1, 0, 2)).reshape(rows, heads_here * DH))
    return jnp.stack(results)


def solution(mesh):
    placed = (
        P("req", None, "ctx"),
        P("req", "ctx", None),
        P("req", "ctx", None),
        P("req", None, "ctx"),
        P("req", None, "ctx"),
        P("req", None, None),
        P("req"),
    )
    return jax.shard_map(
        body, mesh=mesh, in_specs=placed, out_specs=P("req", None, "ctx"), check_vma=False
    )
```

time: 314 us -> 187 us (0.60)
  blocking collectives: 108 us -> 0 us
  starting transfers between devices: 0.09 us -> 74.8 us
  waiting for transfers between devices: 151 us -> 82.2 us
  between operations: 14 us -> 2.02 us
  local copies, waits for them, and re-layouts: 15.3 us -> 7.28 us
  matrix products: 10.9 us -> 7.06 us
    ppermute x0 -> x21, waiting for transfers between devices: none -> 82.2 us  [the longest x14 81.5 us: body(): lax.ppermute(msg, 'ctx', [(s, send_target(s, j, n)) for s in range(n)])]
    reduce_scatter x2 -> x0, waiting for transfers between devices: 75.9 us -> none  [body(): lax.psum_scatter(weighted, 'ctx', scatter_dimension=0, tiled=True)[0]]
    ppermute x0 -> x21, starting transfers between devices: none -> 74.8 us  [the longest x14 53.5 us: body(): lax.ppermute(msg, 'ctx', [(s, send_target(s, j, n)) for s in range(n)])]
    all_gather x1 -> x0, waiting for transfers between devices: 74.7 us -> none  [body(): gathered = lax.all_gather(packed, 'ctx', axis=0)]
    pmax x1 -> x0, blocking collectives: 55.7 us -> none  [body(): overall = lax.pmax(lse, 'ctx')]
    unnamed x1 -> x0, blocking collectives: 52.7 us -> none
    dot_general x8 -> x6, matrix products: 10.9 us -> 6.35 us  [the longest x2 4.52 us: blocks_partial(): jnp.einsum('hqjt,td->hqjd', draft_weight.astype(jnp.bfloat16), draft_v, p...]
    reshape x6 -> x0, local copies, waits for them, and re-layouts: 3.71 us -> none  [the longest x2 1.56 us: body(): draft_v = jnp.transpose(draft_v, (2, 0, 1, 3)).reshape(rows, KVH, DH)]
  transfers between devices with their start and end apart: 3 -> 21, of which waited for: 3 -> 12; matrix products, arithmetic and copies ran while one was open for 5% -> 8% of each run, Pallas kernels for 0% -> 0%
where the time goes in v2:
time: 187 us; the launch traced here: 186 us
  waiting for transfers between devices  82.2 us (44%)
  starting transfers between devices  74.8 us (40%)
  other arithmetic  12.2 us (7%)
  local copies, waits for them, and re-layouts  7.28 us (4%)
  matrix products  7.06 us (4%)
  between operations  2.02 us (1%)
    ppermute x14, waiting for transfers between devices, body(): lax.ppermute(msg, 'ctx', [(s, send_target(s, j, n)) for s in range(n)])  81.5 us
    ppermute x14, starting transfers between devices, body(): lax.ppermute(msg, 'ctx', [(s, send_target(s, j, n)) for s in range(n)])  53.5 us
    ppermute x6, starting transfers between devices, body(): got = lax.ppermute(give, 'ctx', swap)  17.5 us
    reduce_sum x4, other arithmetic, blocks_partial(): total = jnp.sum(cache_weight, -1) + jnp.sum(draft_weight, -1)  4.94 us
    dot_general x2, matrix products, blocks_partial(): jnp.einsum('hqjt,td->hqjd', draft_weight.astype(jnp.bfloat16), draft_v, p...  4.52 us
    ppermute x1, starting transfers between devices, body(): partner = lax.ppermute(packed, 'ctx', swap)  3.83 us
  transfers between devices with their start and end apart: 21, of which 12 were waited for; matrix products, arithmetic and copies ran while one was open for 8% of the time, Pallas kernels for 0%

profile of v2, /device:TPU:6, one launch (start us, length us, event | category | flops | bytes accessed | tf_op | source)
XLA Modules:
  0.0 185.5 jit_solution(3141944255935925662)
XLA Ops:
  1.1 3.8 %collective-permute-start.7 = (bf16[2,48,640]{2,1,0:T(8,128)(2,1)S(1)}, bf16[2,48,640]{2,1,0:T(8,128)(2,1)S(1)}, u32[]{:S(2)}, u32[]{:S(2)}) collective-permute-start(bf16[2,48,640]{2,1,0:T(8,128)(2,1)S(1)} %pad_maximum_fusion.1), channel_id=1, source_target_pairs={{0,1},{1,0},{2,3},{3,2},{4,5},{5,4},{6,7},{7,6},{8,9},{9,8},{10,11... | collective-permute-start | bytes 368648 | tf_op jit(solution)/shard_map/ppermute | solution.py:75
  7.1 14.4 %collective-permute-start.6 = (bf16[2,128,128]{2,1,0:T(8,128)(2,1)S(1)}, bf16[2,128,128]{2,1,0:T(8,128)(2,1)S(1)}, u32[]{:S(2)}, u32[]{:S(2)}) collective-permute-start(bf16[2,128,128]{2,1,0:T(8,128)(2,1)S(1)} %get-tuple-element.33), channel_id=1, source_target_pairs={{0,9},{1,8},{2,11},{3,10},{4,13},{5,12},{6,15},{7,14},{8,1},{9,0},... | collective-permute-start | bytes 196616 | tf_op jit(solution)/shard_map/ppermute | solution.py:98
  21.5 5.2 %collective-permute-start.5 = (bf16[2,128,128]{2,1,0:T(8,128)(2,1)S(1)}, bf16[2,128,128]{2,1,0:T(8,128)(2,1)S(1)}, u32[]{:S(2)}, u32[]{:S(2)}) collective-permute-start(bf16[2,128,128]{2,1,0:T(8,128)(2,1)S(1)} %get-tuple-element.34), channel_id=1, source_target_pairs={{0,6},{1,11},{2,8},{3,13},{4,10},{5,15},{6,12},{7,1},{8,14},{9,3},... | collective-permute-start | bytes 196616 | tf_op jit(solution)/shard_map/ppermute | solution.py:98
  26.7 5.9 %collective-permute-start.4 = (bf16[2,128,128]{2,1,0:T(8,128)(2,1)S(1)}, bf16[2,128,128]{2,1,0:T(8,128)(2,1)S(1)}, u32[]{:S(2)}, u32[]{:S(2)}) collective-permute-start(bf16[2,128,128]{2,1,0:T(8,128)(2,1)S(1)} %get-tuple-element.35), channel_id=1, source_target_pairs={{0,11},{1,6},{2,13},{3,8},{4,15},{5,10},{6,1},{7,12},{8,3},{9,14},... | collective-permute-start | bytes 196616 | tf_op jit(solution)/shard_map/ppermute | solution.py:98
  36.4 4.5 %collective-permute-done.11 = bf16[2,128,128]{2,1,0:T(8,128)(2,1)S(1)} collective-permute-done((bf16[2,128,128]{2,1,0:T(8,128)(2,1)}, bf16[2,128,128]{2,1,0:T(8,128)(2,1)S(1)}, u32[]{:S(2)}, u32[]{:S(2)}) %collective-permute-start.11) | collective-permute-done | bytes 65568 | tf_op jit(solution)/shard_map/ppermute | solution.py:98
  43.1 6.3 %collective-permute-done.12 = bf16[2,128,128]{2,1,0:T(8,128)(2,1)S(1)} collective-permute-done((bf16[2,128,128]{2,1,0:T(8,128)(2,1)}, bf16[2,128,128]{2,1,0:T(8,128)(2,1)S(1)}, u32[]{:S(2)}, u32[]{:S(2)}) %collective-permute-start.12) | collective-permute-done | bytes 65568 | tf_op jit(solution)/shard_map/ppermute | solution.py:98
  49.4 2.2 %collective-permute-start.13 = (bf16[2,128,128]{2,1,0:T(8,128)(2,1)}, bf16[2,128,128]{2,1,0:T(8,128)(2,1)S(1)}, u32[]{:S(2)}, u32[]{:S(2)}) collective-permute-start(bf16[2,128,128]{2,1,0:T(8,128)(2,1)} %get-tuple-element.44), channel_id=1, source_target_pairs={{0,13},{1,4},{2,15},{3,6},{4,1},{5,8},{6,3},{7,10},{8,5},{9,12},{1... | collective-permute-start | bytes 196616 | tf_op jit(solution)/shard_map/ppermute | solution.py:98
  51.6 7.4 %collective-permute-done.13 = bf16[2,128,128]{2,1,0:T(8,128)(2,1)S(1)} collective-permute-done((bf16[2,128,128]{2,1,0:T(8,128)(2,1)}, bf16[2,128,128]{2,1,0:T(8,128)(2,1)S(1)}, u32[]{:S(2)}, u32[]{:S(2)}) %collective-permute-start.13) | collective-permute-done | bytes 65568 | tf_op jit(solution)/shard_map/ppermute | solution.py:98
  59.0 2.6 %collective-permute-start.14 = (bf16[2,128,128]{2,1,0:T(8,128)(2,1)}, bf16[2,128,128]{2,1,0:T(8,128)(2,1)S(1)}, u32[]{:S(2)}, u32[]{:S(2)}) collective-permute-start(bf16[2,128,128]{2,1,0:T(8,128)(2,1)} %get-tuple-element.43), channel_id=1, source_target_pairs={{0,4},{1,13},{2,6},{3,15},{4,8},{5,1},{6,10},{7,3},{8,12},{9,5},{1... | collective-permute-start | bytes 196616 | tf_op jit(solution)/shard_map/ppermute | solution.py:98
  61.6 8.4 %collective-permute-done.14 = bf16[2,128,128]{2,1,0:T(8,128)(2,1)S(1)} collective-permute-done((bf16[2,128,128]{2,1,0:T(8,128)(2,1)}, bf16[2,128,128]{2,1,0:T(8,128)(2,1)S(1)}, u32[]{:S(2)}, u32[]{:S(2)}) %collective-permute-start.14) | collective-permute-done | bytes 65568 | tf_op jit(solution)/shard_map/ppermute | solution.py:98
  70.0 5.0 %collective-permute-start.15 = (bf16[2,128,128]{2,1,0:T(8,128)(2,1)S(1)}, bf16[2,128,128]{2,1,0:T(8,128)(2,1)S(1)}, u32[]{:S(2)}, u32[]{:S(2)}) collective-permute-start(bf16[2,128,128]{2,1,0:T(8,128)(2,1)S(1)} %get-tuple-element.42), channel_id=1, source_target_pairs={{0,11},{1,6},{2,13},{3,8},{4,15},{5,10},{6,1},{7,12},{8,3},{9,14},... | collective-permute-start | bytes 196616 | tf_op jit(solution)/shard_map/ppermute | solution.py:98
  75.0 7.1 %collective-permute-done.15 = bf16[2,128,128]{2,1,0:T(8,128)(2,1)S(1)} collective-permute-done((bf16[2,128,128]{2,1,0:T(8,128)(2,1)S(1)}, bf16[2,128,128]{2,1,0:T(8,128)(2,1)S(1)}, u32[]{:S(2)}, u32[]{:S(2)}) %collective-permute-start.15) | collective-permute-done | bytes 65568 | tf_op jit(solution)/shard_map/ppermute | solution.py:98
  84.1 11.1 %collective-permute-done.16 = bf16[2,128,128]{2,1,0:T(8,128)(2,1)S(1)} collective-permute-done((bf16[2,128,128]{2,1,0:T(8,128)(2,1)S(1)}, bf16[2,128,128]{2,1,0:T(8,128)(2,1)S(1)}, u32[]{:S(2)}, u32[]{:S(2)}) %collective-permute-start.16) | collective-permute-done | bytes 65568 | tf_op jit(solution)/shard_map/ppermute | solution.py:98
  95.2 2.2 %collective-permute-start.17 = (bf16[2,128,128]{2,1,0:T(8,128)(2,1)S(1)}, bf16[2,128,128]{2,1,0:T(8,128)(2,1)S(1)}, u32[]{:S(2)}, u32[]{:S(2)}) collective-permute-start(bf16[2,128,128]{2,1,0:T(8,128)(2,1)S(1)} %get-tuple-element.40), channel_id=1, source_target_pairs={{0,9},{1,8},{2,11},{3,10},{4,13},{5,12},{6,15},{7,14},{8,1},{9,0},... | collective-permute-start | bytes 196616 | tf_op jit(solution)/shard_map/ppermute | solution.py:98
  97.5 11.7 %collective-permute-done.17 = bf16[2,128,128]{2,1,0:T(8,128)(2,1)S(1)} collective-permute-done((bf16[2,128,128]{2,1,0:T(8,128)(2,1)S(1)}, bf16[2,128,128]{2,1,0:T(8,128)(2,1)S(1)}, u32[]{:S(2)}, u32[]{:S(2)}) %collective-permute-start.17) | collective-permute-done | bytes 65568 | tf_op jit(solution)/shard_map/ppermute | solution.py:98
  111.3 5.2 %collective-permute-done = bf16[2,128,128]{2,1,0:T(8,128)(2,1)S(1)} collective-permute-done((bf16[2,128,128]{2,1,0:T(8,128)(2,1)S(1)}, bf16[2,128,128]{2,1,0:T(8,128)(2,1)S(1)}, u32[]{:S(2)}, u32[]{:S(2)}) %collective-permute-start) | collective-permute-done | bytes 65568 | tf_op jit(solution)/shard_map/ppermute | solution.py:98
  118.5 6.3 %collective-permute-done.1 = bf16[2,128,128]{2,1,0:T(8,128)(2,1)S(1)} collective-permute-done((bf16[2,128,128]{2,1,0:T(8,128)(2,1)S(1)}, bf16[2,128,128]{2,1,0:T(8,128)(2,1)S(1)}, u32[]{:S(2)}, u32[]{:S(2)}) %collective-permute-start.1) | collective-permute-done | bytes 65568 | tf_op jit(solution)/shard_map/ppermute | solution.py:98
  126.8 7.5 %collective-permute-done.2 = bf16[2,128,128]{2,1,0:T(8,128)(2,1)S(1)} collective-permute-done((bf16[2,128,128]{2,1,0:T(8,128)(2,1)S(1)}, bf16[2,128,128]{2,1,0:T(8,128)(2,1)S(1)}, u32[]{:S(2)}, u32[]{:S(2)}) %collective-permute-start.2) | collective-permute-done | bytes 65568 | tf_op jit(solution)/shard_map/ppermute | solution.py:98
  134.2 4.1 %collective-permute-start.3 = (bf16[2,128,128]{2,1,0:T(8,128)(2,1)S(1)}, bf16[2,128,128]{2,1,0:T(8,128)(2,1)S(1)}, u32[]{:S(2)}, u32[]{:S(2)}) collective-permute-start(bf16[2,128,128]{2,1,0:T(8,128)(2,1)S(1)} %get-tuple-element.36), channel_id=1, source_target_pairs={{0,4},{1,13},{2,6},{3,15},{4,8},{5,1},{6,10},{7,3},{8,12},{9,5},{1... | collective-permute-start | bytes 196616 | tf_op jit(solution)/shard_map/ppermute | solution.py:98
  138.4 5.9 %collective-permute-done.3 = bf16[2,128,128]{2,1,0:T(8,128)(2,1)S(1)} collective-permute-done((bf16[2,128,128]{2,1,0:T(8,128)(2,1)S(1)}, bf16[2,128,128]{2,1,0:T(8,128)(2,1)S(1)}, u32[]{:S(2)}, u32[]{:S(2)}) %collective-permute-start.3) | collective-permute-done | bytes 65568 | tf_op jit(solution)/shard_map/ppermute | solution.py:98
  156.4 3.9 %collective-permute-start.8 = (f32[4,48]{1,0:T(4,128)}, f32[4,48]{1,0:T(4,128)}, u32[]{:S(2)}, u32[]{:S(2)}) collective-permute-start(f32[4,48]{1,0:T(4,128)} %slice_select_fusion.6), channel_id=1, source_target_pairs={{0,1},{1,0},{2,3},{3,2},{4,5},{5,4},{6,7},{7,6},{8,9},{9,8},{10,11... | collective-permute-start | bytes 2312 | tf_op jit(solution)/shard_map/ppermute | solution.py:117
  161.1 2.9 %multiply_reduce_fusion.1 = f32[8,48,128]{2,1,0:T(8,128)S(1)} fusion(f32[8,48,8,128]{3,1,0,2:T(8,128)S(1)} %bitcast.192, bf16[8,48,8,48]{3,2,1,0:T(8,128)(2,1)S(1)} %get-tuple-element.47, f32[8,48,8]{1,0,2:T(8,128)S(1)} %get-tuple-element.13, f32[8,48,8]{1,0,2:T(8,128)} %get-tuple-element.11, pred[8,48,8]{1,0,2:T(8,128)(4,1)} %copy-done.14, ...), kind=kOutput, calls=%fused_computation.18 | convolution fusion | flops 40083456 | bytes 2104320 | tf_op jit(solution)/shard_map/hqjt,td->hqjd/dot_general | solution.py:42
  170.5 3.9 %collective-permute-start.20 = (f32[4,48]{1,0:T(4,128)S(1)}, f32[4,48]{1,0:T(4,128)S(1)}, u32[]{:S(2)}, u32[]{:S(2)}) collective-permute-start(f32[4,48]{1,0:T(4,128)S(1)} %slice_select_fusion.2), channel_id=1, source_target_pairs={{0,1},{1,0},{2,3},{3,2},{4,5},{5,4},{6,7},{7,6},{8,9},{9,8},{10,11... | collective-permute-start | bytes 2312 | tf_op jit(solution)/shard_map/ppermute | solution.py:117
  178.1 3.9 %collective-permute-start.19 = (f32[4,48,128]{2,1,0:T(8,128)S(1)}, f32[4,48,128]{2,1,0:T(8,128)S(1)}, u32[]{:S(2)}, u32[]{:S(2)}) collective-permute-start(f32[4,48,128]{2,1,0:T(8,128)S(1)} %slice_select_fusion), channel_id=1, source_target_pairs={{0,1},{1,0},{2,3},{3,2},{4,5},{5,4},{6,7},{7,6},{8,9},{9,8},{10,11... | collective-permute-start | bytes 294920 | tf_op jit(solution)/shard_map/ppermute | solution.py:117
  (141 shorter events, 42.0 us)
Async XLA Ops:
  1.1 143.3 %collective-permute-start.7 = (bf16[2,48,640]{2,1,0:T(8,128)(2,1)S(1)}, bf16[2,48,640]{2,1,0:T(8,128)(2,1)S(1)}, u32[]{:S(2)}, u32[]{:S(2)}) collective-permute-start(bf16[2,48,640]{2,1,0:T(8,128)(2,1)S(1)} %pad_maximum_fusion.1), channel_id=1, source_target_pairs={{0,1},{1,0},{2,3},{3,2},{4,5},{5,4},{6,7},{7,6},{8,9},{9,8},{10,11... | collective-permute-start | bytes 368648 | tf_op jit(solution)/shard_map/ppermute | solution.py:75
  7.1 137.3 %collective-permute-start.6 = (bf16[2,128,128]{2,1,0:T(8,128)(2,1)S(1)}, bf16[2,128,128]{2,1,0:T(8,128)(2,1)S(1)}, u32[]{:S(2)}, u32[]{:S(2)}) collective-permute-start(bf16[2,128,128]{2,1,0:T(8,128)(2,1)S(1)} %get-tuple-element.33), channel_id=1, source_target_pairs={{0,9},{1,8},{2,11},{3,10},{4,13},{5,12},{6,15},{7,14},{8,1},{9,0},... | collective-permute-start | bytes 196616 | tf_op jit(solution)/shard_map/ppermute | solution.py:98
  21.5 122.8 %collective-permute-start.5 = (bf16[2,128,128]{2,1,0:T(8,128)(2,1)S(1)}, bf16[2,128,128]{2,1,0:T(8,128)(2,1)S(1)}, u32[]{:S(2)}, u32[]{:S(2)}) collective-permute-start(bf16[2,128,128]{2,1,0:T(8,128)(2,1)S(1)} %get-tuple-element.34), channel_id=1, source_target_pairs={{0,6},{1,11},{2,8},{3,13},{4,10},{5,15},{6,12},{7,1},{8,14},{9,3},... | collective-permute-start | bytes 196616 | tf_op jit(solution)/shard_map/ppermute | solution.py:98
  26.7 117.6 %collective-permute-start.4 = (bf16[2,128,128]{2,1,0:T(8,128)(2,1)S(1)}, bf16[2,128,128]{2,1,0:T(8,128)(2,1)S(1)}, u32[]{:S(2)}, u32[]{:S(2)}) collective-permute-start(bf16[2,128,128]{2,1,0:T(8,128)(2,1)S(1)} %get-tuple-element.35), channel_id=1, source_target_pairs={{0,11},{1,6},{2,13},{3,8},{4,15},{5,10},{6,1},{7,12},{8,3},{9,14},... | collective-permute-start | bytes 196616 | tf_op jit(solution)/shard_map/ppermute | solution.py:98
  32.6 111.8 %copy-start.5 = (bf16[2,48,512]{2,1,0:T(8,128)(2,1)S(1)}, bf16[2,48,512]{2,1,0:T(8,128)(2,1)}, u32[]{:S(2)}) copy-start(bf16[2,48,512]{2,1,0:T(8,128)(2,1)} %param.7) | copy-start | bytes 294916
  32.6 111.8 %copy-start.8 = (bf16[2,48,64]{2,1,0:T(8,128)(2,1)S(1)}, bf16[2,48,64]{2,1,0:T(8,128)(2,1)}, u32[]{:S(2)}) copy-start(bf16[2,48,64]{2,1,0:T(8,128)(2,1)} %param.11) | copy-start | bytes 36868
  33.4 7.6 %collective-permute-start.11 = (bf16[2,128,128]{2,1,0:T(8,128)(2,1)}, bf16[2,128,128]{2,1,0:T(8,128)(2,1)S(1)}, u32[]{:S(2)}, u32[]{:S(2)}) collective-permute-start(bf16[2,128,128]{2,1,0:T(8,128)(2,1)} %get-tuple-element.46), channel_id=1, source_target_pairs={{0,15},{1,2},{2,1},{3,4},{4,3},{5,6},{6,5},{7,8},{8,7},{9,10},{10,... | collective-permute-start | bytes 196616 | tf_op jit(solution)/shard_map/ppermute | solution.py:98
  36.3 112.6 %copy-start.18 = (pred[8,128]{1,0:T(8,128)(4,1)}, pred[8,128]{1,0:T(8,128)(4,1)S(1)}, u32[]{:S(2)}) copy-start(pred[8,128]{1,0:T(8,128)(4,1)S(1)} %add_compare_fusion) | copy-start | bytes 3076
  40.9 8.5 %collective-permute-start.12 = (bf16[2,128,128]{2,1,0:T(8,128)(2,1)}, bf16[2,128,128]{2,1,0:T(8,128)(2,1)S(1)}, u32[]{:S(2)}, u32[]{:S(2)}) collective-permute-start(bf16[2,128,128]{2,1,0:T(8,128)(2,1)} %get-tuple-element.45), channel_id=1, source_target_pairs={{0,2},{1,15},{2,4},{3,1},{4,6},{5,3},{6,8},{7,5},{8,10},{9,7},{10,... | collective-permute-start | bytes 196616 | tf_op jit(solution)/shard_map/ppermute | solution.py:98
  49.4 9.6 %collective-permute-start.13 = (bf16[2,128,128]{2,1,0:T(8,128)(2,1)}, bf16[2,128,128]{2,1,0:T(8,128)(2,1)S(1)}, u32[]{:S(2)}, u32[]{:S(2)}) collective-permute-start(bf16[2,128,128]{2,1,0:T(8,128)(2,1)} %get-tuple-element.44), channel_id=1, source_target_pairs={{0,13},{1,4},{2,15},{3,6},{4,1},{5,8},{6,3},{7,10},{8,5},{9,12},{1... | collective-permute-start | bytes 196616 | tf_op jit(solution)/shard_map/ppermute | solution.py:98
  59.0 11.0 %collective-permute-start.14 = (bf16[2,128,128]{2,1,0:T(8,128)(2,1)}, bf16[2,128,128]{2,1,0:T(8,128)(2,1)S(1)}, u32[]{:S(2)}, u32[]{:S(2)}) collective-permute-start(bf16[2,128,128]{2,1,0:T(8,128)(2,1)} %get-tuple-element.43), channel_id=1, source_target_pairs={{0,4},{1,13},{2,6},{3,15},{4,8},{5,1},{6,10},{7,3},{8,12},{9,5},{1... | collective-permute-start | bytes 196616 | tf_op jit(solution)/shard_map/ppermute | solution.py:98
  70.0 12.2 %collective-permute-start.15 = (bf16[2,128,128]{2,1,0:T(8,128)(2,1)S(1)}, bf16[2,128,128]{2,1,0:T(8,128)(2,1)S(1)}, u32[]{:S(2)}, u32[]{:S(2)}) collective-permute-start(bf16[2,128,128]{2,1,0:T(8,128)(2,1)S(1)} %get-tuple-element.42), channel_id=1, source_target_pairs={{0,11},{1,6},{2,13},{3,8},{4,15},{5,10},{6,1},{7,12},{8,3},{9,14},... | collective-permute-start | bytes 196616 | tf_op jit(solution)/shard_map/ppermute | solution.py:98
  82.2 13.1 %collective-permute-start.16 = (bf16[2,128,128]{2,1,0:T(8,128)(2,1)S(1)}, bf16[2,128,128]{2,1,0:T(8,128)(2,1)S(1)}, u32[]{:S(2)}, u32[]{:S(2)}) collective-permute-start(bf16[2,128,128]{2,1,0:T(8,128)(2,1)S(1)} %get-tuple-element.41), channel_id=1, source_target_pairs={{0,6},{1,11},{2,8},{3,13},{4,10},{5,15},{6,12},{7,1},{8,14},{9,3},... | collective-permute-start | bytes 196616 | tf_op jit(solution)/shard_map/ppermute | solution.py:98
  95.2 14.0 %collective-permute-start.17 = (bf16[2,128,128]{2,1,0:T(8,128)(2,1)S(1)}, bf16[2,128,128]{2,1,0:T(8,128)(2,1)S(1)}, u32[]{:S(2)}, u32[]{:S(2)}) collective-permute-start(bf16[2,128,128]{2,1,0:T(8,128)(2,1)S(1)} %get-tuple-element.40), channel_id=1, source_target_pairs={{0,9},{1,8},{2,11},{3,10},{4,13},{5,12},{6,15},{7,14},{8,1},{9,0},... | collective-permute-start | bytes 196616 | tf_op jit(solution)/shard_map/ppermute | solution.py:98
  109.2 7.4 %collective-permute-start = (bf16[2,128,128]{2,1,0:T(8,128)(2,1)S(1)}, bf16[2,128,128]{2,1,0:T(8,128)(2,1)S(1)}, u32[]{:S(2)}, u32[]{:S(2)}) collective-permute-start(bf16[2,128,128]{2,1,0:T(8,128)(2,1)S(1)} %get-tuple-element.39), channel_id=1, source_target_pairs={{0,15},{1,2},{2,1},{3,4},{4,3},{5,6},{6,5},{7,8},{8,7},{9,10},{10,... | collective-permute-start | bytes 196616 | tf_op jit(solution)/shard_map/ppermute | solution.py:98
  116.6 8.3 %collective-permute-start.1 = (bf16[2,128,128]{2,1,0:T(8,128)(2,1)S(1)}, bf16[2,128,128]{2,1,0:T(8,128)(2,1)S(1)}, u32[]{:S(2)}, u32[]{:S(2)}) collective-permute-start(bf16[2,128,128]{2,1,0:T(8,128)(2,1)S(1)} %get-tuple-element.38), channel_id=1, source_target_pairs={{0,2},{1,15},{2,4},{3,1},{4,6},{5,3},{6,8},{7,5},{8,10},{9,7},{10,... | collective-permute-start | bytes 196616 | tf_op jit(solution)/shard_map/ppermute | solution.py:98
  124.8 9.4 %collective-permute-start.2 = (bf16[2,128,128]{2,1,0:T(8,128)(2,1)S(1)}, bf16[2,128,128]{2,1,0:T(8,128)(2,1)S(1)}, u32[]{:S(2)}, u32[]{:S(2)}) collective-permute-start(bf16[2,128,128]{2,1,0:T(8,128)(2,1)S(1)} %get-tuple-element.37), channel_id=1, source_target_pairs={{0,13},{1,4},{2,15},{3,6},{4,1},{5,8},{6,3},{7,10},{8,5},{9,12},{1... | collective-permute-start | bytes 196616 | tf_op jit(solution)/shard_map/ppermute | solution.py:98
  134.2 10.1 %collective-permute-start.3 = (bf16[2,128,128]{2,1,0:T(8,128)(2,1)S(1)}, bf16[2,128,128]{2,1,0:T(8,128)(2,1)S(1)}, u32[]{:S(2)}, u32[]{:S(2)}) collective-permute-start(bf16[2,128,128]{2,1,0:T(8,128)(2,1)S(1)} %get-tuple-element.36), channel_id=1, source_target_pairs={{0,4},{1,13},{2,6},{3,15},{4,8},{5,1},{6,10},{7,3},{8,12},{9,5},{1... | collective-permute-start | bytes 196616 | tf_op jit(solution)/shard_map/ppermute | solution.py:98
  154.5 23.6 %collective-permute-start.10 = (f32[4,48]{1,0:T(4,128)}, f32[4,48]{1,0:T(4,128)}, u32[]{:S(2)}, u32[]{:S(2)}) collective-permute-start(f32[4,48]{1,0:T(4,128)} %slice_select_fusion.5), channel_id=1, source_target_pairs={{0,1},{1,0},{2,3},{3,2},{4,5},{5,4},{6,7},{7,6},{8,9},{9,8},{10,11... | collective-permute-start | bytes 2312 | tf_op jit(solution)/shard_map/ppermute | solution.py:117
  156.4 25.6 %collective-permute-start.8 = (f32[4,48]{1,0:T(4,128)}, f32[4,48]{1,0:T(4,128)}, u32[]{:S(2)}, u32[]{:S(2)}) collective-permute-start(f32[4,48]{1,0:T(4,128)} %slice_select_fusion.6), channel_id=1, source_target_pairs={{0,1},{1,0},{2,3},{3,2},{4,5},{5,4},{6,7},{7,6},{8,9},{9,8},{10,11... | collective-permute-start | bytes 2312 | tf_op jit(solution)/shard_map/ppermute | solution.py:117
  164.6 18.2 %collective-permute-start.9 = (f32[4,48,128]{2,1,0:T(8,128)}, f32[4,48,128]{2,1,0:T(8,128)}, u32[]{:S(2)}, u32[]{:S(2)}) collective-permute-start(f32[4,48,128]{2,1,0:T(8,128)} %slice_select_fusion.1), channel_id=1, source_target_pairs={{0,1},{1,0},{2,3},{3,2},{4,5},{5,4},{6,7},{7,6},{8,9},{9,8},{10,11... | collective-permute-start | bytes 294920 | tf_op jit(solution)/shard_map/ppermute | solution.py:117
  170.5 12.3 %collective-permute-start.20 = (f32[4,48]{1,0:T(4,128)S(1)}, f32[4,48]{1,0:T(4,128)S(1)}, u32[]{:S(2)}, u32[]{:S(2)}) collective-permute-start(f32[4,48]{1,0:T(4,128)S(1)} %slice_select_fusion.2), channel_id=1, source_target_pairs={{0,1},{1,0},{2,3},{3,2},{4,5},{5,4},{6,7},{7,6},{8,9},{9,8},{10,11... | collective-permute-start | bytes 2312 | tf_op jit(solution)/shard_map/ppermute | solution.py:117
  174.4 8.4 %collective-permute-start.18 = (f32[4,48]{1,0:T(4,128)S(1)}, f32[4,48]{1,0:T(4,128)S(1)}, u32[]{:S(2)}, u32[]{:S(2)}) collective-permute-start(f32[4,48]{1,0:T(4,128)S(1)} %slice_select_fusion.3), channel_id=1, source_target_pairs={{0,1},{1,0},{2,3},{3,2},{4,5},{5,4},{6,7},{7,6},{8,9},{9,8},{10,11... | collective-permute-start | bytes 2312 | tf_op jit(solution)/shard_map/ppermute | solution.py:117
  178.1 6.5 %collective-permute-start.19 = (f32[4,48,128]{2,1,0:T(8,128)S(1)}, f32[4,48,128]{2,1,0:T(8,128)S(1)}, u32[]{:S(2)}, u32[]{:S(2)}) collective-permute-start(f32[4,48,128]{2,1,0:T(8,128)S(1)} %slice_select_fusion), channel_id=1, source_target_pairs={{0,1},{1,0},{2,3},{3,2},{4,5},{5,4},{6,7},{7,6},{8,9},{9,8},{10,11... | collective-permute-start | bytes 294920 | tf_op jit(solution)/shard_map/ppermute | solution.py:117
  (17 other events, 254.7 us)

commit v3 on v2

--- a/solution.py
+++ b/solution.py
@@ -79,7 +79,7 @@
     kv = jnp.stack(
         [key_cache.reshape(layers, local_len, KVH, DH), value_cache.reshape(layers, local_len, KVH, DH)], 1
     )
-    kv = jnp.transpose(kv, (0, 3, 1, 2, 4))
+    kv = jnp.transpose(kv, (3, 0, 1, 2, 4))
 
     sources = jnp.where(own == 0, d - jnp.arange(reach), d + jnp.arange(reach)) % n
     tree_keep = (
@@ -88,15 +88,15 @@
     cache_keep = sources[:, None] * local_len + jnp.arange(local_len)[None, :] < context_length[0]
     draft_keep = jnp.logical_and(tree_keep[:, None, :], (sources == 0)[None, :, None])
 
-    results = []
+    blocks = [lax.dynamic_index_in_dim(kv, pair, 0, keepdims=False)]
+    for j in range(1, reach):
+        target = jnp.where((d + j) % 2 == 0, (d + j) % n, (d - j) % n)
+        msg = lax.dynamic_index_in_dim(kv, target // 2, 0, keepdims=False)
+        blocks.append(lax.ppermute(msg, "ctx", [(s, send_target(s, j, n)) for s in range(n)]))
+    blocks = jnp.stack(blocks, 1)
+
+    keeps, gives = [], []
     for layer_index in range(layers):
-        here = kv[layer_index]
-        blocks = [lax.dynamic_index_in_dim(here, pair, 0, keepdims=False)]
-        for j in range(1, reach):
-            target = jnp.where((d + j) % 2 == 0, (d + j) % n, (d - j) % n)
-            msg = lax.dynamic_index_in_dim(here, target // 2, 0, keepdims=False)
-            blocks.append(lax.ppermute(msg, "ctx", [(s, send_target(s, j, n)) for s in range(n)]))
-        blocks = jnp.stack(blocks)
         f = first[layer_index]
         s2 = second[layer_index]
         query_heads = jnp.concatenate(
@@ -104,22 +104,26 @@
         )
         draft_k = jnp.concatenate([f[:, q_cols:q_cols + kv_cols], s2[:, q_cols:q_cols + kv_cols]], 1)
         draft_v = jnp.concatenate([f[:, q_cols + kv_cols:], s2[:, q_cols + kv_cols:]], 1)
+        here = blocks[layer_index]
         top, total, acc = blocks_partial(
-            query_heads, blocks[:, 0], blocks[:, 1], draft_k, draft_v, cache_keep, draft_keep, score_scale
+            query_heads, here[:, 0], here[:, 1], draft_k, draft_v, cache_keep, draft_keep, score_scale
         )
-        top = top.reshape(2, heads_here, rows)
-        total = total.reshape(2, heads_here, rows)
-        acc = acc.reshape(2, heads_here, rows, DH)
-        keep = (jnp.where(own == 0, top[0], top[1]), jnp.where(own == 0, total[0], total[1]),
-                jnp.where(own == 0, acc[0], acc[1]))
-        give = (jnp.where(own == 0, top[1], top[0]), jnp.where(own == 0, total[1], total[0]),
-                jnp.where(own == 0, acc[1], acc[0]))
-        got = lax.ppermute(give, "ctx", swap)
-        overall = jnp.maximum(keep[0], got[0])
-        f_keep = jnp.exp(keep[0] - overall)
-        f_got = jnp.exp(got[0] - overall)
-        mine = (keep[2] * f_keep[..., None] + got[2] * f_got[..., None]) / (
-            keep[1] * f_keep + got[1] * f_got
+        stats = jnp.concatenate([top, total, jnp.zeros((top.shape[0], DH - 2 * rows), jnp.float32)], 1)
+        merged = jnp.concatenate([acc, stats[:, None, :]], 1).reshape(2, heads_here, rows + 1, DH)
+        keeps.append(jnp.where(own == 0, merged[0], merged[1]))
+        gives.append(jnp.where(own == 0, merged[1], merged[0]))
+    keeps = jnp.stack(keeps)
+    gots = lax.ppermute(jnp.stack(gives), "ctx", swap)
+    results = []
+    for layer_index in range(layers):
+        keep, got = keeps[layer_index], gots[layer_index]
+        top_keep, total_keep = keep[:, rows, :rows], keep[:, rows, rows:2 * rows]
+        top_got, total_got = got[:, rows, :rows], got[:, rows, rows:2 * rows]
+        overall = jnp.maximum(top_keep, top_got)
+        f_keep = jnp.exp(top_keep - overall)
+        f_got = jnp.exp(top_got - overall)
+        mine = (keep[:, :rows] * f_keep[..., None] + got[:, :rows] * f_got[..., None]) / (
+            total_keep * f_keep + total_got * f_got
         )[..., None]
         results.append(jnp.transpose(mine, (1, 0, 2)).reshape(rows, heads_here * DH))
     return jnp.stack(results)

time: 187 us -> 104 us (0.56)
  waiting for transfers between devices: 82.2 us -> 27.8 us
  starting transfers between devices: 74.8 us -> 48.1 us
  other arithmetic: 12.2 us -> 8.11 us
  local copies, waits for them, and re-layouts: 7.28 us -> 11.3 us
    ppermute x14 -> x7, waiting for transfers between devices: 81.5 us -> 14.7 us  [body(): lax.ppermute(msg, 'ctx', [(s, send_target(s, j, n)) for s in range(n)])]
    ppermute x6 -> x1, starting transfers between devices: 17.5 us -> 1.92 us  [body(): gots = lax.ppermute(jnp.stack(gives), 'ctx', swap)]
    ppermute x14 -> x7, starting transfers between devices: 53.5 us -> 43.8 us  [body(): lax.ppermute(msg, 'ctx', [(s, send_target(s, j, n)) for s in range(n)])]
    ppermute x6 -> x1, waiting for transfers between devices: 0.67 us -> 7.43 us  [body(): gots = lax.ppermute(jnp.stack(gives), 'ctx', swap)]
    ppermute x1, waiting for transfers between devices: 0.01 us -> 5.68 us  [body(): partner = lax.ppermute(packed, 'ctx', swap)]
    unnamed x57 -> x29, local copies, waits for them, and re-layouts: 1.78 us -> 6.98 us
    convert_element_type x0 -> x3, other arithmetic: none -> 3.24 us  [the longest x2 1.83 us: blocks_partial(): cache_weight.astype(jnp.bfloat16)]
    reduce_sum x4 -> x1, other arithmetic: 4.94 us -> 2.3 us  [blocks_partial(): total = jnp.sum(cache_weight, -1) + jnp.sum(draft_weight, -1)]
  transfers between devices with their start and end apart: 21 -> 9, of which waited for: 12 -> 4; matrix products, arithmetic and copies ran while one was open for 8% -> 7% of each run, Pallas kernels for 0% -> 0%
where the time goes in v3:
time: 104 us
  starting transfers between devices  48.1 us (46%)
  waiting for transfers between devices  27.8 us (27%)
  local copies, waits for them, and re-layouts  11.3 us (11%)
  other arithmetic  8.11 us (8%)
  matrix products  7.11 us (7%)
  between operations  1.22 us (1%)
    ppermute x7, starting transfers between devices, body(): lax.ppermute(msg, 'ctx', [(s, send_target(s, j, n)) for s in range(n)])  43.8 us
    ppermute x7, waiting for transfers between devices, body(): lax.ppermute(msg, 'ctx', [(s, send_target(s, j, n)) for s in range(n)])  14.7 us
    ppermute x1, waiting for transfers between devices, body(): gots = lax.ppermute(jnp.stack(gives), 'ctx', swap)  7.43 us
    unnamed x29, local copies, waits for them, and re-layouts  6.98 us
    ppermute x1, waiting for transfers between devices, body(): partner = lax.ppermute(packed, 'ctx', swap)  5.68 us
    dot_general x2, matrix products, blocks_partial(): jnp.einsum('hqjt,td->hqjd', draft_weight.astype(jnp.bfloat16), draft_v, p...  3.37 us
    ppermute x1, starting transfers between devices, body(): partner = lax.ppermute(packed, 'ctx', swap)  2.46 us
    reduce_sum x1, other arithmetic, blocks_partial(): total = jnp.sum(cache_weight, -1) + jnp.sum(draft_weight, -1)  2.3 us
  transfers between devices with their start and end apart: 9, of which 4 were waited for; matrix products, arithmetic and copies ran while one was open for 7% of the time, Pallas kernels for 0%

profile of v3, /device:TPU:6, one launch (start us, length us, event | category | flops | bytes accessed | tf_op | source)
XLA Modules:
  0.0 103.8 jit_solution(3874581669458073455)
XLA Ops:
  0.0 1.2 %copy.120 = bf16[32,8,8,128]{3,2,1,0:T(8,128)(2,1)S(1)} copy(bf16[32,8,8,128]{3,1,2,0:T(8,128)(2,1)} %bitcast.224) | data formatting | bytes 1048576
  1.8 11.4 %collective-permute-start = (bf16[2,2,128,128]{3,2,1,0:T(8,128)(2,1)S(1)}, bf16[2,2,128,128]{3,2,1,0:T(8,128)(2,1)S(1)}, u32[]{:S(2)}, u32[]{:S(2)}) collective-permute-start(bf16[2,2,128,128]{3,2,1,0:T(8,128)(2,1)S(1)} %get-tuple-element.42), channel_id=1, source_target_pairs={{0,15},{1,2},{2,1},{3,4},{4,3},{5,6},{6,5},{7,8},{8,7},{9,10},{10,... | collective-permute-start | bytes 393224 | tf_op jit(solution)/shard_map/ppermute | solution.py:95
  13.2 1.9 %collective-permute-start.1 = (bf16[2,2,128,128]{3,2,1,0:T(8,128)(2,1)S(1)}, bf16[2,2,128,128]{3,2,1,0:T(8,128)(2,1)S(1)}, u32[]{:S(2)}, u32[]{:S(2)}) collective-permute-start(bf16[2,2,128,128]{3,2,1,0:T(8,128)(2,1)S(1)} %get-tuple-element.41), channel_id=1, source_target_pairs={{0,2},{1,15},{2,4},{3,1},{4,6},{5,3},{6,8},{7,5},{8,10},{9,7},{10,... | collective-permute-start | bytes 393224 | tf_op jit(solution)/shard_map/ppermute | solution.py:95
  15.1 6.5 %collective-permute-start.2 = (bf16[2,2,128,128]{3,2,1,0:T(8,128)(2,1)S(1)}, bf16[2,2,128,128]{3,2,1,0:T(8,128)(2,1)S(1)}, u32[]{:S(2)}, u32[]{:S(2)}) collective-permute-start(bf16[2,2,128,128]{3,2,1,0:T(8,128)(2,1)S(1)} %get-tuple-element.40), channel_id=1, source_target_pairs={{0,13},{1,4},{2,15},{3,6},{4,1},{5,8},{6,3},{7,10},{8,5},{9,12},{1... | collective-permute-start | bytes 393224 | tf_op jit(solution)/shard_map/ppermute | solution.py:95
  21.6 3.3 %collective-permute-start.3 = (bf16[2,2,128,128]{3,2,1,0:T(8,128)(2,1)S(1)}, bf16[2,2,128,128]{3,2,1,0:T(8,128)(2,1)S(1)}, u32[]{:S(2)}, u32[]{:S(2)}) collective-permute-start(bf16[2,2,128,128]{3,2,1,0:T(8,128)(2,1)S(1)} %get-tuple-element.39), channel_id=1, source_target_pairs={{0,4},{1,13},{2,6},{3,15},{4,8},{5,1},{6,10},{7,3},{8,12},{9,5},{1... | collective-permute-start | bytes 393224 | tf_op jit(solution)/shard_map/ppermute | solution.py:95
  25.0 2.5 %collective-permute-start.7 = (bf16[2,48,640]{2,1,0:T(8,128)(2,1)S(1)}, bf16[2,48,640]{2,1,0:T(8,128)(2,1)S(1)}, u32[]{:S(2)}, u32[]{:S(2)}) collective-permute-start(bf16[2,48,640]{2,1,0:T(8,128)(2,1)S(1)} %pad_maximum_fusion.2), channel_id=1, source_target_pairs={{0,1},{1,0},{2,3},{3,2},{4,5},{5,4},{6,7},{7,6},{8,9},{9,8},{10,11... | collective-permute-start | bytes 368648 | tf_op jit(solution)/shard_map/ppermute | solution.py:75
  29.3 5.7 %collective-permute-done.7 = bf16[2,48,640]{2,1,0:T(8,128)(2,1)S(1)} collective-permute-done((bf16[2,48,640]{2,1,0:T(8,128)(2,1)S(1)}, bf16[2,48,640]{2,1,0:T(8,128)(2,1)S(1)}, u32[]{:S(2)}, u32[]{:S(2)}) %collective-permute-start.7) | collective-permute-done | bytes 122912 | tf_op jit(solution)/shard_map/ppermute | solution.py:75
  35.0 7.6 %collective-permute-start.4 = (bf16[2,2,128,128]{3,2,1,0:T(8,128)(2,1)S(1)}, bf16[2,2,128,128]{3,2,1,0:T(8,128)(2,1)S(1)}, u32[]{:S(2)}, u32[]{:S(2)}) collective-permute-start(bf16[2,2,128,128]{3,2,1,0:T(8,128)(2,1)S(1)} %get-tuple-element.38), channel_id=1, source_target_pairs={{0,11},{1,6},{2,13},{3,8},{4,15},{5,10},{6,1},{7,12},{8,3},{9,14},... | collective-permute-start | bytes 393224 | tf_op jit(solution)/shard_map/ppermute | solution.py:95
  44.4 5.0 %collective-permute-start.5 = (bf16[2,2,128,128]{3,2,1,0:T(8,128)(2,1)S(1)}, bf16[2,2,128,128]{3,2,1,0:T(8,128)(2,1)S(1)}, u32[]{:S(2)}, u32[]{:S(2)}) collective-permute-start(bf16[2,2,128,128]{3,2,1,0:T(8,128)(2,1)S(1)} %get-tuple-element.37), channel_id=1, source_target_pairs={{0,6},{1,11},{2,8},{3,13},{4,10},{5,15},{6,12},{7,1},{8,14},{9,3},... | collective-permute-start | bytes 393224 | tf_op jit(solution)/shard_map/ppermute | solution.py:95
  49.4 0.7 bitcast_dynamic-update-slice_fusion.6
  50.1 8.1 %collective-permute-start.6 = (bf16[2,2,128,128]{3,2,1,0:T(8,128)(2,1)S(1)}, bf16[2,2,128,128]{3,2,1,0:T(8,128)(2,1)S(1)}, u32[]{:S(2)}, u32[]{:S(2)}) collective-permute-start(bf16[2,2,128,128]{3,2,1,0:T(8,128)(2,1)S(1)} %get-tuple-element.36), channel_id=1, source_target_pairs={{0,9},{1,8},{2,11},{3,10},{4,13},{5,12},{6,15},{7,14},{8,1},{9,0},... | collective-permute-start | bytes 393224 | tf_op jit(solution)/shard_map/ppermute | solution.py:95
  61.0 1.6 %collective-permute-done.5 = bf16[2,2,128,128]{3,2,1,0:T(8,128)(2,1)S(1)} collective-permute-done((bf16[2,2,128,128]{3,2,1,0:T(8,128)(2,1)S(1)}, bf16[2,2,128,128]{3,2,1,0:T(8,128)(2,1)S(1)}, u32[]{:S(2)}, u32[]{:S(2)}) %collective-permute-start.5) | collective-permute-done | bytes 131104 | tf_op jit(solution)/shard_map/ppermute | solution.py:95
  63.3 13.1 %collective-permute-done.6 = bf16[2,2,128,128]{3,2,1,0:T(8,128)(2,1)S(1)} collective-permute-done((bf16[2,2,128,128]{3,2,1,0:T(8,128)(2,1)S(1)}, bf16[2,2,128,128]{3,2,1,0:T(8,128)(2,1)S(1)}, u32[]{:S(2)}, u32[]{:S(2)}) %collective-permute-start.6) | collective-permute-done | bytes 131104 | tf_op jit(solution)/shard_map/ppermute | solution.py:95
  77.1 1.3 %slice_bitcast_fusion.1 = (bf16[8,2,128,128]{3,2,0,1:T(8,128)(2,1)S(1)}, bf16[8,2,128,128]{3,2,0,1:T(8,128)(2,1)S(1)}) fusion(bf16[2,8,2,128,128]{4,3,1,2,0:T(8,128)(2,1)} %bitcast_dynamic-update-slice_fusion), kind=kLoop, calls=%fused_computation.31 | loop fusion | bytes 2097152 | tf_op jit(solution)/shard_map/squeeze | solution.py:107
  79.2 0.9 fusion.8
  80.1 1.5 %fusion.17 = f32[8,128,384]{1,2,0} fusion(bf16[8,128,384]{1,2,0:T(8,128)(2,1)S(1)} %bitcast.218, bf16[8,2,128,128]{3,2,0,1:T(8,128)(2,1)S(1)} %get-tuple-element.34), kind=kOutput, calls=%fused_computation.38 | convolution fusion | flops 100663296 | bytes 2621440
  81.6 2.3 %fusion.2 = (f32[8,48,8]{2,1,0:T(8,128)S(1)}, f32[8,48,8]{2,1,0:T(8,128)S(1)}, bf16[8,48,8,48]{3,2,1,0:T(8,128)(2,1)}) fusion(f32[8,48,8]{2,1,0:T(8,128)S(1)} %copy.81, f32[8,48,48]{2,1,0:T(8,128)S(1)} %copy.79, pred[48,8,48]{2,1,0:T(8,128)(4,1)S(1)} %broadcast_and_fusion, f32[8,48,48]{2,1,0:T(8,128)S(1)} %copy.90), kind=kLoop, calls=%fused_computation.6 | loop fusion | flops 878592 | bytes 497664 | tf_op jit(solution)/shard_map/reduce_sum | solution.py:35
  85.0 1.4 %fusion.4 = (bf16[8,48,8,48]{3,2,1,0:T(8,128)(2,1)}, f32[8,48,8]{2,1,0:T(8,128)S(1)}) fusion(f32[8,48,8]{2,1,0:T(8,128)S(1)} %copy.92, f32[8,48,48]{2,1,0:T(8,128)S(1)} %copy.90, pred[48,8,48]{2,1,0:T(8,128)(4,1)S(1)} %broadcast_and_fusion), kind=kLoop, calls=%fused_computation.8 | loop fusion | flops 586752 | bytes 411648 | tf_op jit(solution)/shard_map/convert_element_type | solution.py:44
  86.4 0.9 fusion.10
  87.8 0.7 copy-done.2
  88.5 1.7 %multiply_reduce_fusion = f32[8,48,128]{2,1,0:T(8,128)S(1)} fusion(f32[8,48,8,128]{3,1,0,2:T(8,128)S(1)} %bitcast.223, bf16[8,48,8,48]{3,2,1,0:T(8,128)(2,1)S(1)} %copy-done.2, f32[8,48,8]{1,0,2:T(8,128)S(1)} %get-tuple-element.24, f32[8,48,8]{1,0,2:T(8,128)S(1)} %get-tuple-element.22, pred[8,48,8]{1,0,2:T(8,128)(4,1)S(1)} %get-tuple-element.25, ...), kind=kOutput, calls=%fused_computation.16 | convolution fusion | flops 40083456 | bytes 2104320 | tf_op jit(solution)/shard_map/hqjt,td->hqjd/dot_general | solution.py:42
  90.5 1.7 %multiply_reduce_fusion.1 = f32[8,48,128]{2,1,0:T(8,128)S(1)} fusion(f32[8,48,8,128]{3,1,0,2:T(8,128)S(1)} %bitcast.222, bf16[8,48,8,48]{3,2,1,0:T(8,128)(2,1)S(1)} %copy-done.1, f32[8,48,8]{1,0,2:T(8,128)S(1)} %get-tuple-element.19, f32[8,48,8]{1,0,2:T(8,128)S(1)} %get-tuple-element.17, pred[8,48,8]{1,0,2:T(8,128)(4,1)S(1)} %get-tuple-element.20, ...), kind=kOutput, calls=%fused_computation.18 | convolution fusion | flops 40083456 | bytes 2104320 | tf_op jit(solution)/shard_map/hqjt,td->hqjd/dot_general | solution.py:42
  92.3 1.9 %collective-permute-start.8 = (f32[2,4,49,128]{3,2,1,0:T(8,128)S(1)}, f32[2,4,49,128]{3,2,1,0:T(8,128)S(1)}, u32[]{:S(2)}, u32[]{:S(2)}) collective-permute-start(f32[2,4,49,128]{3,2,1,0:T(8,128)S(1)} %pad_maximum_fusion), channel_id=1, source_target_pairs={{0,1},{1,0},{2,3},{3,2},{4,5},{5,4},{6,7},{7,6},{8,9},{9,8},{10,11... | collective-permute-start | bytes 602120 | tf_op jit(solution)/shard_map/ppermute | solution.py:116
  94.2 7.4 %collective-permute-done.8 = f32[2,4,49,128]{3,2,1,0:T(8,128)S(1)} collective-permute-done((f32[2,4,49,128]{3,2,1,0:T(8,128)S(1)}, f32[2,4,49,128]{3,2,1,0:T(8,128)S(1)}, u32[]{:S(2)}, u32[]{:S(2)}) %collective-permute-start.8) | collective-permute-done | bytes 200736 | tf_op jit(solution)/shard_map/ppermute | solution.py:116
  (95 shorter events, 12.3 us)
Async XLA Ops:
  0.0 1.3 %copy-start.3 = (bf16[2,128,1024]{2,1,0:T(8,128)(2,1)S(1)}, bf16[2,128,1024]{2,1,0:T(8,128)(2,1)}, u32[]{:S(2)}) copy-start(bf16[2,128,1024]{2,1,0:T(8,128)(2,1)} %param.9) | copy-start | bytes 1572868
  1.4 23.5 %copy-start.4 = (bf16[2,48,512]{2,1,0:T(8,128)(2,1)S(1)}, bf16[2,48,512]{2,1,0:T(8,128)(2,1)}, u32[]{:S(2)}) copy-start(bf16[2,48,512]{2,1,0:T(8,128)(2,1)} %param.7) | copy-start | bytes 294916
  1.4 23.5 %copy-start.5 = (bf16[2,48,64]{2,1,0:T(8,128)(2,1)S(1)}, bf16[2,48,64]{2,1,0:T(8,128)(2,1)}, u32[]{:S(2)}) copy-start(bf16[2,48,64]{2,1,0:T(8,128)(2,1)} %param.11) | copy-start | bytes 36868
  1.4 23.4 %copy-start.6 = (bf16[2,48,64]{2,1,0:T(8,128)(2,1)S(1)}, bf16[2,48,64]{2,1,0:T(8,128)(2,1)}, u32[]{:S(2)}) copy-start(bf16[2,48,64]{2,1,0:T(8,128)(2,1)} %param.10) | copy-start | bytes 36868
  1.5 26.7 %copy-start.7 = (s32[2,24,24]{2,1,0:T(8,128)S(1)}, s32[2,24,24]{2,1,0:T(8,128)}, u32[]{:S(2)}) copy-start(s32[2,24,24]{2,1,0:T(8,128)} %param.12) | copy-start | bytes 13828
  1.8 42.7 %collective-permute-start = (bf16[2,2,128,128]{3,2,1,0:T(8,128)(2,1)S(1)}, bf16[2,2,128,128]{3,2,1,0:T(8,128)(2,1)S(1)}, u32[]{:S(2)}, u32[]{:S(2)}) collective-permute-start(bf16[2,2,128,128]{3,2,1,0:T(8,128)(2,1)S(1)} %get-tuple-element.42), channel_id=1, source_target_pairs={{0,15},{1,2},{2,1},{3,4},{4,3},{5,6},{6,5},{7,8},{8,7},{9,10},{10,... | collective-permute-start | bytes 393224 | tf_op jit(solution)/shard_map/ppermute | solution.py:95
  13.2 36.9 %collective-permute-start.1 = (bf16[2,2,128,128]{3,2,1,0:T(8,128)(2,1)S(1)}, bf16[2,2,128,128]{3,2,1,0:T(8,128)(2,1)S(1)}, u32[]{:S(2)}, u32[]{:S(2)}) collective-permute-start(bf16[2,2,128,128]{3,2,1,0:T(8,128)(2,1)S(1)} %get-tuple-element.41), channel_id=1, source_target_pairs={{0,2},{1,15},{2,4},{3,1},{4,6},{5,3},{6,8},{7,5},{8,10},{9,7},{10,... | collective-permute-start | bytes 393224 | tf_op jit(solution)/shard_map/ppermute | solution.py:95
  15.1 43.8 %collective-permute-start.2 = (bf16[2,2,128,128]{3,2,1,0:T(8,128)(2,1)S(1)}, bf16[2,2,128,128]{3,2,1,0:T(8,128)(2,1)S(1)}, u32[]{:S(2)}, u32[]{:S(2)}) collective-permute-start(bf16[2,2,128,128]{3,2,1,0:T(8,128)(2,1)S(1)} %get-tuple-element.40), channel_id=1, source_target_pairs={{0,13},{1,4},{2,15},{3,6},{4,1},{5,8},{6,3},{7,10},{8,5},{9,12},{1... | collective-permute-start | bytes 393224 | tf_op jit(solution)/shard_map/ppermute | solution.py:95
  21.6 38.1 %collective-permute-start.3 = (bf16[2,2,128,128]{3,2,1,0:T(8,128)(2,1)S(1)}, bf16[2,2,128,128]{3,2,1,0:T(8,128)(2,1)S(1)}, u32[]{:S(2)}, u32[]{:S(2)}) collective-permute-start(bf16[2,2,128,128]{3,2,1,0:T(8,128)(2,1)S(1)} %get-tuple-element.39), channel_id=1, source_target_pairs={{0,4},{1,13},{2,6},{3,15},{4,8},{5,1},{6,10},{7,3},{8,12},{9,5},{1... | collective-permute-start | bytes 393224 | tf_op jit(solution)/shard_map/ppermute | solution.py:95
  25.0 10.0 %collective-permute-start.7 = (bf16[2,48,640]{2,1,0:T(8,128)(2,1)S(1)}, bf16[2,48,640]{2,1,0:T(8,128)(2,1)S(1)}, u32[]{:S(2)}, u32[]{:S(2)}) collective-permute-start(bf16[2,48,640]{2,1,0:T(8,128)(2,1)S(1)} %pad_maximum_fusion.2), channel_id=1, source_target_pairs={{0,1},{1,0},{2,3},{3,2},{4,5},{5,4},{6,7},{7,6},{8,9},{9,8},{10,11... | collective-permute-start | bytes 368648 | tf_op jit(solution)/shard_map/ppermute | solution.py:75
  35.0 25.3 %collective-permute-start.4 = (bf16[2,2,128,128]{3,2,1,0:T(8,128)(2,1)S(1)}, bf16[2,2,128,128]{3,2,1,0:T(8,128)(2,1)S(1)}, u32[]{:S(2)}, u32[]{:S(2)}) collective-permute-start(bf16[2,2,128,128]{3,2,1,0:T(8,128)(2,1)S(1)} %get-tuple-element.38), channel_id=1, source_target_pairs={{0,11},{1,6},{2,13},{3,8},{4,15},{5,10},{6,1},{7,12},{8,3},{9,14},... | collective-permute-start | bytes 393224 | tf_op jit(solution)/shard_map/ppermute | solution.py:95
  44.4 18.2 %collective-permute-start.5 = (bf16[2,2,128,128]{3,2,1,0:T(8,128)(2,1)S(1)}, bf16[2,2,128,128]{3,2,1,0:T(8,128)(2,1)S(1)}, u32[]{:S(2)}, u32[]{:S(2)}) collective-permute-start(bf16[2,2,128,128]{3,2,1,0:T(8,128)(2,1)S(1)} %get-tuple-element.37), channel_id=1, source_target_pairs={{0,6},{1,11},{2,8},{3,13},{4,10},{5,15},{6,12},{7,1},{8,14},{9,3},... | collective-permute-start | bytes 393224 | tf_op jit(solution)/shard_map/ppermute | solution.py:95
  50.1 26.3 %collective-permute-start.6 = (bf16[2,2,128,128]{3,2,1,0:T(8,128)(2,1)S(1)}, bf16[2,2,128,128]{3,2,1,0:T(8,128)(2,1)S(1)}, u32[]{:S(2)}, u32[]{:S(2)}) collective-permute-start(bf16[2,2,128,128]{3,2,1,0:T(8,128)(2,1)S(1)} %get-tuple-element.36), channel_id=1, source_target_pairs={{0,9},{1,8},{2,11},{3,10},{4,13},{5,12},{6,15},{7,14},{8,1},{9,0},... | collective-permute-start | bytes 393224 | tf_op jit(solution)/shard_map/ppermute | solution.py:95
  87.4 1.1 %copy-start.2 = (bf16[8,48,8,48]{3,2,1,0:T(8,128)(2,1)S(1)}, bf16[8,48,8,48]{3,2,1,0:T(8,128)(2,1)}, u32[]{:S(2)}) copy-start(bf16[8,48,8,48]{3,2,1,0:T(8,128)(2,1)} %get-tuple-element.44) | copy-start | bytes 884740
  88.5 2.0 %copy-start = (f32[8,128,384]{1,2,0:S(1)}, f32[8,128,384]{1,2,0}, u32[]{:S(2)}) copy-start(f32[8,128,384]{1,2,0} %fusion.17) | copy-start | bytes 4718596
  88.5 2.0 %copy-start.1 = (bf16[8,48,8,48]{3,2,1,0:T(8,128)(2,1)S(1)}, bf16[8,48,8,48]{3,2,1,0:T(8,128)(2,1)}, u32[]{:S(2)}) copy-start(bf16[8,48,8,48]{3,2,1,0:T(8,128)(2,1)} %get-tuple-element.43) | copy-start | bytes 884740
  92.3 9.4 %collective-permute-start.8 = (f32[2,4,49,128]{3,2,1,0:T(8,128)S(1)}, f32[2,4,49,128]{3,2,1,0:T(8,128)S(1)}, u32[]{:S(2)}, u32[]{:S(2)}) collective-permute-start(f32[2,4,49,128]{3,2,1,0:T(8,128)S(1)} %pad_maximum_fusion), channel_id=1, source_target_pairs={{0,1},{1,0},{2,3},{3,2},{4,5},{5,4},{6,7},{7,6},{8,9},{9,8},{10,11... | collective-permute-start | bytes 602120 | tf_op jit(solution)/shard_map/ppermute | solution.py:116

commit v4 on v2

v4 whole, which is shorter than its diff:
```python
import math

import jax
import jax.numpy as jnp
from jax import lax
from jax.sharding import PartitionSpec as P

H = 64
KVH = 8
DH = 128


masked_score = -1e30


def send_target(s, j, n):
    return (s + j) % n if (s + j) % 2 == 0 else (s - j) % n


def blocks_partial(query_heads, block_keys, block_values, draft_k, draft_v, cache_keep, draft_keep, score_scale):
    scores = (
        jnp.einsum("qhd,jpd->hqjp", query_heads, block_keys, preferred_element_type=jnp.float32)
        * score_scale
    )
    draft_scores = (
        jnp.einsum("qhd,td->hqt", query_heads, draft_k, preferred_element_type=jnp.float32)
        * score_scale
    )
    scores = jnp.where(cache_keep[None, None], scores, masked_score)
    draft_scores = jnp.where(draft_keep[None], draft_scores[:, :, None, :], masked_score)
    top_score = jnp.maximum(jnp.max(scores, -1), jnp.max(draft_scores, -1))
    shift_by = jnp.where(top_score > -1e29, top_score, 0.0)
    cache_weight = jnp.exp(scores - shift_by[..., None])
    draft_weight = jnp.exp(draft_scores - shift_by[..., None])
    total = jnp.sum(cache_weight, -1) + jnp.sum(draft_weight, -1)
    weighted = jnp.einsum(
        "hqjp,jpd->hqjd",
        cache_weight.astype(jnp.bfloat16),
        block_values,
        preferred_element_type=jnp.float32,
    )
    weighted = weighted + jnp.einsum(
        "hqjt,td->hqjd",
        draft_weight.astype(jnp.bfloat16),
        draft_v,
        preferred_element_type=jnp.float32,
    )
    alive = total > 0.0
    safe_total = jnp.where(alive, total, 1.0)
    output = lax.reduce_precision(
        jnp.where(alive[..., None], weighted / safe_total[..., None], 0.0), exponent_bits=8, mantissa_bits=7
    )
    lse = jnp.where(alive, top_score + jnp.log(safe_total), masked_score)
    top = jnp.max(lse, -1)
    factor = jnp.where(lse > -1e29, jnp.exp(lse - top[..., None]), 0.0)
    return top, jnp.sum(factor, -1), jnp.sum(factor[..., None] * output, 2)


def body(queries, key_cache, value_cache, draft_keys, draft_values, ancestors, context_length):
    n = lax.axis_size("ctx")
    d = lax.axis_index("ctx")
    layers, rows, q_cols = queries.shape
    assert n == KVH * layers
    kv_cols = draft_keys.shape[2]
    local_len = key_cache.shape[1]
    trees = ancestors.shape[0]
    heads_here = H // n
    score_scale = 1.0 / math.sqrt(DH)
    own = d % layers
    swap = [(s, s ^ 1) for s in range(n)]

    packed = jnp.concatenate([queries, draft_keys, draft_values], axis=2)
    mine_now = lax.dynamic_index_in_dim(packed, own, 0, keepdims=False)
    partner = lax.ppermute(lax.dynamic_index_in_dim(packed, 1 - own, 0, keepdims=False), "ctx", swap)
    first = jnp.where(own == 0, mine_now, partner)
    second = jnp.where(own == 0, partner, mine_now)

    kv = jnp.stack(
        [key_cache.reshape(layers, local_len, KVH, DH), value_cache.reshape(layers, local_len, KVH, DH)], 1
    )
    kv = jnp.transpose(kv, (3, 0, 1, 2, 4)).reshape(n, 2, local_len, DH)
    blocks = lax.all_to_all(kv, "ctx", 0, 0, tiled=True)

    sources = jnp.arange(n)
    tree_keep = (
        jnp.eye(trees, dtype=jnp.int32)[:, None, :, None] * ancestors[:, :, None, :]
    ).reshape(rows, rows) > 0
    cache_keep = sources[:, None] * local_len + jnp.arange(local_len)[None, :] < context_length[0]
    draft_keep = jnp.logical_and(tree_keep[:, None, :], (sources == 0)[None, :, None])

    query_heads = jnp.concatenate(
        [first[:, :q_cols].reshape(rows, heads_here, DH), second[:, :q_cols].reshape(rows, heads_here, DH)], 1
    )
    draft_k = jnp.concatenate([first[:, q_cols:q_cols + kv_cols], second[:, q_cols:q_cols + kv_cols]], 1)
    draft_v = jnp.concatenate([first[:, q_cols + kv_cols:], second[:, q_cols + kv_cols:]], 1)
    top, total, acc = blocks_partial(
        query_heads, blocks[:, 0], blocks[:, 1], draft_k, draft_v, cache_keep, draft_keep, score_scale
    )
    done = (acc / total[..., None]).reshape(2, heads_here, rows, DH)
    keep = jnp.where(own == 0, done[0], done[1])
    got = lax.ppermute(jnp.where(own == 0, done[1], done[0]), "ctx", swap)
    keep = jnp.transpose(keep, (1, 0, 2)).reshape(rows, heads_here * DH)
    got = jnp.transpose(got, (1, 0, 2)).reshape(rows, heads_here * DH)
    return jnp.stack([jnp.where(own == 0, keep, got), jnp.where(own == 0, got, keep)])


def solution(mesh):
    placed = (
        P("req", None, "ctx"),
        P("req", "ctx", None),
        P("req", "ctx", None),
        P("req", None, "ctx"),
        P("req", None, "ctx"),
        P("req", None, None),
        P("req"),
    )
    return jax.shard_map(
        body, mesh=mesh, in_specs=placed, out_specs=P("req", None, "ctx"), check_vma=False
    )
```

time: 187 us -> 95.6 us (0.51)
  starting transfers between devices: 74.8 us -> 21.4 us
  waiting for transfers between devices: 82.2 us -> 47.7 us
    ppermute x21 -> x2, starting transfers between devices: 74.8 us -> 6.17 us  [the longest x1 3.76 us: body(): lax.ppermute(lax.dynamic_index_in_dim(packed, 1 - own, 0, keepdims=False)...]
    ppermute x21 -> x2, waiting for transfers between devices: 82.2 us -> 47.7 us  [the longest x1 43.6 us: body(): lax.ppermute(lax.dynamic_index_in_dim(packed, 1 - own, 0, keepdims=False)...]
    all_to_all x0 -> x1, starting transfers between devices: none -> 15.2 us  [body(): blocks = lax.all_to_all(kv, 'ctx', 0, 0, tiled=True)]
    slice x5 -> x1, local copies, waits for them, and re-layouts: 2.8 us -> 0.67 us  [body(): first[:, q_cols + kv_cols:]]
    select_n x7 -> x3, other arithmetic: 1.93 us -> 0.05 us  [the longest x1 0.02 us: body(): jnp.where(own == 0, keep, got)]
    dot_general x2 -> x1, matrix products: 4.52 us -> 3.3 us  [blocks_partial(): jnp.einsum('hqjt,td->hqjd', draft_weight.astype(jnp.bfloat16), draft_v, p...]
    reduce_sum x4 -> x2, other arithmetic: 4.94 us -> 5.68 us  [blocks_partial(): total = jnp.sum(cache_weight, -1) + jnp.sum(draft_weight, -1)]
  transfers between devices with their start and end apart: 21 -> 3, of which waited for: 12 -> 2; matrix products, arithmetic and copies ran while one was open for 8% -> 4% of each run, Pallas kernels for 0% -> 0%
where the time goes in v4:
time: 95.6 us; the launch traced here: 95.2 us
  waiting for transfers between devices  47.7 us (50%)
  starting transfers between devices  21.4 us (22%)
  other arithmetic  11.6 us (12%)
  matrix products  7.31 us (8%)
  local copies, waits for them, and re-layouts  6.19 us (6%)
  between operations  0.96 us (1%)
    ppermute x1, waiting for transfers between devices, body(): lax.ppermute(lax.dynamic_index_in_dim(packed, 1 - own, 0, keepdims=False)...  43.6 us
    all_to_all x1, starting transfers between devices, body(): blocks = lax.all_to_all(kv, 'ctx', 0, 0, tiled=True)  15.2 us
    reduce_sum x2, other arithmetic, blocks_partial(): total = jnp.sum(cache_weight, -1) + jnp.sum(draft_weight, -1)  5.68 us
    ppermute x1, waiting for transfers between devices, body(): got = lax.ppermute(jnp.where(own == 0, done[1], done[0]), 'ctx', swap)  4.09 us
    ppermute x1, starting transfers between devices, body(): lax.ppermute(lax.dynamic_index_in_dim(packed, 1 - own, 0, keepdims=False)...  3.76 us
    dot_general x1, matrix products, blocks_partial(): jnp.einsum('hqjt,td->hqjd', draft_weight.astype(jnp.bfloat16), draft_v, p...  3.3 us
    ppermute x1, starting transfers between devices, body(): got = lax.ppermute(jnp.where(own == 0, done[1], done[0]), 'ctx', swap)  2.41 us
    unnamed x19, local copies, waits for them, and re-layouts  2.36 us
  transfers between devices with their start and end apart: 3, of which 2 were waited for; matrix products, arithmetic and copies ran while one was open for 4% of the time, Pallas kernels for 0%

profile of v4, /device:TPU:6, one launch (start us, length us, event | category | flops | bytes accessed | tf_op | source)
XLA Modules:
  0.0 95.2 jit_solution(9214782924277161885)
XLA Ops:
  0.0 1.1 %copy.69 = bf16[32,8,8,128]{3,2,1,0:T(8,128)(2,1)S(1)} copy(bf16[32,8,8,128]{3,1,2,0:T(8,128)(2,1)} %bitcast.83) | data formatting | bytes 1048576
  1.3 1.2 %copy.68 = bf16[32,8,8,128]{3,2,1,0:T(8,128)(2,1)S(1)} copy(bf16[32,8,8,128]{3,1,2,0:T(8,128)(2,1)} %bitcast.84) | data formatting | bytes 1048576
  2.6 1.1 %pad_maximum_fusion = bf16[2,2,128,8,128]{4,2,1,0,3:T(8,128)(2,1)} fusion(bf16[2,1,128,8,128]{4,2,1,0,3:T(8,128)(2,1)S(1)} %copy.49, bf16[2,1,128,8,128]{4,2,1,0,3:T(8,128)(2,1)S(1)} %copy.48), kind=kLoop, calls=%fused_computation.15 | loop fusion | flops 524288 | bytes 2097152 | tf_op jit(solution)/shard_map/stack | solution.py:78
  3.7 15.2 %all-to-all-start = ((bf16[16,2,128,128]{3,2,1,0:T(8,128)(2,1)}), bf16[16,2,128,128]{3,2,1,0:T(8,128)(2,1)}, u32[]{:S(2)}, u32[]{:S(2)}) async-start(bf16[16,2,128,128]{3,2,1,0:T(8,128)(2,1)} %bitcast.2), calls=%async_computation | async-start | bytes 2097152 | tf_op jit(solution)/shard_map/all_to_all | solution.py:82
  19.1 3.8 %collective-permute-start = (bf16[48,640]{1,0:T(8,128)(2,1)S(1)}, bf16[48,640]{1,0:T(8,128)(2,1)S(1)}, u32[]{:S(2)}, u32[]{:S(2)}) collective-permute-start(bf16[48,640]{1,0:T(8,128)(2,1)S(1)} %dynamic-slice_bitcast_fusion), channel_id=1, source_target_pairs={{0,1},{1,0},{2,3},{3,2},{4,5},{5,4},{6,7},{7,6},{8,9},{9,8},{10,11... | collective-permute-start | bytes 184328 | tf_op jit(solution)/shard_map/ppermute | solution.py:74
  23.9 43.6 %collective-permute-done = bf16[48,640]{1,0:T(8,128)(2,1)S(1)} collective-permute-done((bf16[48,640]{1,0:T(8,128)(2,1)S(1)}, bf16[48,640]{1,0:T(8,128)(2,1)S(1)}, u32[]{:S(2)}, u32[]{:S(2)}) %collective-permute-start) | collective-permute-done | bytes 61472 | tf_op jit(solution)/shard_map/ppermute | solution.py:74
  67.5 0.7 fusion.19
  68.2 0.2 fusion.7
  68.6 1.1 %select_reduce_fusion = f32[8,48,16]{2,1,0:T(8,128)S(1)} fusion(f32[8,48,48]{2,1,0:T(8,128)S(1)} %copy.53, pred[48,16,48]{2,1,0:T(8,128)(4,1)S(1)} %broadcast_and_fusion), kind=kLoop, calls=%fused_computation.1 | loop fusion | flops 583680 | bytes 135168 | tf_op jit(solution)/shard_map/reduce_max | solution.py:31
  69.8 0.7 copy.54
  70.5 2.2 %bitcast_reduce_fusion = (f32[8,48,16]{1,0,2:T(8,128)S(1)}, f32[16,128,48,8]{1,2,3,0:T(8,128)S(1)}) fusion(pred[16,128]{1,0:T(8,128)(4,1)S(1)} %add_compare_fusion, bf16[48,8,128]{2,0,1:T(8,128)(2,1)S(1)} %bitcast_dynamic-update-slice_fusion, bf16[16,2,128,128]{3,2,1,0:T(8,128)(2,1)} %all-to-all-done), kind=kOutput, calls=%fused_computation.6 | convolution fusion | flops 203679744 | bytes 3794944 | tf_op jit(solution)/shard_map/qhd,jpd->hqjp/dot_general | solution.py:22
  72.7 0.6 compare_select_fusion
  73.3 0.8 copy.55
  74.1 3.0 %fusion.5 = (f32[8,48,16]{1,0,2:T(8,128)}, bf16[8,48,16,128]{3,1,0,2:T(8,128)(2,1)}) fusion(f32[16,128,48,8]{1,2,3,0:T(8,128)S(1)} %get-tuple-element.25, f32[8,48,16]{1,0,2:T(8,128)S(1)} %get-tuple-element.10, pred[16,128]{1,0:T(8,128)(4,1)S(1)} %add_compare_fusion), kind=kLoop, calls=%fused_computation.11 | loop fusion | flops 3926016 | bytes 4769792 | tf_op jit(solution)/shard_map/reduce_sum | solution.py:35
  77.1 2.7 %fusion.2 = (f32[8,48,16]{2,1,0:T(8,128)}, bf16[8,48,16,48]{3,2,1,0:T(8,128)(2,1)S(1)}) fusion(f32[8,48,16]{2,1,0:T(8,128)S(1)} %copy-done.1, f32[8,48,48]{2,1,0:T(8,128)S(1)} %copy.53, pred[48,16,48]{2,1,0:T(8,128)(4,1)S(1)} %broadcast_and_fusion), kind=kLoop, calls=%fused_computation.4 | loop fusion | flops 1173504 | bytes 749568 | tf_op jit(solution)/shard_map/reduce_sum | solution.py:35
  79.8 1.0 %copy.56 = f32[8,48,16]{1,0,2:T(8,128)S(1)} copy(f32[8,48,16]{2,1,0:T(8,128)} %get-tuple-element.14) | data formatting | bytes 49152 | tf_op jit(solution)/shard_map/reduce_sum | solution.py:35
  80.9 0.9 fusion.11
  81.8 0.9 fusion.18
  82.7 1.6 %fusion.8 = f32[16,128,384]{1,2,0:S(1)} fusion(bf16[16,128,384]{1,2,0:T(8,128)(2,1)S(1)} %bitcast.79, bf16[16,2,128,128]{3,2,1,0:T(8,128)(2,1)} %all-to-all-done), kind=kOutput, calls=%fused_computation.17 | convolution fusion | flops 201326592 | bytes 5242880
  84.3 3.3 %multiply_reduce_fusion = f32[8,48,128]{2,1,0:T(8,128)S(1)} fusion(f32[8,48,16,128]{3,1,0,2:T(8,128)S(1)} %bitcast.80, bf16[8,48,16,48]{3,2,1,0:T(8,128)(2,1)S(1)} %get-tuple-element.15, f32[8,48,16]{1,0,2:T(8,128)S(1)} %get-tuple-element.8, f32[8,48,16]{1,0,2:T(8,128)S(1)} %get-tuple-element.6, pred[8,48,16]{1,0,2:T(8,128)(4,1)S(1)} %get-tuple-element.9, ...), kind=kOutput, calls=%fused_computation.8 | convolution fusion | flops 80191488 | bytes 3999744 | tf_op jit(solution)/shard_map/hqjt,td->hqjd/dot_general | solution.py:42
  87.6 0.1 broadcast_divide_fusion
  87.7 2.4 %collective-permute-start.1 = (f32[4,48,128]{2,1,0:T(8,128)S(1)}, f32[4,48,128]{2,1,0:T(8,128)S(1)}, u32[]{:S(2)}, u32[]{:S(2)}) collective-permute-start(f32[4,48,128]{2,1,0:T(8,128)S(1)} %slice_select_fusion), channel_id=1, source_target_pairs={{0,1},{1,0},{2,3},{3,2},{4,5},{5,4},{6,7},{7,6},{8,9},{9,8},{10,11... | collective-permute-start | bytes 294920 | tf_op jit(solution)/shard_map/ppermute | solution.py:101
  90.2 4.1 %collective-permute-done.1 = f32[4,48,128]{2,1,0:T(8,128)S(1)} collective-permute-done((f32[4,48,128]{2,1,0:T(8,128)S(1)}, f32[4,48,128]{2,1,0:T(8,128)S(1)}, u32[]{:S(2)}, u32[]{:S(2)}) %collective-permute-start.1) | collective-permute-done | bytes 98336 | tf_op jit(solution)/shard_map/ppermute | solution.py:101
  94.5 0.7 pad_maximum_fusion.1
  (38 shorter events, 1.1 us)
Async XLA Ops:
  1.2 17.7 %copy-start.3 = (bf16[2,48,512]{2,1,0:T(8,128)(2,1)S(1)}, bf16[2,48,512]{2,1,0:T(8,128)(2,1)}, u32[]{:S(2)}) copy-start(bf16[2,48,512]{2,1,0:T(8,128)(2,1)} %param.7) | copy-start | bytes 294916
  1.3 17.7 %copy-start.4 = (bf16[2,48,64]{2,1,0:T(8,128)(2,1)S(1)}, bf16[2,48,64]{2,1,0:T(8,128)(2,1)}, u32[]{:S(2)}) copy-start(bf16[2,48,64]{2,1,0:T(8,128)(2,1)} %param.11) | copy-start | bytes 36868
  1.3 17.7 %copy-start.5 = (bf16[2,48,64]{2,1,0:T(8,128)(2,1)S(1)}, bf16[2,48,64]{2,1,0:T(8,128)(2,1)}, u32[]{:S(2)}) copy-start(bf16[2,48,64]{2,1,0:T(8,128)(2,1)} %param.10) | copy-start | bytes 36868
  1.3 22.2 %copy-start.6 = (s32[2,24,24]{2,1,0:T(8,128)S(1)}, s32[2,24,24]{2,1,0:T(8,128)}, u32[]{:S(2)}) copy-start(s32[2,24,24]{2,1,0:T(8,128)} %param.12) | copy-start | bytes 13828
  3.7 66.8 %all-to-all-start = ((bf16[16,2,128,128]{3,2,1,0:T(8,128)(2,1)}), bf16[16,2,128,128]{3,2,1,0:T(8,128)(2,1)}, u32[]{:S(2)}, u32[]{:S(2)}) async-start(bf16[16,2,128,128]{3,2,1,0:T(8,128)(2,1)} %bitcast.2), calls=%async_computation | async-start | bytes 2097152 | tf_op jit(solution)/shard_map/all_to_all | solution.py:82
  19.1 48.5 %collective-permute-start = (bf16[48,640]{1,0:T(8,128)(2,1)S(1)}, bf16[48,640]{1,0:T(8,128)(2,1)S(1)}, u32[]{:S(2)}, u32[]{:S(2)}) collective-permute-start(bf16[48,640]{1,0:T(8,128)(2,1)S(1)} %dynamic-slice_bitcast_fusion), channel_id=1, source_target_pairs={{0,1},{1,0},{2,3},{3,2},{4,5},{5,4},{6,7},{7,6},{8,9},{9,8},{10,11... | collective-permute-start | bytes 184328 | tf_op jit(solution)/shard_map/ppermute | solution.py:74
  70.5 2.2 %copy-start.2 = (f32[8,48,16]{1,0,2:T(8,128)S(1)}, f32[8,48,16]{1,0,2:T(8,128)}, u32[]{:S(2)}) copy-start(f32[8,48,16]{1,0,2:T(8,128)} %copy.54) | copy-start | bytes 73732
  74.1 3.0 %copy-start.1 = (f32[8,48,16]{2,1,0:T(8,128)S(1)}, f32[8,48,16]{2,1,0:T(8,128)}, u32[]{:S(2)}) copy-start(f32[8,48,16]{2,1,0:T(8,128)} %copy.55) | copy-start | bytes 73732
  77.1 5.5 %copy-start = (bf16[8,48,16,128]{3,1,0,2:T(8,128)(2,1)S(1)}, bf16[8,48,16,128]{3,1,0,2:T(8,128)(2,1)}, u32[]{:S(2)}) copy-start(bf16[8,48,16,128]{3,1,0,2:T(8,128)(2,1)} %get-tuple-element.13) | copy-start | bytes 4718596
  79.8 4.5 %copy-start.7 = (bf16[48,64]{1,0:T(8,128)(2,1)S(1)}, bf16[48,64]{1,0:T(8,128)(2,1)}, u32[]{:S(2)}) copy-start(bf16[48,64]{1,0:T(8,128)(2,1)} %get-tuple-element.27) | copy-start | bytes 18436
  87.7 6.5 %collective-permute-start.1 = (f32[4,48,128]{2,1,0:T(8,128)S(1)}, f32[4,48,128]{2,1,0:T(8,128)S(1)}, u32[]{:S(2)}, u32[]{:S(2)}) collective-permute-start(f32[4,48,128]{2,1,0:T(8,128)S(1)} %slice_select_fusion), channel_id=1, source_target_pairs={{0,1},{1,0},{2,3},{3,2},{4,5},{5,4},{6,7},{7,6},{8,9},{9,8},{10,11... | collective-permute-start | bytes 294920 | tf_op jit(solution)/shard_map/ppermute | solution.py:101

commit v5 on v4

--- a/solution.py
+++ b/solution.py
@@ -3,6 +3,8 @@
 import jax
 import jax.numpy as jnp
 from jax import lax
+from jax.experimental import pallas as pl
+from jax.experimental.pallas import tpu as pltpu
 from jax.sharding import PartitionSpec as P
 
 H = 64
@@ -56,6 +58,60 @@
     return top, jnp.sum(factor, -1), jnp.sum(factor[..., None] * output, 2)
 
 
+def _dot(a, b, dims):
+    return lax.dot_general(a, b, dims, preferred_element_type=jnp.float32)
+
+
+def attend_kernel(len_ref, q_ref, k_ref, v_ref, dk_ref, dv_ref, tree_ref, o_ref, out_sc, lse_sc):
+    blocks, block_len, _ = k_ref.shape
+    score_scale = 1.0 / math.sqrt(DH)
+    nt = (((1,), (1,)), ((), ()))
+    nn = (((1,), (0,)), ((), ()))
+    q = q_ref[...]
+    ctx_len = len_ref[0]
+    for j in range(blocks):
+        scores = _dot(q, k_ref[j], nt) * score_scale
+        pos = j * block_len + lax.broadcasted_iota(jnp.int32, scores.shape, 1)
+        scores = jnp.where(pos < ctx_len, scores, masked_score)
+        top = jnp.max(scores, axis=1, keepdims=True)
+        if j == 0:
+            draft = _dot(q, dk_ref[...], nt) * score_scale
+            draft = jnp.where(tree_ref[...] > 0, draft, masked_score)
+            top = jnp.maximum(top, jnp.max(draft, axis=1, keepdims=True))
+        shift = jnp.where(top > -1e29, top, 0.0)
+        weight = jnp.exp(scores - shift)
+        total = jnp.sum(weight, axis=1, keepdims=True)
+        acc = _dot(weight.astype(jnp.bfloat16), v_ref[j], nn)
+        if j == 0:
+            draft_weight = jnp.exp(draft - shift)
+            total = total + jnp.sum(draft_weight, axis=1, keepdims=True)
+            acc = acc + _dot(draft_weight.astype(jnp.bfloat16), dv_ref[...], nn)
+        alive = total > 0.0
+        safe = jnp.where(alive, total, 1.0)
+        out_sc[j] = jnp.where(alive, acc / safe, 0.0).astype(jnp.bfloat16).astype(jnp.float32)
+        lse_sc[:, j:j + 1] = jnp.where(alive, top + jnp.log(safe), masked_score)
+    lse = lse_sc[...]
+    overall = jnp.max(lse, axis=1, keepdims=True)
+    factor = jnp.exp(lse - overall)
+    weighted = factor[:, 0:1] * out_sc[0]
+    for j in range(1, blocks):
+        weighted = weighted + factor[:, j:j + 1] * out_sc[j]
+    o_ref[...] = weighted / jnp.sum(factor, axis=1, keepdims=True)
+
+
+def attend(context_length, q_rows, block_keys, block_values, draft_k, draft_v, tree_rows):
+    rows = q_rows.shape[0]
+    blocks = block_keys.shape[0]
+    vmem = pl.BlockSpec(memory_space=pltpu.VMEM)
+    return pl.pallas_call(
+        attend_kernel,
+        out_shape=jax.ShapeDtypeStruct((rows, DH), jnp.float32),
+        in_specs=[pl.BlockSpec(memory_space=pltpu.SMEM)] + [vmem] * 6,
+        out_specs=vmem,
+        scratch_shapes=[pltpu.VMEM((blocks, rows, DH), jnp.float32), pltpu.VMEM((rows, blocks), jnp.float32)],
+    )(context_length, q_rows, block_keys, block_values, draft_k, draft_v, tree_rows)
+
+
 def body(queries, key_cache, value_cache, draft_keys, draft_values, ancestors, context_length):
     n = lax.axis_size("ctx")
     d = lax.axis_index("ctx")
@@ -81,22 +137,19 @@
     kv = jnp.transpose(kv, (3, 0, 1, 2, 4)).reshape(n, 2, local_len, DH)
     blocks = lax.all_to_all(kv, "ctx", 0, 0, tiled=True)
 
-    sources = jnp.arange(n)
     tree_keep = (
         jnp.eye(trees, dtype=jnp.int32)[:, None, :, None] * ancestors[:, :, None, :]
-    ).reshape(rows, rows) > 0
-    cache_keep = sources[:, None] * local_len + jnp.arange(local_len)[None, :] < context_length[0]
-    draft_keep = jnp.logical_and(tree_keep[:, None, :], (sources == 0)[None, :, None])
-
+    ).reshape(rows, rows)
+    pair_heads = 2 * heads_here
     query_heads = jnp.concatenate(
         [first[:, :q_cols].reshape(rows, heads_here, DH), second[:, :q_cols].reshape(rows, heads_here, DH)], 1
     )
+    q_rows = jnp.transpose(query_heads, (1, 0, 2)).reshape(pair_heads * rows, DH)
     draft_k = jnp.concatenate([first[:, q_cols:q_cols + kv_cols], second[:, q_cols:q_cols + kv_cols]], 1)
     draft_v = jnp.concatenate([first[:, q_cols + kv_cols:], second[:, q_cols + kv_cols:]], 1)
-    top, total, acc = blocks_partial(
-        query_heads, blocks[:, 0], blocks[:, 1], draft_k, draft_v, cache_keep, draft_keep, score_scale
-    )
-    done = (acc / total[..., None]).reshape(2, heads_here, rows, DH)
+    tree_rows = jnp.tile(tree_keep, (pair_heads, 1))
+    done = attend(context_length, q_rows, blocks[:, 0], blocks[:, 1], draft_k, draft_v, tree_rows)
+    done = done.reshape(2, heads_here, rows, DH)
     keep = jnp.where(own == 0, done[0], done[1])
     got = lax.ppermute(jnp.where(own == 0, done[1], done[0]), "ctx", swap)
     keep = jnp.transpose(keep, (1, 0, 2)).reshape(rows, heads_here * DH)

time: 95.6 us -> 86.1 us (0.901)
  matrix products: 7.31 us -> 0 us
  other arithmetic: 11.6 us -> 4.33 us
  Pallas kernels: 0 us -> 5.75 us
  waiting for transfers between devices: 47.7 us -> 46.5 us
    reduce_sum x3 -> x0, other arithmetic: 6.56 us -> none  [the longest x2 5.68 us: blocks_partial(): total = jnp.sum(cache_weight, -1) + jnp.sum(draft_weight, -1)]
    pallas_call x0 -> x1, Pallas kernels: none -> 5.75 us  [attend(): pl.pallas_call(attend_kernel, out_shape=jax.ShapeDtypeStruct((rows, DH),...]
    dot_general x3 -> x0, matrix products: 5.71 us -> none  [the longest x1 3.3 us: blocks_partial(): jnp.einsum('hqjt,td->hqjd', draft_weight.astype(jnp.bfloat16), draft_v, p...]
    reduce_max x2 -> x0, other arithmetic: 2.05 us -> none  [the longest x1 1.14 us: blocks_partial(): top_score = jnp.maximum(jnp.max(scores, -1), jnp.max(draft_scores, -1))]
    unnamed x1 -> x0, matrix products: 1.6 us -> none
    concatenate x0 -> x2, other arithmetic: none -> 1.35 us  [the longest x1 0.68 us: body(): jnp.concatenate([first[:, q_cols:q_cols + kv_cols], second[:, q_cols:q_co...]
    squeeze x0 -> x1, local copies, waits for them, and re-layouts: none -> 1.09 us  [body(): blocks[:, 1]]
    reduce_sum x1 -> x0, local copies, waits for them, and re-layouts: 1.04 us -> none  [blocks_partial(): total = jnp.sum(cache_weight, -1) + jnp.sum(draft_weight, -1)]
  transfers between devices with their start and end apart: 3 -> 3, of which waited for: 2 -> 2; matrix products, arithmetic and copies ran while one was open for 4% -> 3% of each run, Pallas kernels for 0% -> 0%
where the time goes in v5:
time: 86.1 us; the launch traced here: 85.6 us
  waiting for transfers between devices  46.5 us (54%)
  starting transfers between devices  22.2 us (26%)
  local copies, waits for them, and re-layouts  5.89 us (7%)
  Pallas kernels  5.75 us (7%)
  other arithmetic  4.33 us (5%)
  between operations  0.88 us (1%)
    ppermute x1, waiting for transfers between devices, body(): lax.ppermute(lax.dynamic_index_in_dim(packed, 1 - own, 0, keepdims=False)...  43.1 us
    all_to_all x1, starting transfers between devices, body(): blocks = lax.all_to_all(kv, 'ctx', 0, 0, tiled=True)  15.3 us
    pallas_call x1, Pallas kernels, attend(): pl.pallas_call(attend_kernel, out_shape=jax.ShapeDtypeStruct((rows, DH),...  5.75 us
    ppermute x1, starting transfers between devices, body(): lax.ppermute(lax.dynamic_index_in_dim(packed, 1 - own, 0, keepdims=False)...  3.83 us
    ppermute x1, waiting for transfers between devices, body(): got = lax.ppermute(jnp.where(own == 0, done[1], done[0]), 'ctx', swap)  3.46 us
    ppermute x1, starting transfers between devices, body(): got = lax.ppermute(jnp.where(own == 0, done[1], done[0]), 'ctx', swap)  3.04 us
    unnamed x12, local copies, waits for them, and re-layouts  2.87 us
  transfers between devices with their start and end apart: 3, of which 2 were waited for; matrix products, arithmetic and copies ran while one was open for 3% of the time, Pallas kernels for 0%

profile of v5, /device:TPU:6, one launch (start us, length us, event | category | flops | bytes accessed | tf_op | source)
XLA Modules:
  0.0 85.6 jit_solution(3485271701923273981)
XLA Ops:
  0.0 1.1 %copy.22 = bf16[32,8,8,128]{3,2,1,0:T(8,128)(2,1)S(1)} copy(bf16[32,8,8,128]{3,1,2,0:T(8,128)(2,1)} %bitcast.39) | data formatting | bytes 1048576
  1.2 0.1 copy.14
  1.3 0.9 %copy-done = bf16[2,128,1024]{2,1,0:T(8,128)(2,1)S(1)} copy-done((bf16[2,128,1024]{2,1,0:T(8,128)(2,1)S(1)}, bf16[2,128,1024]{2,1,0:T(8,128)(2,1)}, u32[]{:S(2)}) %copy-start) | copy-done | bytes 524312
  2.2 0.1 copy.23
  2.3 0.1 copy.15
  2.4 1.1 %pad_maximum_fusion = bf16[2,2,128,8,128]{4,2,1,0,3:T(8,128)(2,1)} fusion(bf16[2,1,128,8,128]{4,2,1,0,3:T(8,128)(2,1)S(1)} %copy.15, bf16[2,1,128,8,128]{4,2,1,0,3:T(8,128)(2,1)S(1)} %copy.14), kind=kLoop, calls=%fused_computation | loop fusion | flops 524288 | bytes 2097152 | tf_op jit(solution)/shard_map/stack | solution.py:134
  3.5 15.3 %all-to-all-start = ((bf16[16,2,128,128]{3,2,1,0:T(8,128)(2,1)}), bf16[16,2,128,128]{3,2,1,0:T(8,128)(2,1)S(1)}, u32[]{:S(2)}, u32[]{:S(2)}) async-start(bf16[16,2,128,128]{3,2,1,0:T(8,128)(2,1)} %bitcast.5), calls=%async_computation | async-start | bytes 2097152 | tf_op jit(solution)/shard_map/all_to_all | solution.py:138
  18.8 0.7 copy-done.2
  19.5 0.1 pad_maximum_fusion.2
  19.6 3.8 %collective-permute-start = (bf16[48,640]{1,0:T(8,128)(2,1)S(1)}, bf16[48,640]{1,0:T(8,128)(2,1)S(1)}, u32[]{:S(2)}, u32[]{:S(2)}) collective-permute-start(bf16[48,640]{1,0:T(8,128)(2,1)S(1)} %dynamic-slice_bitcast_fusion), channel_id=1, source_target_pairs={{0,1},{1,0},{2,3},{3,2},{4,5},{5,4},{6,7},{7,6},{8,9},{9,8},{10,11... | collective-permute-start | bytes 184328 | tf_op jit(solution)/shard_map/ppermute | solution.py:130
  23.5 0.1 broadcast_multiply_fusion
  23.6 0.1 mul.23
  24.4 43.1 %collective-permute-done = bf16[48,640]{1,0:T(8,128)(2,1)S(1)} collective-permute-done((bf16[48,640]{1,0:T(8,128)(2,1)S(1)}, bf16[48,640]{1,0:T(8,128)(2,1)S(1)}, u32[]{:S(2)}, u32[]{:S(2)}) %collective-permute-start) | collective-permute-done | bytes 61472 | tf_op jit(solution)/shard_map/ppermute | solution.py:130
  67.6 0.7 copy.13
  68.3 0.1 fusion
  68.3 0.7 pad_maximum_fusion.3.dk_ref
  69.0 0.7 pad_maximum_fusion.4.dv_ref
  69.7 1.1 %slice_bitcast_fusion = (bf16[16,128,128]{2,1,0:T(8,128)(2,1)}, bf16[16,128,128]{2,1,0:T(8,128)(2,1)}) fusion(bf16[16,2,128,128]{3,2,1,0:T(8,128)(2,1)S(1)} %all-to-all-done), kind=kLoop, calls=%fused_computation.1 | loop fusion | bytes 2097152 | tf_op jit(solution)/shard_map/squeeze | solution.py:151
  70.8 0.7 tile.8
  71.5 5.8 %shard_map.73 = f32[384,128]{1,0:T(8,128)} custom-call(s32[1]{0:T(128)S(6)} %copy.24.len_ref, bf16[384,128]{1,0:T(8,128)(2,1)} %bitcast.41, bf16[16,128,128]{2,1,0:T(8,128)(2,1)} %get-tuple-element.6.k_ref, bf16[16,128,128]{2,1,0:T(8,128)(2,1)} %get-tuple-element.5.v_ref, bf16[48,128]{1,0:T(8,128)(2,1)} %pad_maximum_fusion.3.dk_ref, ...), custom_call_target="tpu_custom_call" | custom-call | tf_op jit(solution)/shard_map/pallas_call | solution.py:106
  77.2 1.0 %slice_select_fusion.1 = (f32[192,128]{1,0:T(8,128)S(1)}, f32[192,128]{1,0:T(8,128)S(1)}) fusion(f32[384,128]{1,0:T(8,128)} %shard_map.73, pred[]{:T(512)S(6)} %eq.17), kind=kLoop, calls=%fused_computation.9 | loop fusion | flops 49152 | bytes 393217 | tf_op jit(solution)/shard_map/jit(_where)/select_n | solution.py:153
  78.2 3.0 %collective-permute-start.1 = (f32[4,48,128]{2,1,0:T(8,128)S(1)}, f32[4,48,128]{2,1,0:T(8,128)S(1)}, u32[]{:S(2)}, u32[]{:S(2)}) collective-permute-start(f32[4,48,128]{2,1,0:T(8,128)S(1)} %bitcast.43), channel_id=1, source_target_pairs={{0,1},{1,0},{2,3},{3,2},{4,5},{5,4},{6,7},{7,6},{8,9},{9,8},{10,11... | collective-permute-start | bytes 294920 | tf_op jit(solution)/shard_map/ppermute | solution.py:154
  81.2 3.5 %collective-permute-done.1 = f32[4,48,128]{2,1,0:T(8,128)S(1)} collective-permute-done((f32[4,48,128]{2,1,0:T(8,128)S(1)}, f32[4,48,128]{2,1,0:T(8,128)S(1)}, u32[]{:S(2)}, u32[]{:S(2)}) %collective-permute-start.1) | collective-permute-done | bytes 98336 | tf_op jit(solution)/shard_map/ppermute | solution.py:154
  84.9 0.7 pad_maximum_fusion.1
  (22 shorter events, 0.3 us)
Async XLA Ops:
  1.1 1.0 %copy-start = (bf16[2,128,1024]{2,1,0:T(8,128)(2,1)S(1)}, bf16[2,128,1024]{2,1,0:T(8,128)(2,1)}, u32[]{:S(2)}) copy-start(bf16[2,128,1024]{2,1,0:T(8,128)(2,1)} %param.9) | copy-start | bytes 1572868
  3.5 15.4 %copy-start.1 = (bf16[2,48,512]{2,1,0:T(8,128)(2,1)S(1)}, bf16[2,48,512]{2,1,0:T(8,128)(2,1)}, u32[]{:S(2)}) copy-start(bf16[2,48,512]{2,1,0:T(8,128)(2,1)} %param.7) | copy-start | bytes 294916
  3.5 15.4 %copy-start.3 = (bf16[2,48,64]{2,1,0:T(8,128)(2,1)S(1)}, bf16[2,48,64]{2,1,0:T(8,128)(2,1)}, u32[]{:S(2)}) copy-start(bf16[2,48,64]{2,1,0:T(8,128)(2,1)} %param.10) | copy-start | bytes 36868
  3.5 66.2 %all-to-all-start = ((bf16[16,2,128,128]{3,2,1,0:T(8,128)(2,1)}), bf16[16,2,128,128]{3,2,1,0:T(8,128)(2,1)S(1)}, u32[]{:S(2)}, u32[]{:S(2)}) async-start(bf16[16,2,128,128]{3,2,1,0:T(8,128)(2,1)} %bitcast.5), calls=%async_computation | async-start | bytes 2097152 | tf_op jit(solution)/shard_map/all_to_all | solution.py:138
  18.8 0.7 copy-start.2
  19.6 3.9 %copy-start.4 = (s32[2,24,24]{2,1,0:T(8,128)S(1)}, s32[2,24,24]{2,1,0:T(8,128)}, u32[]{:S(2)}) copy-start(s32[2,24,24]{2,1,0:T(8,128)} %param.12) | copy-start | bytes 13828
  19.6 47.8 %collective-permute-start = (bf16[48,640]{1,0:T(8,128)(2,1)S(1)}, bf16[48,640]{1,0:T(8,128)(2,1)S(1)}, u32[]{:S(2)}, u32[]{:S(2)}) collective-permute-start(bf16[48,640]{1,0:T(8,128)(2,1)S(1)} %dynamic-slice_bitcast_fusion), channel_id=1, source_target_pairs={{0,1},{1,0},{2,3},{3,2},{4,5},{5,4},{6,7},{7,6},{8,9},{9,8},{10,11... | collective-permute-start | bytes 184328 | tf_op jit(solution)/shard_map/ppermute | solution.py:130
  78.2 6.5 %collective-permute-start.1 = (f32[4,48,128]{2,1,0:T(8,128)S(1)}, f32[4,48,128]{2,1,0:T(8,128)S(1)}, u32[]{:S(2)}, u32[]{:S(2)}) collective-permute-start(f32[4,48,128]{2,1,0:T(8,128)S(1)} %bitcast.43), channel_id=1, source_target_pairs={{0,1},{1,0},{2,3},{3,2},{4,5},{5,4},{6,7},{7,6},{8,9},{9,8},{10,11... | collective-permute-start | bytes 294920 | tf_op jit(solution)/shard_map/ppermute | solution.py:154

commit v6 on v5

--- a/solution.py
+++ b/solution.py
@@ -62,15 +62,15 @@
     return lax.dot_general(a, b, dims, preferred_element_type=jnp.float32)
 
 
-def attend_kernel(len_ref, q_ref, k_ref, v_ref, dk_ref, dv_ref, tree_ref, o_ref, out_sc, lse_sc):
-    blocks, block_len, _ = k_ref.shape
+def attend_kernel(len_ref, q_ref, kv_ref, dk_ref, dv_ref, tree_ref, o_ref, out_sc, lse_sc):
+    blocks, _, block_len, _ = kv_ref.shape
     score_scale = 1.0 / math.sqrt(DH)
     nt = (((1,), (1,)), ((), ()))
     nn = (((1,), (0,)), ((), ()))
     q = q_ref[...]
     ctx_len = len_ref[0]
     for j in range(blocks):
-        scores = _dot(q, k_ref[j], nt) * score_scale
+        scores = _dot(q, kv_ref[j, 0], nt) * score_scale
         pos = j * block_len + lax.broadcasted_iota(jnp.int32, scores.shape, 1)
         scores = jnp.where(pos < ctx_len, scores, masked_score)
         top = jnp.max(scores, axis=1, keepdims=True)
@@ -81,7 +81,7 @@
         shift = jnp.where(top > -1e29, top, 0.0)
         weight = jnp.exp(scores - shift)
         total = jnp.sum(weight, axis=1, keepdims=True)
-        acc = _dot(weight.astype(jnp.bfloat16), v_ref[j], nn)
+        acc = _dot(weight.astype(jnp.bfloat16), kv_ref[j, 1], nn)
         if j == 0:
             draft_weight = jnp.exp(draft - shift)
             total = total + jnp.sum(draft_weight, axis=1, keepdims=True)
@@ -99,17 +99,17 @@
     o_ref[...] = weighted / jnp.sum(factor, axis=1, keepdims=True)
 
 
-def attend(context_length, q_rows, block_keys, block_values, draft_k, draft_v, tree_rows):
+def attend(context_length, q_rows, blocks_kv, draft_k, draft_v, tree_rows):
     rows = q_rows.shape[0]
-    blocks = block_keys.shape[0]
+    blocks = blocks_kv.shape[0]
     vmem = pl.BlockSpec(memory_space=pltpu.VMEM)
     return pl.pallas_call(
         attend_kernel,
         out_shape=jax.ShapeDtypeStruct((rows, DH), jnp.float32),
-        in_specs=[pl.BlockSpec(memory_space=pltpu.SMEM)] + [vmem] * 6,
+        in_specs=[pl.BlockSpec(memory_space=pltpu.SMEM)] + [vmem] * 5,
         out_specs=vmem,
         scratch_shapes=[pltpu.VMEM((blocks, rows, DH), jnp.float32), pltpu.VMEM((rows, blocks), jnp.float32)],
-    )(context_length, q_rows, block_keys, block_values, draft_k, draft_v, tree_rows)
+    )(context_length, q_rows, blocks_kv, draft_k, draft_v, tree_rows)
 
 
 def body(queries, key_cache, value_cache, draft_keys, draft_values, ancestors, context_length):
@@ -140,18 +140,16 @@
     tree_keep = (
         jnp.eye(trees, dtype=jnp.int32)[:, None, :, None] * ancestors[:, :, None, :]
     ).reshape(rows, rows)
-    pair_heads = 2 * heads_here
-    query_heads = jnp.concatenate(
-        [first[:, :q_cols].reshape(rows, heads_here, DH), second[:, :q_cols].reshape(rows, heads_here, DH)], 1
-    )
-    q_rows = jnp.transpose(query_heads, (1, 0, 2)).reshape(pair_heads * rows, DH)
+    own_q = mine_now[:, :q_cols].reshape(rows, heads_here, DH)
+    other_q = partner[:, :q_cols].reshape(rows, heads_here, DH)
     draft_k = jnp.concatenate([first[:, q_cols:q_cols + kv_cols], second[:, q_cols:q_cols + kv_cols]], 1)
     draft_v = jnp.concatenate([first[:, q_cols + kv_cols:], second[:, q_cols + kv_cols:]], 1)
-    tree_rows = jnp.tile(tree_keep, (pair_heads, 1))
-    done = attend(context_length, q_rows, blocks[:, 0], blocks[:, 1], draft_k, draft_v, tree_rows)
-    done = done.reshape(2, heads_here, rows, DH)
-    keep = jnp.where(own == 0, done[0], done[1])
-    got = lax.ppermute(jnp.where(own == 0, done[1], done[0]), "ctx", swap)
+    tree_rows = jnp.tile(tree_keep, (heads_here, 1))
+    give = attend(context_length, jnp.transpose(other_q, (1, 0, 2)).reshape(heads_here * rows, DH),
+                  blocks, draft_k, draft_v, tree_rows)
+    got = lax.ppermute(give.reshape(heads_here, rows, DH), "ctx", swap)
+    keep = attend(context_length, jnp.transpose(own_q, (1, 0, 2)).reshape(heads_here * rows, DH),
+                  blocks, draft_k, draft_v, tree_rows).reshape(heads_here, rows, DH)
     keep = jnp.transpose(keep, (1, 0, 2)).reshape(rows, heads_here * DH)
     got = jnp.transpose(got, (1, 0, 2)).reshape(rows, heads_here * DH)
     return jnp.stack([jnp.where(own == 0, keep, got), jnp.where(own == 0, got, keep)])

time: 86.1 us -> 89.2 us (1.036)
  Pallas kernels: 5.75 us -> 12.4 us
  waiting for transfers between devices: 46.5 us -> 43.5 us
    pallas_call x1 -> x2, Pallas kernels: 5.75 us -> 12.4 us  [attend(): pl.pallas_call(attend_kernel, out_shape=jax.ShapeDtypeStruct((rows, DH),...]
    ppermute x1, waiting for transfers between devices: 3.46 us -> 0.01 us  [body(): got = lax.ppermute(give.reshape(heads_here, rows, DH), 'ctx', swap)]
    squeeze x1 -> x0, local copies, waits for them, and re-layouts: 1.09 us -> none  [body(): blocks[:, 1]]
    select_n x1, other arithmetic: 0.96 us -> 0.01 us  [body(): second = jnp.where(own == 0, partner, mine_now)]
    select_n x1, other arithmetic: 0.02 us -> 0.91 us  [body(): jnp.where(own == 0, keep, got)]
    unnamed x12 -> x14, local copies, waits for them, and re-layouts: 2.87 us -> 3.2 us
  transfers between devices with their start and end apart: 3 -> 3, of which waited for: 2 -> 2; matrix products, arithmetic and copies ran while one was open for 3% -> 3% of each run, Pallas kernels for 0% -> 7%
where the time goes in v6:
time: 89.2 us; the launch traced here: 88.6 us
  waiting for transfers between devices  43.5 us (49%)
  starting transfers between devices  22.5 us (25%)
  Pallas kernels  12.4 us (14%)
  local copies, waits for them, and re-layouts  5.8 us (7%)
  other arithmetic  3.56 us (4%)
    ppermute x1, waiting for transfers between devices, body(): lax.ppermute(lax.dynamic_index_in_dim(packed, 1 - own, 0, keepdims=False)...  43.1 us
    all_to_all x1, starting transfers between devices, body(): blocks = lax.all_to_all(kv, 'ctx', 0, 0, tiled=True)  15.3 us
    pallas_call x2, Pallas kernels, attend(): pl.pallas_call(attend_kernel, out_shape=jax.ShapeDtypeStruct((rows, DH),...  12.4 us
    ppermute x1, starting transfers between devices, body(): lax.ppermute(lax.dynamic_index_in_dim(packed, 1 - own, 0, keepdims=False)...  3.83 us
    ppermute x1, starting transfers between devices, body(): got = lax.ppermute(give.reshape(heads_here, rows, DH), 'ctx', swap)  3.34 us
    unnamed x14, local copies, waits for them, and re-layouts  3.2 us
  transfers between devices with their start and end apart: 3, of which 2 were waited for; matrix products, arithmetic and copies ran while one was open for 3% of the time, Pallas kernels for 7%

profile of v6, /device:TPU:6, one launch (start us, length us, event | category | flops | bytes accessed | tf_op | source)
XLA Modules:
  0.0 88.6 jit_solution(4847877391885892962)
XLA Ops:
  0.0 1.1 %copy.15 = bf16[32,8,8,128]{3,2,1,0:T(8,128)(2,1)S(1)} copy(bf16[32,8,8,128]{3,1,2,0:T(8,128)(2,1)} %bitcast.33) | data formatting | bytes 1048576
  1.2 0.1 copy.10
  1.3 0.9 %copy-done.1 = bf16[2,128,1024]{2,1,0:T(8,128)(2,1)S(1)} copy-done((bf16[2,128,1024]{2,1,0:T(8,128)(2,1)S(1)}, bf16[2,128,1024]{2,1,0:T(8,128)(2,1)}, u32[]{:S(2)}) %copy-start.1) | copy-done | bytes 524312
  2.2 0.1 copy.14
  2.3 0.1 copy.9
  2.4 1.1 %pad_maximum_fusion = bf16[2,2,128,8,128]{4,2,1,0,3:T(8,128)(2,1)} fusion(bf16[2,1,128,8,128]{4,2,1,0,3:T(8,128)(2,1)S(1)} %copy.10, bf16[2,1,128,8,128]{4,2,1,0,3:T(8,128)(2,1)S(1)} %copy.9), kind=kLoop, calls=%fused_computation | loop fusion | flops 524288 | bytes 2097152 | tf_op jit(solution)/shard_map/stack | solution.py:134
  3.5 15.3 %all-to-all-start = ((bf16[16,2,128,128]{3,2,1,0:T(8,128)(2,1)}), bf16[16,2,128,128]{3,2,1,0:T(8,128)(2,1)S(1)}, u32[]{:S(2)}, u32[]{:S(2)}) async-start(bf16[16,2,128,128]{3,2,1,0:T(8,128)(2,1)} %bitcast.4), calls=%async_computation | async-start | bytes 2097152 | tf_op jit(solution)/shard_map/all_to_all | solution.py:138
  18.9 0.7 copy-done.3
  19.5 0.1 pad_maximum_fusion.2
  19.7 3.8 %collective-permute-start = (bf16[48,640]{1,0:T(8,128)(2,1)S(1)}, bf16[48,640]{1,0:T(8,128)(2,1)S(1)}, u32[]{:S(2)}, u32[]{:S(2)}) collective-permute-start(bf16[48,640]{1,0:T(8,128)(2,1)S(1)} %dynamic-slice_bitcast_fusion), channel_id=1, source_target_pairs={{0,1},{1,0},{2,3},{3,2},{4,5},{5,4},{6,7},{7,6},{8,9},{9,8},{10,11... | collective-permute-start | bytes 184328 | tf_op jit(solution)/shard_map/ppermute | solution.py:130
  23.5 0.1 broadcast_multiply_fusion
  23.6 0.1 mul.23
  24.4 43.1 %collective-permute-done = bf16[48,640]{1,0:T(8,128)(2,1)S(1)} collective-permute-done((bf16[48,640]{1,0:T(8,128)(2,1)S(1)}, bf16[48,640]{1,0:T(8,128)(2,1)S(1)}, u32[]{:S(2)}, u32[]{:S(2)}) %collective-permute-start) | collective-permute-done | bytes 61472 | tf_op jit(solution)/shard_map/ppermute | solution.py:130
  67.5 0.6 copy.11
  68.3 0.7 pad_maximum_fusion.3
  69.0 0.4 all-to-all-done.kv_ref
  69.4 0.7 tile.8
  70.1 0.3 copy-done
  70.4 6.2 %shard_map.74 = f32[192,128]{1,0:T(8,128)} custom-call(s32[1]{0:T(128)S(6)} %copy.16.len_ref, bf16[192,128]{1,0:T(8,128)(2,1)} %bitcast.36, bf16[16,2,128,128]{3,2,1,0:T(8,128)(2,1)} %copy-done, bf16[48,128]{1,0:T(8,128)(2,1)} %get-tuple-element.13.dk_ref, bf16[48,128]{1,0:T(8,128)(2,1)} %get-tuple-element.14.dv_ref, s32[192,48]{1,0:T(8,128)} %bitcast.31), custom_call_target="tpu_custom_call" | custom-call | tf_op jit(solution)/shard_map/pallas_call | solution.py:106
  76.6 3.3 %collective-permute-start.1 = (f32[4,48,128]{2,1,0:T(8,128)}, f32[4,48,128]{2,1,0:T(8,128)S(1)}, u32[]{:S(2)}, u32[]{:S(2)}) collective-permute-start(f32[4,48,128]{2,1,0:T(8,128)} %bitcast.40), channel_id=1, source_target_pairs={{0,1},{1,0},{2,3},{3,2},{4,5},{5,4},{6,7},{7,6},{8,9},{9,8},{10,11... | collective-permute-start | bytes 294920 | tf_op jit(solution)/shard_map/ppermute | solution.py:150
  80.0 0.6 copy.8
  80.6 6.2 %shard_map.73 = f32[192,128]{1,0:T(8,128)} custom-call(s32[1]{0:T(128)S(6)} %copy.16.len_ref, bf16[192,128]{1,0:T(8,128)(2,1)} %bitcast.37, bf16[16,2,128,128]{3,2,1,0:T(8,128)(2,1)} %copy-done, bf16[48,128]{1,0:T(8,128)(2,1)} %get-tuple-element.13.dk_ref, bf16[48,128]{1,0:T(8,128)(2,1)} %get-tuple-element.14.dv_ref, s32[192,48]{1,0:T(8,128)} %bitcast.32), custom_call_target="tpu_custom_call" | custom-call | tf_op jit(solution)/shard_map/pallas_call | solution.py:106
  86.8 0.9 %select_bitcast_fusion.1 = (f32[48,4,128]{2,0,1:T(8,128)S(1)}, f32[48,4,128]{2,0,1:T(8,128)S(1)}) fusion(f32[4,48,128]{2,1,0:T(8,128)} %bitcast.35, f32[4,48,128]{2,1,0:T(8,128)S(1)} %collective-permute-done.1, pred[]{:T(512)S(6)} %eq.15), kind=kLoop, calls=%fused_computation.4 | loop fusion | flops 49152 | bytes 393217 | tf_op jit(solution)/shard_map/jit(_where)/select_n | solution.py:155
  87.9 0.7 pad_maximum_fusion.1
  (24 shorter events, 0.4 us)
Async XLA Ops:
  1.1 1.0 %copy-start.1 = (bf16[2,128,1024]{2,1,0:T(8,128)(2,1)S(1)}, bf16[2,128,1024]{2,1,0:T(8,128)(2,1)}, u32[]{:S(2)}) copy-start(bf16[2,128,1024]{2,1,0:T(8,128)(2,1)} %param.8) | copy-start | bytes 1572868
  3.5 15.4 %copy-start.2 = (bf16[2,48,512]{2,1,0:T(8,128)(2,1)S(1)}, bf16[2,48,512]{2,1,0:T(8,128)(2,1)}, u32[]{:S(2)}) copy-start(bf16[2,48,512]{2,1,0:T(8,128)(2,1)} %param.7) | copy-start | bytes 294916
  3.5 15.4 %copy-start.4 = (bf16[2,48,64]{2,1,0:T(8,128)(2,1)S(1)}, bf16[2,48,64]{2,1,0:T(8,128)(2,1)}, u32[]{:S(2)}) copy-start(bf16[2,48,64]{2,1,0:T(8,128)(2,1)} %param.10) | copy-start | bytes 36868
  3.5 65.9 %all-to-all-start = ((bf16[16,2,128,128]{3,2,1,0:T(8,128)(2,1)}), bf16[16,2,128,128]{3,2,1,0:T(8,128)(2,1)S(1)}, u32[]{:S(2)}, u32[]{:S(2)}) async-start(bf16[16,2,128,128]{3,2,1,0:T(8,128)(2,1)} %bitcast.4), calls=%async_computation | async-start | bytes 2097152 | tf_op jit(solution)/shard_map/all_to_all | solution.py:138
  18.8 0.7 copy-start.3
  19.6 3.9 %copy-start.5 = (s32[2,24,24]{2,1,0:T(8,128)S(1)}, s32[2,24,24]{2,1,0:T(8,128)}, u32[]{:S(2)}) copy-start(s32[2,24,24]{2,1,0:T(8,128)} %param.12) | copy-start | bytes 13828
  19.7 47.8 %collective-permute-start = (bf16[48,640]{1,0:T(8,128)(2,1)S(1)}, bf16[48,640]{1,0:T(8,128)(2,1)S(1)}, u32[]{:S(2)}, u32[]{:S(2)}) collective-permute-start(bf16[48,640]{1,0:T(8,128)(2,1)S(1)} %dynamic-slice_bitcast_fusion), channel_id=1, source_target_pairs={{0,1},{1,0},{2,3},{3,2},{4,5},{5,4},{6,7},{7,6},{8,9},{9,8},{10,11... | collective-permute-start | bytes 184328 | tf_op jit(solution)/shard_map/ppermute | solution.py:130
  69.4 1.0 %copy-start = (bf16[16,2,128,128]{3,2,1,0:T(8,128)(2,1)}, bf16[16,2,128,128]{3,2,1,0:T(8,128)(2,1)S(1)}, u32[]{:S(2)}) copy-start(bf16[16,2,128,128]{3,2,1,0:T(8,128)(2,1)S(1)} %all-to-all-done.kv_ref) | copy-start | bytes 3145732
  76.6 10.2 %collective-permute-start.1 = (f32[4,48,128]{2,1,0:T(8,128)}, f32[4,48,128]{2,1,0:T(8,128)S(1)}, u32[]{:S(2)}, u32[]{:S(2)}) collective-permute-start(f32[4,48,128]{2,1,0:T(8,128)} %bitcast.40), channel_id=1, source_target_pairs={{0,1},{1,0},{2,3},{3,2},{4,5},{5,4},{6,7},{7,6},{8,9},{9,8},{10,11... | collective-permute-start | bytes 294920 | tf_op jit(solution)/shard_map/ppermute | solution.py:150

commit v7 on v5

--- a/solution.py
+++ b/solution.py
@@ -62,54 +62,54 @@
     return lax.dot_general(a, b, dims, preferred_element_type=jnp.float32)
 
 
-def attend_kernel(len_ref, q_ref, k_ref, v_ref, dk_ref, dv_ref, tree_ref, o_ref, out_sc, lse_sc):
-    blocks, block_len, _ = k_ref.shape
+def attend_kernel(len_ref, q_ref, kv_ref, dk_ref, dvt_ref, tree_ref, o_ref, out_sc, lse_sc):
+    blocks, _, block_len, _ = kv_ref.shape
     score_scale = 1.0 / math.sqrt(DH)
     nt = (((1,), (1,)), ((), ()))
     nn = (((1,), (0,)), ((), ()))
     q = q_ref[...]
     ctx_len = len_ref[0]
     for j in range(blocks):
-        scores = _dot(q, k_ref[j], nt) * score_scale
-        pos = j * block_len + lax.broadcasted_iota(jnp.int32, scores.shape, 1)
+        scores = _dot(kv_ref[j, 0], q, nt) * score_scale
+        pos = j * block_len + lax.broadcasted_iota(jnp.int32, scores.shape, 0)
         scores = jnp.where(pos < ctx_len, scores, masked_score)
-        top = jnp.max(scores, axis=1, keepdims=True)
+        top = jnp.max(scores, axis=0, keepdims=True)
         if j == 0:
-            draft = _dot(q, dk_ref[...], nt) * score_scale
+            draft = _dot(dk_ref[...], q, nt) * score_scale
             draft = jnp.where(tree_ref[...] > 0, draft, masked_score)
-            top = jnp.maximum(top, jnp.max(draft, axis=1, keepdims=True))
+            top = jnp.maximum(top, jnp.max(draft, axis=0, keepdims=True))
         shift = jnp.where(top > -1e29, top, 0.0)
         weight = jnp.exp(scores - shift)
-        total = jnp.sum(weight, axis=1, keepdims=True)
-        acc = _dot(weight.astype(jnp.bfloat16), v_ref[j], nn)
+        total = jnp.sum(weight, axis=0, keepdims=True)
+        acc = _dot(kv_ref[j, 1], weight.astype(jnp.bfloat16), nn)
         if j == 0:
             draft_weight = jnp.exp(draft - shift)
-            total = total + jnp.sum(draft_weight, axis=1, keepdims=True)
-            acc = acc + _dot(draft_weight.astype(jnp.bfloat16), dv_ref[...], nn)
+            total = total + jnp.sum(draft_weight, axis=0, keepdims=True)
+            acc = acc + _dot(dvt_ref[...], draft_weight.astype(jnp.bfloat16), nn)
         alive = total > 0.0
         safe = jnp.where(alive, total, 1.0)
         out_sc[j] = jnp.where(alive, acc / safe, 0.0).astype(jnp.bfloat16).astype(jnp.float32)
-        lse_sc[:, j:j + 1] = jnp.where(alive, top + jnp.log(safe), masked_score)
+        lse_sc[j:j + 1, :] = jnp.where(alive, top + jnp.log(safe), masked_score)
     lse = lse_sc[...]
-    overall = jnp.max(lse, axis=1, keepdims=True)
+    overall = jnp.max(lse, axis=0, keepdims=True)
     factor = jnp.exp(lse - overall)
-    weighted = factor[:, 0:1] * out_sc[0]
+    weighted = factor[0:1] * out_sc[0]
     for j in range(1, blocks):
-        weighted = weighted + factor[:, j:j + 1] * out_sc[j]
-    o_ref[...] = weighted / jnp.sum(factor, axis=1, keepdims=True)
+        weighted = weighted + factor[j:j + 1] * out_sc[j]
+    o_ref[...] = weighted / jnp.sum(factor, axis=0, keepdims=True)
 
 
-def attend(context_length, q_rows, block_keys, block_values, draft_k, draft_v, tree_rows):
+def attend(context_length, q_rows, blocks_kv, draft_k, draft_vt, tree_cols):
     rows = q_rows.shape[0]
-    blocks = block_keys.shape[0]
+    blocks = blocks_kv.shape[0]
     vmem = pl.BlockSpec(memory_space=pltpu.VMEM)
     return pl.pallas_call(
         attend_kernel,
-        out_shape=jax.ShapeDtypeStruct((rows, DH), jnp.float32),
-        in_specs=[pl.BlockSpec(memory_space=pltpu.SMEM)] + [vmem] * 6,
+        out_shape=jax.ShapeDtypeStruct((DH, rows), jnp.float32),
+        in_specs=[pl.BlockSpec(memory_space=pltpu.SMEM)] + [vmem] * 5,
         out_specs=vmem,
-        scratch_shapes=[pltpu.VMEM((blocks, rows, DH), jnp.float32), pltpu.VMEM((rows, blocks), jnp.float32)],
-    )(context_length, q_rows, block_keys, block_values, draft_k, draft_v, tree_rows)
+        scratch_shapes=[pltpu.VMEM((blocks, DH, rows), jnp.float32), pltpu.VMEM((blocks, rows), jnp.float32)],
+    )(context_length, q_rows, blocks_kv, draft_k, draft_vt, tree_cols)
 
 
 def body(queries, key_cache, value_cache, draft_keys, draft_values, ancestors, context_length):
@@ -131,10 +131,9 @@
     first = jnp.where(own == 0, mine_now, partner)
     second = jnp.where(own == 0, partner, mine_now)
 
-    kv = jnp.stack(
-        [key_cache.reshape(layers, local_len, KVH, DH), value_cache.reshape(layers, local_len, KVH, DH)], 1
-    )
-    kv = jnp.transpose(kv, (3, 0, 1, 2, 4)).reshape(n, 2, local_len, DH)
+    keys_out = jnp.transpose(key_cache.reshape(layers, local_len, KVH, DH), (2, 0, 1, 3))
+    values_out = jnp.transpose(value_cache.reshape(layers, local_len, KVH, DH), (2, 0, 3, 1))
+    kv = jnp.stack([keys_out, values_out], 2).reshape(n, 2, local_len, DH)
     blocks = lax.all_to_all(kv, "ctx", 0, 0, tiled=True)
 
     tree_keep = (
@@ -147,9 +146,9 @@
     q_rows = jnp.transpose(query_heads, (1, 0, 2)).reshape(pair_heads * rows, DH)
     draft_k = jnp.concatenate([first[:, q_cols:q_cols + kv_cols], second[:, q_cols:q_cols + kv_cols]], 1)
     draft_v = jnp.concatenate([first[:, q_cols + kv_cols:], second[:, q_cols + kv_cols:]], 1)
-    tree_rows = jnp.tile(tree_keep, (pair_heads, 1))
-    done = attend(context_length, q_rows, blocks[:, 0], blocks[:, 1], draft_k, draft_v, tree_rows)
-    done = done.reshape(2, heads_here, rows, DH)
+    tree_cols = jnp.tile(jnp.transpose(tree_keep), (1, pair_heads))
+    done = attend(context_length, q_rows, blocks, draft_k, jnp.transpose(draft_v), tree_cols)
+    done = jnp.transpose(done.reshape(DH, 2, heads_here, rows), (1, 2, 3, 0))
     keep = jnp.where(own == 0, done[0], done[1])
     got = lax.ppermute(jnp.where(own == 0, done[1], done[0]), "ctx", swap)
     keep = jnp.transpose(keep, (1, 0, 2)).reshape(rows, heads_here * DH)

time: 86.1 us -> 85.2 us (0.990)
  other arithmetic: 4.33 us -> 2.8 us
  local copies, waits for them, and re-layouts: 5.89 us -> 7.05 us
    squeeze x1 -> x0, local copies, waits for them, and re-layouts: 1.09 us -> none  [body(): blocks[:, 1]]
    pallas_call x0 -> x1, local copies, waits for them, and re-layouts: none -> 1.05 us  [attend(): pl.pallas_call(attend_kernel, out_shape=jax.ShapeDtypeStruct((DH, rows),...]
    select_n x1, other arithmetic: 0.96 us -> 0.01 us  [body(): got = lax.ppermute(jnp.where(own == 0, done[1], done[0]), 'ctx', swap)]
    unnamed x12 -> x14, local copies, waits for them, and re-layouts: 2.87 us -> 2.96 us
  transfers between devices with their start and end apart: 3 -> 3, of which waited for: 2 -> 2; matrix products, arithmetic and copies ran while one was open for 3% -> 4% of each run, Pallas kernels for 0% -> 0%
where the time goes in v7:
time: 85.2 us; the launch traced here: 84.7 us
  waiting for transfers between devices  45.8 us (54%)
  starting transfers between devices  22.1 us (26%)
  local copies, waits for them, and re-layouts  7.05 us (8%)
  Pallas kernels  6.1 us (7%)
  other arithmetic  2.8 us (3%)
  between operations  0.87 us (1%)
    ppermute x1, waiting for transfers between devices, body(): lax.ppermute(lax.dynamic_index_in_dim(packed, 1 - own, 0, keepdims=False)...  42.2 us
    all_to_all x1, starting transfers between devices, body(): blocks = lax.all_to_all(kv, 'ctx', 0, 0, tiled=True)  15.3 us
    pallas_call x1, Pallas kernels, attend(): pl.pallas_call(attend_kernel, out_shape=jax.ShapeDtypeStruct((DH, rows),...  6.1 us
    ppermute x1, starting transfers between devices, body(): lax.ppermute(lax.dynamic_index_in_dim(packed, 1 - own, 0, keepdims=False)...  3.83 us
    ppermute x1, waiting for transfers between devices, body(): got = lax.ppermute(jnp.where(own == 0, done[1], done[0]), 'ctx', swap)  3.57 us
    unnamed x14, local copies, waits for them, and re-layouts  2.96 us
    ppermute x1, starting transfers between devices, body(): got = lax.ppermute(jnp.where(own == 0, done[1], done[0]), 'ctx', swap)  2.93 us
  transfers between devices with their start and end apart: 3, of which 2 were waited for; matrix products, arithmetic and copies ran while one was open for 4% of the time, Pallas kernels for 0%

profile of v7, /device:TPU:6, one launch (start us, length us, event | category | flops | bytes accessed | tf_op | source)
XLA Modules:
  0.0 84.7 jit_solution(12350157060036566655)
XLA Ops:
  0.0 1.2 %copy.48 = bf16[32,8,8,128]{3,2,1,0:T(8,128)(2,1)S(1)} copy(bf16[32,8,8,128]{3,1,2,0:T(8,128)(2,1)} %bitcast.48) | data formatting | bytes 1048576
  1.2 0.4 copy.41
  1.6 0.1 copy_bitcast_fusion
  1.7 1.1 %pad_maximum_fusion = bf16[16,2,128,128]{3,2,1,0:T(8,128)(2,1)} fusion(bf16[16,1,128,128]{3,2,1,0:T(8,128)(2,1)S(1)} %bitcast.44, bf16[16,1,128,128]{3,2,1,0:T(8,128)(2,1)S(1)} %bitcast.45), kind=kLoop, calls=%fused_computation | loop fusion | flops 524288 | bytes 2097152 | tf_op jit(solution)/shard_map/stack | solution.py:136
  2.8 15.3 %all-to-all-start = ((bf16[16,2,128,128]{3,2,1,0:T(8,128)(2,1)}), bf16[16,2,128,128]{3,2,1,0:T(8,128)(2,1)S(1)}, u32[]{:S(2)}, u32[]{:S(2)}) async-start(bf16[16,2,128,128]{3,2,1,0:T(8,128)(2,1)} %pad_maximum_fusion), calls=%async_computation | async-start | bytes 2097152 | tf_op jit(solution)/shard_map/all_to_all | solution.py:137
  18.2 0.7 copy-done.3
  18.9 0.1 pad_maximum_fusion.2
  19.0 3.8 %collective-permute-start = (bf16[48,640]{1,0:T(8,128)(2,1)S(1)}, bf16[48,640]{1,0:T(8,128)(2,1)S(1)}, u32[]{:S(2)}, u32[]{:S(2)}) collective-permute-start(bf16[48,640]{1,0:T(8,128)(2,1)S(1)} %dynamic-slice_bitcast_fusion), channel_id=1, source_target_pairs={{0,1},{1,0},{2,3},{3,2},{4,5},{5,4},{6,7},{7,6},{8,9},{9,8},{10,11... | collective-permute-start | bytes 184328 | tf_op jit(solution)/shard_map/ppermute | solution.py:130
  22.9 0.1 copy.43
  22.9 0.1 broadcast_multiply_fusion
  23.0 0.1 mul.20
  23.2 0.7 tile.10.tree_ref
  24.6 42.2 %collective-permute-done = bf16[48,640]{1,0:T(8,128)(2,1)S(1)} collective-permute-done((bf16[48,640]{1,0:T(8,128)(2,1)S(1)}, bf16[48,640]{1,0:T(8,128)(2,1)S(1)}, u32[]{:S(2)}, u32[]{:S(2)}) %collective-permute-start) | collective-permute-done | bytes 61472 | tf_op jit(solution)/shard_map/ppermute | solution.py:130
  66.8 0.1 fusion.2
  66.9 0.1 pad_maximum_fusion.4
  67.0 0.7 copy.42
  67.8 0.6 copy.39
  68.5 0.7 pad_maximum_fusion.3.dk_ref
  69.2 1.0 %copy-done.1 = bf16[16,2,128,128]{3,2,1,0:T(8,128)(2,1)} copy-done((bf16[16,2,128,128]{3,2,1,0:T(8,128)(2,1)}, bf16[16,2,128,128]{3,2,1,0:T(8,128)(2,1)S(1)}, u32[]{:S(2)}) %copy-start.1) | copy-done | bytes 1048600
  70.1 6.1 %shard_map.73 = f32[128,384]{1,0:T(8,128)} custom-call(s32[1]{0:T(128)S(6)} %copy.50.len_ref, bf16[384,128]{1,0:T(8,128)(2,1)} %bitcast.49, bf16[16,2,128,128]{3,2,1,0:T(8,128)(2,1)} %copy-done.1, bf16[48,128]{1,0:T(8,128)(2,1)} %pad_maximum_fusion.3.dk_ref, bf16[128,48]{1,0:T(8,128)(2,1)} %bitcast.50, s32[48,384]{1,0:T(8,128)} %tile.10.tree_ref), custom_call_target="tpu_custom_call" | custom-call | tf_op jit(solution)/shard_map/pallas_call | solution.py:106
  76.2 1.1 %copy.44 = f32[128,384]{0,1:T(8,128)S(1)} copy(f32[128,384]{1,0:T(8,128)} %shard_map.73) | data formatting | bytes 393216 | tf_op jit(solution)/shard_map/pallas_call | solution.py:106
  77.3 2.9 %collective-permute-start.1 = (f32[4,48,128]{2,1,0:T(8,128)S(1)}, f32[4,48,128]{2,1,0:T(8,128)S(1)}, u32[]{:S(2)}, u32[]{:S(2)}) collective-permute-start(f32[4,48,128]{2,1,0:T(8,128)S(1)} %select_bitcast_fusion), channel_id=1, source_target_pairs={{0,1},{1,0},{2,3},{3,2},{4,5},{5,4},{6,7},{7,6},{8,9},{9,8},{10,11... | collective-permute-start | bytes 294920 | tf_op jit(solution)/shard_map/ppermute | solution.py:153
  80.2 3.6 %collective-permute-done.1 = f32[4,48,128]{2,1,0:T(8,128)S(1)} collective-permute-done((f32[4,48,128]{2,1,0:T(8,128)S(1)}, f32[4,48,128]{2,1,0:T(8,128)S(1)}, u32[]{:S(2)}, u32[]{:S(2)}) %collective-permute-start.1) | collective-permute-done | bytes 98336 | tf_op jit(solution)/shard_map/ppermute | solution.py:153
  84.0 0.7 pad_maximum_fusion.1
  (26 shorter events, 0.4 us)
Async XLA Ops:
  0.0 1.6 %copy-start = (bf16[2,128,1024]{2,1,0:T(8,128)(2,1)S(1)}, bf16[2,128,1024]{2,1,0:T(8,128)(2,1)}, u32[]{:S(2)}) copy-start(bf16[2,128,1024]{2,1,0:T(8,128)(2,1)} %param.8) | copy-start | bytes 1572868
  2.8 15.4 %copy-start.2 = (bf16[2,48,512]{2,1,0:T(8,128)(2,1)S(1)}, bf16[2,48,512]{2,1,0:T(8,128)(2,1)}, u32[]{:S(2)}) copy-start(bf16[2,48,512]{2,1,0:T(8,128)(2,1)} %param.7) | copy-start | bytes 294916
  2.8 15.4 %copy-start.4 = (bf16[2,48,64]{2,1,0:T(8,128)(2,1)S(1)}, bf16[2,48,64]{2,1,0:T(8,128)(2,1)}, u32[]{:S(2)}) copy-start(bf16[2,48,64]{2,1,0:T(8,128)(2,1)} %param.10) | copy-start | bytes 36868
  2.8 66.3 %all-to-all-start = ((bf16[16,2,128,128]{3,2,1,0:T(8,128)(2,1)}), bf16[16,2,128,128]{3,2,1,0:T(8,128)(2,1)S(1)}, u32[]{:S(2)}, u32[]{:S(2)}) async-start(bf16[16,2,128,128]{3,2,1,0:T(8,128)(2,1)} %pad_maximum_fusion), calls=%async_computation | async-start | bytes 2097152 | tf_op jit(solution)/shard_map/all_to_all | solution.py:137
  18.2 0.7 copy-start.3
  19.0 3.9 %copy-start.5 = (s32[2,24,24]{2,1,0:T(8,128)S(1)}, s32[2,24,24]{2,1,0:T(8,128)}, u32[]{:S(2)}) copy-start(s32[2,24,24]{2,1,0:T(8,128)} %param.12) | copy-start | bytes 13828
  19.0 47.8 %collective-permute-start = (bf16[48,640]{1,0:T(8,128)(2,1)S(1)}, bf16[48,640]{1,0:T(8,128)(2,1)S(1)}, u32[]{:S(2)}, u32[]{:S(2)}) collective-permute-start(bf16[48,640]{1,0:T(8,128)(2,1)S(1)} %dynamic-slice_bitcast_fusion), channel_id=1, source_target_pairs={{0,1},{1,0},{2,3},{3,2},{4,5},{5,4},{6,7},{7,6},{8,9},{9,8},{10,11... | collective-permute-start | bytes 184328 | tf_op jit(solution)/shard_map/ppermute | solution.py:130
  69.2 1.0 %copy-start.1 = (bf16[16,2,128,128]{3,2,1,0:T(8,128)(2,1)}, bf16[16,2,128,128]{3,2,1,0:T(8,128)(2,1)S(1)}, u32[]{:S(2)}) copy-start(bf16[16,2,128,128]{3,2,1,0:T(8,128)(2,1)S(1)} %all-to-all-done.kv_ref) | copy-start | bytes 3145732
  77.3 6.5 %collective-permute-start.1 = (f32[4,48,128]{2,1,0:T(8,128)S(1)}, f32[4,48,128]{2,1,0:T(8,128)S(1)}, u32[]{:S(2)}, u32[]{:S(2)}) collective-permute-start(f32[4,48,128]{2,1,0:T(8,128)S(1)} %select_bitcast_fusion), channel_id=1, source_target_pairs={{0,1},{1,0},{2,3},{3,2},{4,5},{5,4},{6,7},{7,6},{8,9},{9,8},{10,11... | collective-permute-start | bytes 294920 | tf_op jit(solution)/shard_map/ppermute | solution.py:153

commit v8 on v7

--- a/solution.py
+++ b/solution.py
@@ -69,10 +69,12 @@
     nn = (((1,), (0,)), ((), ()))
     q = q_ref[...]
     ctx_len = len_ref[0]
+    all_keys = kv_ref[:, 0].reshape(blocks * block_len, DH)
+    all_scores = _dot(all_keys, q, nt) * score_scale
+    pos = lax.broadcasted_iota(jnp.int32, all_scores.shape, 0)
+    all_scores = jnp.where(pos < ctx_len, all_scores, masked_score)
     for j in range(blocks):
-        scores = _dot(kv_ref[j, 0], q, nt) * score_scale
-        pos = j * block_len + lax.broadcasted_iota(jnp.int32, scores.shape, 0)
-        scores = jnp.where(pos < ctx_len, scores, masked_score)
+        scores = all_scores[j * block_len:(j + 1) * block_len]
         top = jnp.max(scores, axis=0, keepdims=True)
         if j == 0:
             draft = _dot(dk_ref[...], q, nt) * score_scale

time: 85.2 us -> 83 us (0.974)
  Pallas kernels: 6.1 us -> 3.92 us
    pallas_call x1, Pallas kernels: 6.1 us -> 3.92 us  [attend(): pl.pallas_call(attend_kernel, out_shape=jax.ShapeDtypeStruct((DH, rows),...]
where the time goes in v8:
time: 83 us; the launch traced here: 82.5 us
  waiting for transfers between devices  45.8 us (55%)
  starting transfers between devices  22.1 us (27%)
  local copies, waits for them, and re-layouts  7.05 us (8%)
  Pallas kernels  3.92 us (5%)
  other arithmetic  2.8 us (3%)
  between operations  0.87 us (1%)
    ppermute x1, waiting for transfers between devices, body(): lax.ppermute(lax.dynamic_index_in_dim(packed, 1 - own, 0, keepdims=False)...  42.2 us
    all_to_all x1, starting transfers between devices, body(): blocks = lax.all_to_all(kv, 'ctx', 0, 0, tiled=True)  15.3 us
    pallas_call x1, Pallas kernels, attend(): pl.pallas_call(attend_kernel, out_shape=jax.ShapeDtypeStruct((DH, rows),...  3.92 us
    ppermute x1, starting transfers between devices, body(): lax.ppermute(lax.dynamic_index_in_dim(packed, 1 - own, 0, keepdims=False)...  3.83 us
    ppermute x1, waiting for transfers between devices, body(): got = lax.ppermute(jnp.where(own == 0, done[1], done[0]), 'ctx', swap)  3.57 us
    unnamed x14, local copies, waits for them, and re-layouts  2.96 us
    ppermute x1, starting transfers between devices, body(): got = lax.ppermute(jnp.where(own == 0, done[1], done[0]), 'ctx', swap)  2.93 us
  transfers between devices with their start and end apart: 3, of which 2 were waited for; matrix products, arithmetic and copies ran while one was open for 4% of the time, Pallas kernels for 0%

profile of v8, /device:TPU:6, one launch (start us, length us, event | category | flops | bytes accessed | tf_op | source)
XLA Modules:
  0.0 82.5 jit_solution(10880255996503104880)
XLA Ops:
  0.0 1.2 %copy.48 = bf16[32,8,8,128]{3,2,1,0:T(8,128)(2,1)S(1)} copy(bf16[32,8,8,128]{3,1,2,0:T(8,128)(2,1)} %bitcast.48) | data formatting | bytes 1048576
  1.2 0.4 copy.41
  1.6 0.1 copy_bitcast_fusion
  1.7 1.1 %pad_maximum_fusion = bf16[16,2,128,128]{3,2,1,0:T(8,128)(2,1)} fusion(bf16[16,1,128,128]{3,2,1,0:T(8,128)(2,1)S(1)} %bitcast.44, bf16[16,1,128,128]{3,2,1,0:T(8,128)(2,1)S(1)} %bitcast.45), kind=kLoop, calls=%fused_computation | loop fusion | flops 524288 | bytes 2097152 | tf_op jit(solution)/shard_map/stack | solution.py:138
  2.8 15.3 %all-to-all-start = ((bf16[16,2,128,128]{3,2,1,0:T(8,128)(2,1)}), bf16[16,2,128,128]{3,2,1,0:T(8,128)(2,1)S(1)}, u32[]{:S(2)}, u32[]{:S(2)}) async-start(bf16[16,2,128,128]{3,2,1,0:T(8,128)(2,1)} %pad_maximum_fusion), calls=%async_computation | async-start | bytes 2097152 | tf_op jit(solution)/shard_map/all_to_all | solution.py:139
  18.2 0.7 copy-done.3
  18.9 0.1 pad_maximum_fusion.2
  19.0 3.8 %collective-permute-start = (bf16[48,640]{1,0:T(8,128)(2,1)S(1)}, bf16[48,640]{1,0:T(8,128)(2,1)S(1)}, u32[]{:S(2)}, u32[]{:S(2)}) collective-permute-start(bf16[48,640]{1,0:T(8,128)(2,1)S(1)} %dynamic-slice_bitcast_fusion), channel_id=1, source_target_pairs={{0,1},{1,0},{2,3},{3,2},{4,5},{5,4},{6,7},{7,6},{8,9},{9,8},{10,11... | collective-permute-start | bytes 184328 | tf_op jit(solution)/shard_map/ppermute | solution.py:132
  22.9 0.1 copy.43
  22.9 0.1 broadcast_multiply_fusion
  23.0 0.1 mul.20
  23.2 0.7 tile.10.tree_ref
  24.6 42.2 %collective-permute-done = bf16[48,640]{1,0:T(8,128)(2,1)S(1)} collective-permute-done((bf16[48,640]{1,0:T(8,128)(2,1)S(1)}, bf16[48,640]{1,0:T(8,128)(2,1)S(1)}, u32[]{:S(2)}, u32[]{:S(2)}) %collective-permute-start) | collective-permute-done | bytes 61472 | tf_op jit(solution)/shard_map/ppermute | solution.py:132
  66.8 0.1 fusion.2
  66.9 0.1 pad_maximum_fusion.4
  67.0 0.7 copy.42
  67.8 0.6 copy.39
  68.5 0.7 pad_maximum_fusion.3.dk_ref
  69.2 1.0 %copy-done.1 = bf16[16,2,128,128]{3,2,1,0:T(8,128)(2,1)} copy-done((bf16[16,2,128,128]{3,2,1,0:T(8,128)(2,1)}, bf16[16,2,128,128]{3,2,1,0:T(8,128)(2,1)S(1)}, u32[]{:S(2)}) %copy-start.1) | copy-done | bytes 1048600
  70.1 3.9 %shard_map.73 = f32[128,384]{1,0:T(8,128)} custom-call(s32[1]{0:T(128)S(6)} %copy.50.len_ref, bf16[384,128]{1,0:T(8,128)(2,1)} %bitcast.49, bf16[16,2,128,128]{3,2,1,0:T(8,128)(2,1)} %copy-done.1, bf16[48,128]{1,0:T(8,128)(2,1)} %pad_maximum_fusion.3.dk_ref, bf16[128,48]{1,0:T(8,128)(2,1)} %bitcast.50, s32[48,384]{1,0:T(8,128)} %tile.10.tree_ref), custom_call_target="tpu_custom_call" | custom-call | tf_op jit(solution)/shard_map/pallas_call | solution.py:108
  74.0 1.1 %copy.44 = f32[128,384]{0,1:T(8,128)S(1)} copy(f32[128,384]{1,0:T(8,128)} %shard_map.73) | data formatting | bytes 393216 | tf_op jit(solution)/shard_map/pallas_call | solution.py:108
  75.1 2.9 %collective-permute-start.1 = (f32[4,48,128]{2,1,0:T(8,128)S(1)}, f32[4,48,128]{2,1,0:T(8,128)S(1)}, u32[]{:S(2)}, u32[]{:S(2)}) collective-permute-start(f32[4,48,128]{2,1,0:T(8,128)S(1)} %select_bitcast_fusion), channel_id=1, source_target_pairs={{0,1},{1,0},{2,3},{3,2},{4,5},{5,4},{6,7},{7,6},{8,9},{9,8},{10,11... | collective-permute-start | bytes 294920 | tf_op jit(solution)/shard_map/ppermute | solution.py:155
  78.1 3.6 %collective-permute-done.1 = f32[4,48,128]{2,1,0:T(8,128)S(1)} collective-permute-done((f32[4,48,128]{2,1,0:T(8,128)S(1)}, f32[4,48,128]{2,1,0:T(8,128)S(1)}, u32[]{:S(2)}, u32[]{:S(2)}) %collective-permute-start.1) | collective-permute-done | bytes 98336 | tf_op jit(solution)/shard_map/ppermute | solution.py:155
  81.9 0.7 pad_maximum_fusion.1
  (26 shorter events, 0.4 us)
Async XLA Ops:
  0.0 1.6 %copy-start = (bf16[2,128,1024]{2,1,0:T(8,128)(2,1)S(1)}, bf16[2,128,1024]{2,1,0:T(8,128)(2,1)}, u32[]{:S(2)}) copy-start(bf16[2,128,1024]{2,1,0:T(8,128)(2,1)} %param.8) | copy-start | bytes 1572868
  2.8 15.4 %copy-start.2 = (bf16[2,48,512]{2,1,0:T(8,128)(2,1)S(1)}, bf16[2,48,512]{2,1,0:T(8,128)(2,1)}, u32[]{:S(2)}) copy-start(bf16[2,48,512]{2,1,0:T(8,128)(2,1)} %param.7) | copy-start | bytes 294916
  2.8 15.4 %copy-start.4 = (bf16[2,48,64]{2,1,0:T(8,128)(2,1)S(1)}, bf16[2,48,64]{2,1,0:T(8,128)(2,1)}, u32[]{:S(2)}) copy-start(bf16[2,48,64]{2,1,0:T(8,128)(2,1)} %param.10) | copy-start | bytes 36868
  2.8 66.3 %all-to-all-start = ((bf16[16,2,128,128]{3,2,1,0:T(8,128)(2,1)}), bf16[16,2,128,128]{3,2,1,0:T(8,128)(2,1)S(1)}, u32[]{:S(2)}, u32[]{:S(2)}) async-start(bf16[16,2,128,128]{3,2,1,0:T(8,128)(2,1)} %pad_maximum_fusion), calls=%async_computation | async-start | bytes 2097152 | tf_op jit(solution)/shard_map/all_to_all | solution.py:139
  18.2 0.7 copy-start.3
  19.0 3.9 %copy-start.5 = (s32[2,24,24]{2,1,0:T(8,128)S(1)}, s32[2,24,24]{2,1,0:T(8,128)}, u32[]{:S(2)}) copy-start(s32[2,24,24]{2,1,0:T(8,128)} %param.12) | copy-start | bytes 13828
  19.0 47.8 %collective-permute-start = (bf16[48,640]{1,0:T(8,128)(2,1)S(1)}, bf16[48,640]{1,0:T(8,128)(2,1)S(1)}, u32[]{:S(2)}, u32[]{:S(2)}) collective-permute-start(bf16[48,640]{1,0:T(8,128)(2,1)S(1)} %dynamic-slice_bitcast_fusion), channel_id=1, source_target_pairs={{0,1},{1,0},{2,3},{3,2},{4,5},{5,4},{6,7},{7,6},{8,9},{9,8},{10,11... | collective-permute-start | bytes 184328 | tf_op jit(solution)/shard_map/ppermute | solution.py:132
  69.2 1.0 %copy-start.1 = (bf16[16,2,128,128]{3,2,1,0:T(8,128)(2,1)}, bf16[16,2,128,128]{3,2,1,0:T(8,128)(2,1)S(1)}, u32[]{:S(2)}) copy-start(bf16[16,2,128,128]{3,2,1,0:T(8,128)(2,1)S(1)} %all-to-all-done.kv_ref) | copy-start | bytes 3145732
  75.1 6.5 %collective-permute-start.1 = (f32[4,48,128]{2,1,0:T(8,128)S(1)}, f32[4,48,128]{2,1,0:T(8,128)S(1)}, u32[]{:S(2)}, u32[]{:S(2)}) collective-permute-start(f32[4,48,128]{2,1,0:T(8,128)S(1)} %select_bitcast_fusion), channel_id=1, source_target_pairs={{0,1},{1,0},{2,3},{3,2},{4,5},{5,4},{6,7},{7,6},{8,9},{9,8},{10,11... | collective-permute-start | bytes 294920 | tf_op jit(solution)/shard_map/ppermute | solution.py:155

commit v9 on v8

--- a/solution.py
+++ b/solution.py
@@ -141,18 +141,16 @@
     tree_keep = (
         jnp.eye(trees, dtype=jnp.int32)[:, None, :, None] * ancestors[:, :, None, :]
     ).reshape(rows, rows)
-    pair_heads = 2 * heads_here
-    query_heads = jnp.concatenate(
-        [first[:, :q_cols].reshape(rows, heads_here, DH), second[:, :q_cols].reshape(rows, heads_here, DH)], 1
-    )
-    q_rows = jnp.transpose(query_heads, (1, 0, 2)).reshape(pair_heads * rows, DH)
+    own_q = jnp.transpose(mine_now[:, :q_cols].reshape(rows, heads_here, DH), (1, 0, 2))
+    other_q = jnp.transpose(partner[:, :q_cols].reshape(rows, heads_here, DH), (1, 0, 2))
     draft_k = jnp.concatenate([first[:, q_cols:q_cols + kv_cols], second[:, q_cols:q_cols + kv_cols]], 1)
-    draft_v = jnp.concatenate([first[:, q_cols + kv_cols:], second[:, q_cols + kv_cols:]], 1)
-    tree_cols = jnp.tile(jnp.transpose(tree_keep), (1, pair_heads))
-    done = attend(context_length, q_rows, blocks, draft_k, jnp.transpose(draft_v), tree_cols)
-    done = jnp.transpose(done.reshape(DH, 2, heads_here, rows), (1, 2, 3, 0))
-    keep = jnp.where(own == 0, done[0], done[1])
-    got = lax.ppermute(jnp.where(own == 0, done[1], done[0]), "ctx", swap)
+    draft_vt = jnp.transpose(jnp.concatenate([first[:, q_cols + kv_cols:], second[:, q_cols + kv_cols:]], 1))
+    tree_cols = jnp.tile(jnp.transpose(tree_keep), (1, heads_here))
+    give = attend(context_length, other_q.reshape(heads_here * rows, DH), blocks, draft_k, draft_vt, tree_cols)
+    got = lax.ppermute(give, "ctx", swap)
+    keep = attend(context_length, own_q.reshape(heads_here * rows, DH), blocks, draft_k, draft_vt, tree_cols)
+    keep = jnp.transpose(keep.reshape(DH, heads_here, rows), (1, 2, 0))
+    got = jnp.transpose(got.reshape(DH, heads_here, rows), (1, 2, 0))
     keep = jnp.transpose(keep, (1, 0, 2)).reshape(rows, heads_here * DH)
     got = jnp.transpose(got, (1, 0, 2)).reshape(rows, heads_here * DH)
     return jnp.stack([jnp.where(own == 0, keep, got), jnp.where(own == 0, got, keep)])

time: 83 us -> 82.9 us (level)
  waiting for transfers between devices: 45.8 us -> 42.3 us
  Pallas kernels: 3.92 us -> 6.73 us
  other arithmetic: 2.8 us -> 3.64 us
    ppermute x1, waiting for transfers between devices: 3.57 us -> 0.02 us  [body(): got = lax.ppermute(give, 'ctx', swap)]
    pallas_call x1 -> x2, Pallas kernels: 3.92 us -> 6.73 us  [attend(): pl.pallas_call(attend_kernel, out_shape=jax.ShapeDtypeStruct((DH, rows),...]
    reshape x2, local copies, waits for them, and re-layouts: 0.04 us -> 1.25 us  [the longest x1 0.63 us: body(): partner[:, :q_cols].reshape(rows, heads_here, DH)]
    pallas_call x1 -> x0, local copies, waits for them, and re-layouts: 1.05 us -> none  [attend(): pl.pallas_call(attend_kernel, out_shape=jax.ShapeDtypeStruct((DH, rows),...]
    select_n x1, other arithmetic: 0.02 us -> 0.92 us  [body(): jnp.where(own == 0, keep, got)]
  transfers between devices with their start and end apart: 3 -> 3, of which waited for: 2 -> 1; matrix products, arithmetic and copies ran while one was open for 4% -> 5% of each run, Pallas kernels for 0% -> 4%
where the time goes in v9:
time: 82.9 us; the launch traced here: 82.4 us
  waiting for transfers between devices  42.3 us (51%)
  starting transfers between devices  22.2 us (27%)
  local copies, waits for them, and re-layouts  6.73 us (8%)
  Pallas kernels  6.73 us (8%)
  other arithmetic  3.64 us (4%)
  between operations  0.86 us (1%)
    ppermute x1, waiting for transfers between devices, body(): lax.ppermute(lax.dynamic_index_in_dim(packed, 1 - own, 0, keepdims=False)...  42.3 us
    all_to_all x1, starting transfers between devices, body(): blocks = lax.all_to_all(kv, 'ctx', 0, 0, tiled=True)  15.3 us
    pallas_call x2, Pallas kernels, attend(): pl.pallas_call(attend_kernel, out_shape=jax.ShapeDtypeStruct((DH, rows),...  6.73 us
    ppermute x1, starting transfers between devices, body(): lax.ppermute(lax.dynamic_index_in_dim(packed, 1 - own, 0, keepdims=False)...  3.83 us
    ppermute x1, starting transfers between devices, body(): got = lax.ppermute(give, 'ctx', swap)  3.04 us
    unnamed x14, local copies, waits for them, and re-layouts  2.96 us
  transfers between devices with their start and end apart: 3, of which 1 were waited for; matrix products, arithmetic and copies ran while one was open for 5% of the time, Pallas kernels for 4%

profile of v9, /device:TPU:6, one launch (start us, length us, event | category | flops | bytes accessed | tf_op | source)
XLA Modules:
  0.0 82.4 jit_solution(3914083859103870504)
XLA Ops:
  0.0 1.2 %copy.56 = bf16[32,8,8,128]{3,2,1,0:T(8,128)(2,1)S(1)} copy(bf16[32,8,8,128]{3,1,2,0:T(8,128)(2,1)} %bitcast.49) | data formatting | bytes 1048576
  1.2 0.4 copy.45
  1.6 0.1 copy_bitcast_fusion
  1.7 1.1 %pad_maximum_fusion = bf16[16,2,128,128]{3,2,1,0:T(8,128)(2,1)} fusion(bf16[16,1,128,128]{3,2,1,0:T(8,128)(2,1)S(1)} %bitcast.47, bf16[16,1,128,128]{3,2,1,0:T(8,128)(2,1)S(1)} %bitcast.48), kind=kLoop, calls=%fused_computation | loop fusion | flops 524288 | bytes 2097152 | tf_op jit(solution)/shard_map/stack | solution.py:138
  2.8 15.3 %all-to-all-start = ((bf16[16,2,128,128]{3,2,1,0:T(8,128)(2,1)}), bf16[16,2,128,128]{3,2,1,0:T(8,128)(2,1)S(1)}, u32[]{:S(2)}, u32[]{:S(2)}) async-start(bf16[16,2,128,128]{3,2,1,0:T(8,128)(2,1)} %pad_maximum_fusion), calls=%async_computation | async-start | bytes 2097152 | tf_op jit(solution)/shard_map/all_to_all | solution.py:139
  18.2 0.7 copy-done.3
  18.9 0.1 pad_maximum_fusion.2
  19.0 3.8 %collective-permute-start = (bf16[48,640]{1,0:T(8,128)(2,1)S(1)}, bf16[48,640]{1,0:T(8,128)(2,1)S(1)}, u32[]{:S(2)}, u32[]{:S(2)}) collective-permute-start(bf16[48,640]{1,0:T(8,128)(2,1)S(1)} %dynamic-slice_bitcast_fusion), channel_id=1, source_target_pairs={{0,1},{1,0},{2,3},{3,2},{4,5},{5,4},{6,7},{7,6},{8,9},{9,8},{10,11... | collective-permute-start | bytes 184328 | tf_op jit(solution)/shard_map/ppermute | solution.py:132
  22.9 0.1 broadcast_multiply_fusion
  23.0 0.1 mul.20
  23.2 0.7 tile.10.tree_ref
  24.5 42.3 %collective-permute-done = bf16[48,640]{1,0:T(8,128)(2,1)S(1)} collective-permute-done((bf16[48,640]{1,0:T(8,128)(2,1)S(1)}, bf16[48,640]{1,0:T(8,128)(2,1)S(1)}, u32[]{:S(2)}, u32[]{:S(2)}) %collective-permute-start) | collective-permute-done | bytes 61472 | tf_op jit(solution)/shard_map/ppermute | solution.py:132
  67.0 0.7 copy.46
  67.7 0.7 pad_maximum_fusion.3.dk_ref
  68.4 0.6 copy_bitcast_fusion.1
  69.0 1.0 %copy-done.1 = bf16[16,2,128,128]{3,2,1,0:T(8,128)(2,1)} copy-done((bf16[16,2,128,128]{3,2,1,0:T(8,128)(2,1)}, bf16[16,2,128,128]{3,2,1,0:T(8,128)(2,1)S(1)}, u32[]{:S(2)}) %copy-start.1) | copy-done | bytes 1048600
  70.0 3.4 %shard_map.74 = f32[128,192]{1,0:T(8,128)} custom-call(s32[1]{0:T(128)S(6)} %copy.60.len_ref, bf16[192,128]{1,0:T(8,128)(2,1)} %bitcast.54, bf16[16,2,128,128]{3,2,1,0:T(8,128)(2,1)} %copy-done.1, bf16[48,128]{1,0:T(8,128)(2,1)} %pad_maximum_fusion.3.dk_ref, bf16[128,48]{1,0:T(8,128)(2,1)} %bitcast.52, s32[48,192]{1,0:T(8,128)} %tile.10.tree_ref), custom_call_target="tpu_custom_call" | custom-call | tf_op jit(solution)/shard_map/pallas_call | solution.py:108
  73.4 3.0 %collective-permute-start.1 = (f32[128,192]{1,0:T(8,128)}, f32[128,192]{1,0:T(8,128)S(1)}, u32[]{:S(2)}, u32[]{:S(2)}) collective-permute-start(f32[128,192]{1,0:T(8,128)} %shard_map.74), channel_id=1, source_target_pairs={{0,1},{1,0},{2,3},{3,2},{4,5},{5,4},{6,7},{7,6},{8,9},{9,8},{10,11... | collective-permute-start | bytes 294920 | tf_op jit(solution)/shard_map/ppermute | solution.py:150
  76.4 0.6 copy_bitcast_fusion.2
  77.0 3.4 %shard_map.73 = f32[128,192]{1,0:T(8,128)} custom-call(s32[1]{0:T(128)S(6)} %copy.60.len_ref, bf16[192,128]{1,0:T(8,128)(2,1)} %bitcast.55, bf16[16,2,128,128]{3,2,1,0:T(8,128)(2,1)} %copy-done.1, bf16[48,128]{1,0:T(8,128)(2,1)} %pad_maximum_fusion.3.dk_ref, bf16[128,48]{1,0:T(8,128)(2,1)} %bitcast.53, s32[48,192]{1,0:T(8,128)} %tile.10.tree_ref), custom_call_target="tpu_custom_call" | custom-call | tf_op jit(solution)/shard_map/pallas_call | solution.py:108
  80.4 0.9 %broadcast_select_fusion.1 = (f32[128,192]{1,0:T(8,128)S(1)}, f32[128,192]{1,0:T(8,128)S(1)}) fusion(f32[128,192]{1,0:T(8,128)} %shard_map.73, f32[128,192]{1,0:T(8,128)S(1)} %collective-permute-done.1, pred[]{:T(512)S(6)} %eq.15), kind=kLoop, calls=%fused_computation.5 | loop fusion | flops 49152 | bytes 393217 | tf_op jit(solution)/shard_map/jit(_where)/select_n | solution.py:156
  81.4 0.1 copy.49
  81.6 0.1 copy.51
  81.8 0.7 pad_maximum_fusion.1
  (24 shorter events, 0.5 us)
Async XLA Ops:
  0.0 1.6 %copy-start = (bf16[2,128,1024]{2,1,0:T(8,128)(2,1)S(1)}, bf16[2,128,1024]{2,1,0:T(8,128)(2,1)}, u32[]{:S(2)}) copy-start(bf16[2,128,1024]{2,1,0:T(8,128)(2,1)} %param.8) | copy-start | bytes 1572868
  2.8 15.4 %copy-start.2 = (bf16[2,48,512]{2,1,0:T(8,128)(2,1)S(1)}, bf16[2,48,512]{2,1,0:T(8,128)(2,1)}, u32[]{:S(2)}) copy-start(bf16[2,48,512]{2,1,0:T(8,128)(2,1)} %param.7) | copy-start | bytes 294916
  2.8 15.4 %copy-start.4 = (bf16[2,48,64]{2,1,0:T(8,128)(2,1)S(1)}, bf16[2,48,64]{2,1,0:T(8,128)(2,1)}, u32[]{:S(2)}) copy-start(bf16[2,48,64]{2,1,0:T(8,128)(2,1)} %param.10) | copy-start | bytes 36868
  2.8 66.2 %all-to-all-start = ((bf16[16,2,128,128]{3,2,1,0:T(8,128)(2,1)}), bf16[16,2,128,128]{3,2,1,0:T(8,128)(2,1)S(1)}, u32[]{:S(2)}, u32[]{:S(2)}) async-start(bf16[16,2,128,128]{3,2,1,0:T(8,128)(2,1)} %pad_maximum_fusion), calls=%async_computation | async-start | bytes 2097152 | tf_op jit(solution)/shard_map/all_to_all | solution.py:139
  18.2 0.7 copy-start.3
  19.0 3.9 %copy-start.5 = (s32[2,24,24]{2,1,0:T(8,128)S(1)}, s32[2,24,24]{2,1,0:T(8,128)}, u32[]{:S(2)}) copy-start(s32[2,24,24]{2,1,0:T(8,128)} %param.12) | copy-start | bytes 13828
  19.0 47.8 %collective-permute-start = (bf16[48,640]{1,0:T(8,128)(2,1)S(1)}, bf16[48,640]{1,0:T(8,128)(2,1)S(1)}, u32[]{:S(2)}, u32[]{:S(2)}) collective-permute-start(bf16[48,640]{1,0:T(8,128)(2,1)S(1)} %dynamic-slice_bitcast_fusion), channel_id=1, source_target_pairs={{0,1},{1,0},{2,3},{3,2},{4,5},{5,4},{6,7},{7,6},{8,9},{9,8},{10,11... | collective-permute-start | bytes 184328 | tf_op jit(solution)/shard_map/ppermute | solution.py:132
  69.0 1.0 %copy-start.1 = (bf16[16,2,128,128]{3,2,1,0:T(8,128)(2,1)}, bf16[16,2,128,128]{3,2,1,0:T(8,128)(2,1)S(1)}, u32[]{:S(2)}) copy-start(bf16[16,2,128,128]{3,2,1,0:T(8,128)(2,1)S(1)} %all-to-all-done.kv_ref) | copy-start | bytes 3145732
  73.4 7.1 %collective-permute-start.1 = (f32[128,192]{1,0:T(8,128)}, f32[128,192]{1,0:T(8,128)S(1)}, u32[]{:S(2)}, u32[]{:S(2)}) collective-permute-start(f32[128,192]{1,0:T(8,128)} %shard_map.74), channel_id=1, source_target_pairs={{0,1},{1,0},{2,3},{3,2},{4,5},{5,4},{6,7},{7,6},{8,9},{9,8},{10,11... | collective-permute-start | bytes 294920 | tf_op jit(solution)/shard_map/ppermute | solution.py:150

commit v10 on v9

--- a/solution.py
+++ b/solution.py
@@ -66,7 +66,7 @@
     blocks, _, block_len, _ = kv_ref.shape
     score_scale = 1.0 / math.sqrt(DH)
     nt = (((1,), (1,)), ((), ()))
-    nn = (((1,), (0,)), ((), ()))
+    tn = (((0,), (0,)), ((), ()))
     q = q_ref[...]
     ctx_len = len_ref[0]
     all_keys = kv_ref[:, 0].reshape(blocks * block_len, DH)
@@ -83,11 +83,11 @@
         shift = jnp.where(top > -1e29, top, 0.0)
         weight = jnp.exp(scores - shift)
         total = jnp.sum(weight, axis=0, keepdims=True)
-        acc = _dot(kv_ref[j, 1], weight.astype(jnp.bfloat16), nn)
+        acc = _dot(kv_ref[j, 1], weight.astype(jnp.bfloat16), tn)
         if j == 0:
             draft_weight = jnp.exp(draft - shift)
             total = total + jnp.sum(draft_weight, axis=0, keepdims=True)
-            acc = acc + _dot(dvt_ref[...], draft_weight.astype(jnp.bfloat16), nn)
+            acc = acc + _dot(dvt_ref[...], draft_weight.astype(jnp.bfloat16), tn)
         alive = total > 0.0
         safe = jnp.where(alive, total, 1.0)
         out_sc[j] = jnp.where(alive, acc / safe, 0.0).astype(jnp.bfloat16).astype(jnp.float32)
@@ -127,34 +127,36 @@
     own = d % layers
     swap = [(s, s ^ 1) for s in range(n)]
 
-    packed = jnp.concatenate([queries, draft_keys, draft_values], axis=2)
-    mine_now = lax.dynamic_index_in_dim(packed, own, 0, keepdims=False)
-    partner = lax.ppermute(lax.dynamic_index_in_dim(packed, 1 - own, 0, keepdims=False), "ctx", swap)
-    first = jnp.where(own == 0, mine_now, partner)
-    second = jnp.where(own == 0, partner, mine_now)
+    other = 1 - own
+    swapped = [
+        lax.ppermute(lax.dynamic_index_in_dim(a, other, 0, keepdims=False), "ctx", swap)
+        for a in (queries, draft_keys, draft_values)
+    ]
+    mine_now = [lax.dynamic_index_in_dim(a, own, 0, keepdims=False) for a in (queries, draft_keys, draft_values)]
+    first = [jnp.where(own == 0, a, b) for a, b in zip(mine_now, swapped)]
+    second = [jnp.where(own == 0, b, a) for a, b in zip(mine_now, swapped)]
 
     keys_out = jnp.transpose(key_cache.reshape(layers, local_len, KVH, DH), (2, 0, 1, 3))
-    values_out = jnp.transpose(value_cache.reshape(layers, local_len, KVH, DH), (2, 0, 3, 1))
+    values_out = jnp.transpose(value_cache.reshape(layers, local_len, KVH, DH), (2, 0, 1, 3))
     kv = jnp.stack([keys_out, values_out], 2).reshape(n, 2, local_len, DH)
     blocks = lax.all_to_all(kv, "ctx", 0, 0, tiled=True)
 
     tree_keep = (
         jnp.eye(trees, dtype=jnp.int32)[:, None, :, None] * ancestors[:, :, None, :]
     ).reshape(rows, rows)
-    own_q = jnp.transpose(mine_now[:, :q_cols].reshape(rows, heads_here, DH), (1, 0, 2))
-    other_q = jnp.transpose(partner[:, :q_cols].reshape(rows, heads_here, DH), (1, 0, 2))
-    draft_k = jnp.concatenate([first[:, q_cols:q_cols + kv_cols], second[:, q_cols:q_cols + kv_cols]], 1)
-    draft_vt = jnp.transpose(jnp.concatenate([first[:, q_cols + kv_cols:], second[:, q_cols + kv_cols:]], 1))
+    own_q = jnp.transpose(mine_now[0].reshape(rows, heads_here, DH), (1, 0, 2))
+    other_q = jnp.transpose(swapped[0].reshape(rows, heads_here, DH), (1, 0, 2))
+    draft_k = jnp.concatenate([first[1], second[1]], 1)
+    draft_vt = jnp.concatenate([first[2], second[2]], 1)
     tree_cols = jnp.tile(jnp.transpose(tree_keep), (1, heads_here))
     give = attend(context_length, other_q.reshape(heads_here * rows, DH), blocks, draft_k, draft_vt, tree_cols)
     got = lax.ppermute(give, "ctx", swap)
     keep = attend(context_length, own_q.reshape(heads_here * rows, DH), blocks, draft_k, draft_vt, tree_cols)
-    keep = jnp.transpose(keep.reshape(DH, heads_here, rows), (1, 2, 0))
-    got = jnp.transpose(got.reshape(DH, heads_here, rows), (1, 2, 0))
-    keep = jnp.transpose(keep, (1, 0, 2)).reshape(rows, heads_here * DH)
-    got = jnp.transpose(got, (1, 0, 2)).reshape(rows, heads_here * DH)
-    return jnp.stack([jnp.where(own == 0, keep, got), jnp.where(own == 0, got, keep)])
-
+    keep = jnp.transpose(keep.reshape(DH, heads_here, rows), (2, 1, 0)).reshape(1, rows, heads_here * DH)
+    got = jnp.transpose(got.reshape(DH, heads_here, rows), (2, 1, 0)).reshape(1, rows, heads_here * DH)
+    result = jnp.zeros((layers, rows, heads_here * DH), jnp.float32)
+    result = lax.dynamic_update_slice(result, keep, (own, 0, 0))
+    return lax.dynamic_update_slice(result, got, (other, 0, 0))
 
 def solution(mesh):
     placed = (

time: 82.9 us -> 82.4 us (level)
  starting transfers between devices: 22.2 us -> 28.3 us
  waiting for transfers between devices: 42.3 us -> 36.4 us
  other arithmetic: 3.64 us -> 1.87 us
  local copies, waits for them, and re-layouts: 6.73 us -> 7.71 us
    ppermute x1 -> x3, waiting for transfers between devices: 42.3 us -> 35.5 us  [body(): lax.ppermute(lax.dynamic_index_in_dim(a, other, 0, keepdims=False), 'ctx'...]
    ppermute x1 -> x3, starting transfers between devices: 3.83 us -> 9.66 us  [body(): lax.ppermute(lax.dynamic_index_in_dim(a, other, 0, keepdims=False), 'ctx'...]
    transpose x0 -> x4, local copies, waits for them, and re-layouts: none -> 1.34 us  [the longest x1 0.63 us: body(): other_q = jnp.transpose(swapped[0].reshape(rows, heads_here, DH), (1, 0, 2))]
    reshape x2 -> x4, local copies, waits for them, and re-layouts: 1.25 us -> 0.12 us  [the longest x1 0.04 us: body(): jnp.transpose(keep.reshape(DH, heads_here, rows), (2, 1, 0))]
    pallas_call x0 -> x1, local copies, waits for them, and re-layouts: none -> 1 us  [attend(): pl.pallas_call(attend_kernel, out_shape=jax.ShapeDtypeStruct((DH, rows),...]
    select_n x3 -> x2, other arithmetic: 0.95 us -> 0.01 us  [body(): first = [jnp.where(own == 0, a, b) for a, b in zip(mine_now, swapped)]]
    all_to_all x1, waiting for transfers between devices: 0.01 us -> 0.85 us  [body(): blocks = lax.all_to_all(kv, 'ctx', 0, 0, tiled=True)]
    unnamed x14 -> x17, local copies, waits for them, and re-layouts: 2.96 us -> 3.37 us
  transfers between devices with their start and end apart: 3 -> 5, of which waited for: 1 -> 3; matrix products, arithmetic and copies ran while one was open for 5% -> 5% of each run, Pallas kernels for 4% -> 4%
where the time goes in v10:
time: 82.4 us; the launch traced here: 81.9 us
  waiting for transfers between devices  36.4 us (44%)
  starting transfers between devices  28.3 us (34%)
  local copies, waits for them, and re-layouts  7.71 us (9%)
  Pallas kernels  6.74 us (8%)
  other arithmetic  1.87 us (2%)
  between operations  0.9 us (1%)
    ppermute x3, waiting for transfers between devices, body(): lax.ppermute(lax.dynamic_index_in_dim(a, other, 0, keepdims=False), 'ctx'...  35.5 us
    all_to_all x1, starting transfers between devices, body(): blocks = lax.all_to_all(kv, 'ctx', 0, 0, tiled=True)  15.3 us
    ppermute x3, starting transfers between devices, body(): lax.ppermute(lax.dynamic_index_in_dim(a, other, 0, keepdims=False), 'ctx'...  9.66 us
    pallas_call x2, Pallas kernels, attend(): pl.pallas_call(attend_kernel, out_shape=jax.ShapeDtypeStruct((DH, rows),...  6.74 us
    unnamed x17, local copies, waits for them, and re-layouts  3.37 us
    ppermute x1, starting transfers between devices, body(): got = lax.ppermute(give, 'ctx', swap)  3.34 us
  transfers between devices with their start and end apart: 5, of which 3 were waited for; matrix products, arithmetic and copies ran while one was open for 5% of the time, Pallas kernels for 4%

profile of v10, /device:TPU:6, one launch (start us, length us, event | category | flops | bytes accessed | tf_op | source)
XLA Modules:
  0.0 81.9 jit_solution(2369277300114048183)
XLA Ops:
  0.0 1.0 %copy-done = bf16[2,128,1024]{2,1,0:T(8,128)(2,1)S(1)} copy-done((bf16[2,128,1024]{2,1,0:T(8,128)(2,1)S(1)}, bf16[2,128,1024]{2,1,0:T(8,128)(2,1)}, u32[]{:S(2)}) %copy-start) | copy-done | bytes 524312
  1.0 0.1 copy_bitcast_fusion.1
  1.2 0.1 copy_bitcast_fusion
  1.3 1.1 %pad_maximum_fusion = bf16[16,2,128,128]{3,2,1,0:T(8,128)(2,1)} fusion(bf16[16,1,128,128]{3,2,1,0:T(8,128)(2,1)S(1)} %bitcast.42, bf16[16,1,128,128]{3,2,1,0:T(8,128)(2,1)S(1)} %bitcast.41), kind=kLoop, calls=%fused_computation | loop fusion | flops 524288 | bytes 2097152 | tf_op jit(solution)/shard_map/stack | solution.py:141
  2.4 15.3 %all-to-all-start = ((bf16[16,2,128,128]{3,2,1,0:T(8,128)(2,1)}), bf16[16,2,128,128]{3,2,1,0:T(8,128)(2,1)S(1)}, u32[]{:S(2)}, u32[]{:S(2)}) async-start(bf16[16,2,128,128]{3,2,1,0:T(8,128)(2,1)} %pad_maximum_fusion), calls=%async_computation | async-start | bytes 2097152 | tf_op jit(solution)/shard_map/all_to_all | solution.py:142
  17.8 0.7 copy-done.6
  18.5 3.8 %collective-permute-start = (bf16[48,64]{1,0:T(8,128)(2,1)S(1)}, bf16[48,64]{1,0:T(8,128)(2,1)S(1)}, u32[]{:S(2)}, u32[]{:S(2)}) collective-permute-start(bf16[48,64]{1,0:T(8,128)(2,1)S(1)} %dynamic-slice_bitcast_fusion.2), channel_id=1, source_target_pairs={{0,1},{1,0},{2,3},{3,2},{4,5},{5,4},{6,7},{7,6},{8,9},{9,8},{10,11... | collective-permute-start | bytes 18440 | tf_op jit(solution)/shard_map/ppermute | solution.py:132
  22.4 2.0 %collective-permute-start.1 = (bf16[48,64]{1,0:T(8,128)(2,1)S(1)}, bf16[48,64]{1,0:T(8,128)(2,1)S(1)}, u32[]{:S(2)}, u32[]{:S(2)}) collective-permute-start(bf16[48,64]{1,0:T(8,128)(2,1)S(1)} %dynamic-slice_bitcast_fusion.1), channel_id=1, source_target_pairs={{0,1},{1,0},{2,3},{3,2},{4,5},{5,4},{6,7},{7,6},{8,9},{9,8},{10,11... | collective-permute-start | bytes 18440 | tf_op jit(solution)/shard_map/ppermute | solution.py:132
  24.4 3.8 %collective-permute-start.2 = (bf16[48,512]{1,0:T(8,128)(2,1)S(1)}, bf16[48,512]{1,0:T(8,128)(2,1)S(1)}, u32[]{:S(2)}, u32[]{:S(2)}) collective-permute-start(bf16[48,512]{1,0:T(8,128)(2,1)S(1)} %get-tuple-element.5), channel_id=1, source_target_pairs={{0,1},{1,0},{2,3},{3,2},{4,5},{5,4},{6,7},{7,6},{8,9},{9,8},{10,11... | collective-permute-start | bytes 147464 | tf_op jit(solution)/shard_map/ppermute | solution.py:132
  28.5 0.1 mul.20
  28.6 0.7 tile.10.tree_ref
  30.0 0.6 copy.20
  30.6 35.4 %collective-permute-done = bf16[48,64]{1,0:T(8,128)(2,1)S(1)} collective-permute-done((bf16[48,64]{1,0:T(8,128)(2,1)S(1)}, bf16[48,64]{1,0:T(8,128)(2,1)S(1)}, u32[]{:S(2)}, u32[]{:S(2)}) %collective-permute-start) | collective-permute-done | bytes 6176 | tf_op jit(solution)/shard_map/ppermute | solution.py:132
  66.0 0.2 collective-permute-done.1
  66.1 0.7 pad_maximum_fusion.1
  66.9 0.6 copy.26
  67.5 0.9 %all-to-all-done.kv_ref = bf16[16,2,128,128]{3,2,1,0:T(8,128)(2,1)S(1)} async-done(((bf16[16,2,128,128]{3,2,1,0:T(8,128)(2,1)}), bf16[16,2,128,128]{3,2,1,0:T(8,128)(2,1)S(1)}, u32[]{:S(2)}, u32[]{:S(2)}) %all-to-all-start) | async-done | bytes 1048608 | tf_op jit(solution)/shard_map/all_to_all | solution.py:142
  68.3 1.0 %copy-done.1 = bf16[16,2,128,128]{3,2,1,0:T(8,128)(2,1)} copy-done((bf16[16,2,128,128]{3,2,1,0:T(8,128)(2,1)}, bf16[16,2,128,128]{3,2,1,0:T(8,128)(2,1)S(1)}, u32[]{:S(2)}) %copy-start.1) | copy-done | bytes 1048600
  69.3 3.4 %shard_map.74 = f32[128,192]{1,0:T(8,128)} custom-call(s32[1]{0:T(128)S(6)} %copy.35.len_ref, bf16[192,128]{1,0:T(8,128)(2,1)} %bitcast.46, bf16[16,2,128,128]{3,2,1,0:T(8,128)(2,1)} %copy-done.1, bf16[48,128]{1,0:T(8,128)(2,1)} %get-tuple-element.11.dk_ref, bf16[48,128]{1,0:T(8,128)(2,1)} %get-tuple-element.12.dvt_ref, s32[48,192]{1,0:T(8,128)} %tile.10.tree_ref), custom_call_target="tpu_custom_call" | custom-call | tf_op jit(solution)/shard_map/pallas_call | solution.py:108
  72.7 3.3 %collective-permute-start.3 = (f32[128,192]{1,0:T(8,128)}, f32[128,192]{1,0:T(8,128)S(1)}, u32[]{:S(2)}, u32[]{:S(2)}) collective-permute-start(f32[128,192]{1,0:T(8,128)} %shard_map.74), channel_id=1, source_target_pairs={{0,1},{1,0},{2,3},{3,2},{4,5},{5,4},{6,7},{7,6},{8,9},{9,8},{10,11... | collective-permute-start | bytes 294920 | tf_op jit(solution)/shard_map/ppermute | solution.py:153
  76.0 3.4 %shard_map.73 = f32[128,192]{1,0:T(8,128)} custom-call(s32[1]{0:T(128)S(6)} %copy.35.len_ref, bf16[192,128]{1,0:T(8,128)(2,1)} %bitcast.45, bf16[16,2,128,128]{3,2,1,0:T(8,128)(2,1)} %copy-done.1, bf16[48,128]{1,0:T(8,128)(2,1)} %get-tuple-element.11.dk_ref, bf16[48,128]{1,0:T(8,128)(2,1)} %get-tuple-element.12.dvt_ref, s32[48,192]{1,0:T(8,128)} %tile.10.tree_ref), custom_call_target="tpu_custom_call" | custom-call | tf_op jit(solution)/shard_map/pallas_call | solution.py:108
  79.4 1.0 %copy.24 = f32[128,192]{0,1:T(8,128)S(1)} copy(f32[128,192]{1,0:T(8,128)} %shard_map.73) | data formatting | bytes 196608 | tf_op jit(solution)/shard_map/pallas_call | solution.py:108
  80.7 0.5 copy-done.3
  81.3 0.7 constant_dynamic-update-slice_fusion
  (32 shorter events, 0.6 us)
Async XLA Ops:
  0.0 1.0 %copy-start = (bf16[2,128,1024]{2,1,0:T(8,128)(2,1)S(1)}, bf16[2,128,1024]{2,1,0:T(8,128)(2,1)}, u32[]{:S(2)}) copy-start(bf16[2,128,1024]{2,1,0:T(8,128)(2,1)} %param.8) | copy-start | bytes 1572868
  0.0 1.2 %copy-start.2 = (bf16[2,128,1024]{2,1,0:T(8,128)(2,1)S(1)}, bf16[2,128,1024]{2,1,0:T(8,128)(2,1)}, u32[]{:S(2)}) copy-start(bf16[2,128,1024]{2,1,0:T(8,128)(2,1)} %param.9) | copy-start | bytes 1572868
  2.4 22.0 %copy-start.4 = (bf16[2,48,512]{2,1,0:T(8,128)(2,1)S(1)}, bf16[2,48,512]{2,1,0:T(8,128)(2,1)}, u32[]{:S(2)}) copy-start(bf16[2,48,512]{2,1,0:T(8,128)(2,1)} %param.7) | copy-start | bytes 294916
  2.4 65.9 %all-to-all-start = ((bf16[16,2,128,128]{3,2,1,0:T(8,128)(2,1)}), bf16[16,2,128,128]{3,2,1,0:T(8,128)(2,1)S(1)}, u32[]{:S(2)}, u32[]{:S(2)}) async-start(bf16[16,2,128,128]{3,2,1,0:T(8,128)(2,1)} %pad_maximum_fusion), calls=%async_computation | async-start | bytes 2097152 | tf_op jit(solution)/shard_map/all_to_all | solution.py:142
  17.8 0.7 copy-start.6
  17.8 4.6 %copy-start.7 = (bf16[2,48,64]{2,1,0:T(8,128)(2,1)S(1)}, bf16[2,48,64]{2,1,0:T(8,128)(2,1)}, u32[]{:S(2)}) copy-start(bf16[2,48,64]{2,1,0:T(8,128)(2,1)} %param.11) | copy-start | bytes 36868
  18.5 47.5 %collective-permute-start = (bf16[48,64]{1,0:T(8,128)(2,1)S(1)}, bf16[48,64]{1,0:T(8,128)(2,1)S(1)}, u32[]{:S(2)}, u32[]{:S(2)}) collective-permute-start(bf16[48,64]{1,0:T(8,128)(2,1)S(1)} %dynamic-slice_bitcast_fusion.2), channel_id=1, source_target_pairs={{0,1},{1,0},{2,3},{3,2},{4,5},{5,4},{6,7},{7,6},{8,9},{9,8},{10,11... | collective-permute-start | bytes 18440 | tf_op jit(solution)/shard_map/ppermute | solution.py:132
  22.4 43.8 %collective-permute-start.1 = (bf16[48,64]{1,0:T(8,128)(2,1)S(1)}, bf16[48,64]{1,0:T(8,128)(2,1)S(1)}, u32[]{:S(2)}, u32[]{:S(2)}) collective-permute-start(bf16[48,64]{1,0:T(8,128)(2,1)S(1)} %dynamic-slice_bitcast_fusion.1), channel_id=1, source_target_pairs={{0,1},{1,0},{2,3},{3,2},{4,5},{5,4},{6,7},{7,6},{8,9},{9,8},{10,11... | collective-permute-start | bytes 18440 | tf_op jit(solution)/shard_map/ppermute | solution.py:132
  24.4 3.9 %copy-start.5 = (s32[2,24,24]{2,1,0:T(8,128)S(1)}, s32[2,24,24]{2,1,0:T(8,128)}, u32[]{:S(2)}) copy-start(s32[2,24,24]{2,1,0:T(8,128)} %param.12) | copy-start | bytes 13828
  24.4 42.4 %collective-permute-start.2 = (bf16[48,512]{1,0:T(8,128)(2,1)S(1)}, bf16[48,512]{1,0:T(8,128)(2,1)S(1)}, u32[]{:S(2)}, u32[]{:S(2)}) collective-permute-start(bf16[48,512]{1,0:T(8,128)(2,1)S(1)} %get-tuple-element.5), channel_id=1, source_target_pairs={{0,1},{1,0},{2,3},{3,2},{4,5},{5,4},{6,7},{7,6},{8,9},{9,8},{10,11... | collective-permute-start | bytes 147464 | tf_op jit(solution)/shard_map/ppermute | solution.py:132
  68.3 1.0 %copy-start.1 = (bf16[16,2,128,128]{3,2,1,0:T(8,128)(2,1)}, bf16[16,2,128,128]{3,2,1,0:T(8,128)(2,1)S(1)}, u32[]{:S(2)}) copy-start(bf16[16,2,128,128]{3,2,1,0:T(8,128)(2,1)S(1)} %all-to-all-done.kv_ref) | copy-start | bytes 3145732
  72.7 7.9 %collective-permute-start.3 = (f32[128,192]{1,0:T(8,128)}, f32[128,192]{1,0:T(8,128)S(1)}, u32[]{:S(2)}, u32[]{:S(2)}) collective-permute-start(f32[128,192]{1,0:T(8,128)} %shard_map.74), channel_id=1, source_target_pairs={{0,1},{1,0},{2,3},{3,2},{4,5},{5,4},{6,7},{7,6},{8,9},{9,8},{10,11... | collective-permute-start | bytes 294920 | tf_op jit(solution)/shard_map/ppermute | solution.py:153
  80.6 0.7 copy-start.3

commit v11 on v10

--- a/solution.py
+++ b/solution.py
@@ -105,13 +105,15 @@
     rows = q_rows.shape[0]
     blocks = blocks_kv.shape[0]
     vmem = pl.BlockSpec(memory_space=pltpu.VMEM)
+    operands = [pltpu.with_memory_space_constraint(a, pltpu.VMEM)
+                for a in (q_rows, blocks_kv, draft_k, draft_vt, tree_cols)]
     return pl.pallas_call(
         attend_kernel,
         out_shape=jax.ShapeDtypeStruct((DH, rows), jnp.float32),
         in_specs=[pl.BlockSpec(memory_space=pltpu.SMEM)] + [vmem] * 5,
         out_specs=vmem,
         scratch_shapes=[pltpu.VMEM((blocks, DH, rows), jnp.float32), pltpu.VMEM((blocks, rows), jnp.float32)],
-    )(context_length, q_rows, blocks_kv, draft_k, draft_vt, tree_cols)
+    )(context_length, *operands)
 
 
 def body(queries, key_cache, value_cache, draft_keys, draft_values, ancestors, context_length):

time: 82.4 us -> 78.9 us (0.958)
  local copies, waits for them, and re-layouts: 7.71 us -> 4.46 us
  waiting for transfers between devices: 36.4 us -> 39.2 us
  Pallas kernels: 6.74 us -> 4.28 us
    pallas_call x2, Pallas kernels: 6.74 us -> 4.28 us  [attend(): pl.pallas_call(attend_kernel, out_shape=jax.ShapeDtypeStruct((DH, rows),...]
    ppermute x3, waiting for transfers between devices: 35.5 us -> 37.2 us  [body(): lax.ppermute(lax.dynamic_index_in_dim(a, other, 0, keepdims=False), 'ctx'...]
    unnamed x17 -> x15, local copies, waits for them, and re-layouts: 3.37 us -> 1.98 us
  transfers between devices with their start and end apart: 5 -> 5, of which waited for: 3 -> 5; matrix products, arithmetic and copies ran while one was open for 5% -> 2% of each run, Pallas kernels for 4% -> 3%
where the time goes in v11:
time: 78.9 us; the launch traced here: 78.5 us
  waiting for transfers between devices  39.2 us (50%)
  starting transfers between devices  28.3 us (36%)
  local copies, waits for them, and re-layouts  4.46 us (6%)
  Pallas kernels  4.28 us (5%)
  other arithmetic  1.26 us (2%)
  between operations  0.9 us (1%)
    ppermute x3, waiting for transfers between devices, body(): lax.ppermute(lax.dynamic_index_in_dim(a, other, 0, keepdims=False), 'ctx'...  37.2 us
    all_to_all x1, starting transfers between devices, body(): blocks = lax.all_to_all(kv, 'ctx', 0, 0, tiled=True)  15.3 us
    ppermute x3, starting transfers between devices, body(): lax.ppermute(lax.dynamic_index_in_dim(a, other, 0, keepdims=False), 'ctx'...  9.66 us
    pallas_call x2, Pallas kernels, attend(): pl.pallas_call(attend_kernel, out_shape=jax.ShapeDtypeStruct((DH, rows),...  4.28 us
    ppermute x1, starting transfers between devices, body(): got = lax.ppermute(give, 'ctx', swap)  3.34 us
    unnamed x15, local copies, waits for them, and re-layouts  1.98 us
    all_to_all x1, waiting for transfers between devices, body(): blocks = lax.all_to_all(kv, 'ctx', 0, 0, tiled=True)  1.64 us
  transfers between devices with their start and end apart: 5, of which 5 were waited for; matrix products, arithmetic and copies ran while one was open for 2% of the time, Pallas kernels for 3%

profile of v11, /device:TPU:6, one launch (start us, length us, event | category | flops | bytes accessed | tf_op | source)
XLA Modules:
  0.0 78.5 jit_solution(4569590454327098408)
XLA Ops:
  0.0 1.0 %copy-done = bf16[2,128,1024]{2,1,0:T(8,128)(2,1)S(1)} copy-done((bf16[2,128,1024]{2,1,0:T(8,128)(2,1)S(1)}, bf16[2,128,1024]{2,1,0:T(8,128)(2,1)}, u32[]{:S(2)}) %copy-start) | copy-done | bytes 524312
  1.0 0.1 copy_bitcast_fusion.1
  1.2 0.1 copy_bitcast_fusion
  1.3 1.1 %pad_maximum_fusion = bf16[16,2,128,128]{3,2,1,0:T(8,128)(2,1)} fusion(bf16[16,1,128,128]{3,2,1,0:T(8,128)(2,1)S(1)} %bitcast.44, bf16[16,1,128,128]{3,2,1,0:T(8,128)(2,1)S(1)} %bitcast.43), kind=kLoop, calls=%fused_computation | loop fusion | flops 524288 | bytes 2097152 | tf_op jit(solution)/shard_map/stack | solution.py:143
  2.4 15.3 %all-to-all-start = ((bf16[16,2,128,128]{3,2,1,0:T(8,128)(2,1)}), bf16[16,2,128,128]{3,2,1,0:T(8,128)(2,1)S(1)}, u32[]{:S(2)}, u32[]{:S(2)}) async-start(bf16[16,2,128,128]{3,2,1,0:T(8,128)(2,1)} %pad_maximum_fusion), calls=%async_computation | async-start | bytes 2097152 | tf_op jit(solution)/shard_map/all_to_all | solution.py:144
  17.8 0.7 copy-done.5
  18.5 3.8 %collective-permute-start = (bf16[48,64]{1,0:T(8,128)(2,1)S(1)}, bf16[48,64]{1,0:T(8,128)(2,1)S(1)}, u32[]{:S(2)}, u32[]{:S(2)}) collective-permute-start(bf16[48,64]{1,0:T(8,128)(2,1)S(1)} %dynamic-slice_bitcast_fusion.2), channel_id=1, source_target_pairs={{0,1},{1,0},{2,3},{3,2},{4,5},{5,4},{6,7},{7,6},{8,9},{9,8},{10,11... | collective-permute-start | bytes 18440 | tf_op jit(solution)/shard_map/ppermute | solution.py:134
  22.3 2.0 %collective-permute-start.1 = (bf16[48,64]{1,0:T(8,128)(2,1)S(1)}, bf16[48,64]{1,0:T(8,128)(2,1)S(1)}, u32[]{:S(2)}, u32[]{:S(2)}) collective-permute-start(bf16[48,64]{1,0:T(8,128)(2,1)S(1)} %dynamic-slice_bitcast_fusion.1), channel_id=1, source_target_pairs={{0,1},{1,0},{2,3},{3,2},{4,5},{5,4},{6,7},{7,6},{8,9},{9,8},{10,11... | collective-permute-start | bytes 18440 | tf_op jit(solution)/shard_map/ppermute | solution.py:134
  24.4 3.8 %collective-permute-start.2 = (bf16[48,512]{1,0:T(8,128)(2,1)S(1)}, bf16[48,512]{1,0:T(8,128)(2,1)S(1)}, u32[]{:S(2)}, u32[]{:S(2)}) collective-permute-start(bf16[48,512]{1,0:T(8,128)(2,1)S(1)} %get-tuple-element.5), channel_id=1, source_target_pairs={{0,1},{1,0},{2,3},{3,2},{4,5},{5,4},{6,7},{7,6},{8,9},{9,8},{10,11... | collective-permute-start | bytes 147464 | tf_op jit(solution)/shard_map/ppermute | solution.py:134
  28.4 0.1 broadcast_multiply_fusion
  28.4 0.1 mul.20
  28.6 0.1 tile.10.tree_ref
  29.4 36.6 %collective-permute-done = bf16[48,64]{1,0:T(8,128)(2,1)S(1)} collective-permute-done((bf16[48,64]{1,0:T(8,128)(2,1)S(1)}, bf16[48,64]{1,0:T(8,128)(2,1)S(1)}, u32[]{:S(2)}, u32[]{:S(2)}) %collective-permute-start) | collective-permute-done | bytes 6176 | tf_op jit(solution)/shard_map/ppermute | solution.py:134
  66.0 0.2 collective-permute-done.1
  66.2 0.4 collective-permute-done.2
  66.7 1.6 %all-to-all-done.kv_ref = bf16[16,2,128,128]{3,2,1,0:T(8,128)(2,1)S(1)} async-done(((bf16[16,2,128,128]{3,2,1,0:T(8,128)(2,1)}), bf16[16,2,128,128]{3,2,1,0:T(8,128)(2,1)S(1)}, u32[]{:S(2)}, u32[]{:S(2)}) %all-to-all-start) | async-done | bytes 1048608 | tf_op jit(solution)/shard_map/all_to_all | solution.py:144
  68.3 2.1 %shard_map.74 = f32[128,192]{1,0:T(8,128)} custom-call(s32[1]{0:T(128)S(6)} %copy.35.len_ref, bf16[192,128]{1,0:T(8,128)(2,1)S(1)} %bitcast.42, bf16[16,2,128,128]{3,2,1,0:T(8,128)(2,1)S(1)} %all-to-all-done.kv_ref, bf16[48,128]{1,0:T(8,128)(2,1)S(1)} %get-tuple-element.11.dk_ref, bf16[48,128]{1,0:T(8,128)(2,1)S(1)} %get-tuple-element.12.dvt_ref, ...), custom_call_target="tpu_custom_call" | custom-call | tf_op jit(solution)/shard_map/pallas_call | solution.py:110
  70.5 3.3 %collective-permute-start.3 = (f32[128,192]{1,0:T(8,128)}, f32[128,192]{1,0:T(8,128)S(1)}, u32[]{:S(2)}, u32[]{:S(2)}) collective-permute-start(f32[128,192]{1,0:T(8,128)} %shard_map.74), channel_id=1, source_target_pairs={{0,1},{1,0},{2,3},{3,2},{4,5},{5,4},{6,7},{7,6},{8,9},{9,8},{10,11... | collective-permute-start | bytes 294920 | tf_op jit(solution)/shard_map/ppermute | solution.py:155
  73.8 2.1 %shard_map.73 = f32[128,192]{1,0:T(8,128)} custom-call(s32[1]{0:T(128)S(6)} %copy.35.len_ref, bf16[192,128]{1,0:T(8,128)(2,1)S(1)} %bitcast.41, bf16[16,2,128,128]{3,2,1,0:T(8,128)(2,1)S(1)} %all-to-all-done.kv_ref, bf16[48,128]{1,0:T(8,128)(2,1)S(1)} %get-tuple-element.11.dk_ref, bf16[48,128]{1,0:T(8,128)(2,1)S(1)} %get-tuple-element.12.dvt_ref, ...), custom_call_target="tpu_custom_call" | custom-call | tf_op jit(solution)/shard_map/pallas_call | solution.py:110
  76.0 1.0 %copy.24 = f32[128,192]{0,1:T(8,128)S(1)} copy(f32[128,192]{1,0:T(8,128)} %shard_map.73) | data formatting | bytes 196608 | tf_op jit(solution)/shard_map/pallas_call | solution.py:110
  77.1 0.4 collective-permute-done.3
  77.5 0.1 copy.27
  77.7 0.1 copy-done.2
  77.8 0.7 constant_dynamic-update-slice_fusion
  (30 shorter events, 0.5 us)
Async XLA Ops:
  0.0 1.0 %copy-start = (bf16[2,128,1024]{2,1,0:T(8,128)(2,1)S(1)}, bf16[2,128,1024]{2,1,0:T(8,128)(2,1)}, u32[]{:S(2)}) copy-start(bf16[2,128,1024]{2,1,0:T(8,128)(2,1)} %param.8) | copy-start | bytes 1572868
  0.0 1.2 %copy-start.1 = (bf16[2,128,1024]{2,1,0:T(8,128)(2,1)S(1)}, bf16[2,128,1024]{2,1,0:T(8,128)(2,1)}, u32[]{:S(2)}) copy-start(bf16[2,128,1024]{2,1,0:T(8,128)(2,1)} %param.9) | copy-start | bytes 1572868
  2.4 22.0 %copy-start.3 = (bf16[2,48,512]{2,1,0:T(8,128)(2,1)S(1)}, bf16[2,48,512]{2,1,0:T(8,128)(2,1)}, u32[]{:S(2)}) copy-start(bf16[2,48,512]{2,1,0:T(8,128)(2,1)} %param.7) | copy-start | bytes 294916
  2.4 65.9 %all-to-all-start = ((bf16[16,2,128,128]{3,2,1,0:T(8,128)(2,1)}), bf16[16,2,128,128]{3,2,1,0:T(8,128)(2,1)S(1)}, u32[]{:S(2)}, u32[]{:S(2)}) async-start(bf16[16,2,128,128]{3,2,1,0:T(8,128)(2,1)} %pad_maximum_fusion), calls=%async_computation | async-start | bytes 2097152 | tf_op jit(solution)/shard_map/all_to_all | solution.py:144
  17.7 0.7 copy-start.5
  17.8 4.6 %copy-start.6 = (bf16[2,48,64]{2,1,0:T(8,128)(2,1)S(1)}, bf16[2,48,64]{2,1,0:T(8,128)(2,1)}, u32[]{:S(2)}) copy-start(bf16[2,48,64]{2,1,0:T(8,128)(2,1)} %param.11) | copy-start | bytes 36868
  18.5 47.5 %collective-permute-start = (bf16[48,64]{1,0:T(8,128)(2,1)S(1)}, bf16[48,64]{1,0:T(8,128)(2,1)S(1)}, u32[]{:S(2)}, u32[]{:S(2)}) collective-permute-start(bf16[48,64]{1,0:T(8,128)(2,1)S(1)} %dynamic-slice_bitcast_fusion.2), channel_id=1, source_target_pairs={{0,1},{1,0},{2,3},{3,2},{4,5},{5,4},{6,7},{7,6},{8,9},{9,8},{10,11... | collective-permute-start | bytes 18440 | tf_op jit(solution)/shard_map/ppermute | solution.py:134
  22.3 43.8 %collective-permute-start.1 = (bf16[48,64]{1,0:T(8,128)(2,1)S(1)}, bf16[48,64]{1,0:T(8,128)(2,1)S(1)}, u32[]{:S(2)}, u32[]{:S(2)}) collective-permute-start(bf16[48,64]{1,0:T(8,128)(2,1)S(1)} %dynamic-slice_bitcast_fusion.1), channel_id=1, source_target_pairs={{0,1},{1,0},{2,3},{3,2},{4,5},{5,4},{6,7},{7,6},{8,9},{9,8},{10,11... | collective-permute-start | bytes 18440 | tf_op jit(solution)/shard_map/ppermute | solution.py:134
  24.4 3.9 %copy-start.4 = (s32[2,24,24]{2,1,0:T(8,128)S(1)}, s32[2,24,24]{2,1,0:T(8,128)}, u32[]{:S(2)}) copy-start(s32[2,24,24]{2,1,0:T(8,128)} %param.12) | copy-start | bytes 13828
  24.4 42.2 %collective-permute-start.2 = (bf16[48,512]{1,0:T(8,128)(2,1)S(1)}, bf16[48,512]{1,0:T(8,128)(2,1)S(1)}, u32[]{:S(2)}, u32[]{:S(2)}) collective-permute-start(bf16[48,512]{1,0:T(8,128)(2,1)S(1)} %get-tuple-element.5), channel_id=1, source_target_pairs={{0,1},{1,0},{2,3},{3,2},{4,5},{5,4},{6,7},{7,6},{8,9},{9,8},{10,11... | collective-permute-start | bytes 147464 | tf_op jit(solution)/shard_map/ppermute | solution.py:134
  70.5 7.1 %collective-permute-start.3 = (f32[128,192]{1,0:T(8,128)}, f32[128,192]{1,0:T(8,128)S(1)}, u32[]{:S(2)}, u32[]{:S(2)}) collective-permute-start(f32[128,192]{1,0:T(8,128)} %shard_map.74), channel_id=1, source_target_pairs={{0,1},{1,0},{2,3},{3,2},{4,5},{5,4},{6,7},{7,6},{8,9},{9,8},{10,11... | collective-permute-start | bytes 294920 | tf_op jit(solution)/shard_map/ppermute | solution.py:155
  77.1 0.7 copy-start.2

commit v12 on v11

--- a/solution.py
+++ b/solution.py
@@ -98,10 +98,13 @@
     weighted = factor[0:1] * out_sc[0]
     for j in range(1, blocks):
         weighted = weighted + factor[j:j + 1] * out_sc[j]
-    o_ref[...] = weighted / jnp.sum(factor, axis=0, keepdims=True)
+    final = jnp.transpose(weighted / jnp.sum(factor, axis=0, keepdims=True))
+    rows = o_ref.shape[0]
+    for i in range(o_ref.shape[1] // DH):
+        o_ref[:, i * DH:(i + 1) * DH] = final[i * rows:(i + 1) * rows, :]
 
 
-def attend(context_length, q_rows, blocks_kv, draft_k, draft_vt, tree_cols):
+def attend(context_length, q_rows, blocks_kv, draft_k, draft_vt, tree_cols, heads):
     rows = q_rows.shape[0]
     blocks = blocks_kv.shape[0]
     vmem = pl.BlockSpec(memory_space=pltpu.VMEM)
@@ -109,7 +112,7 @@
                 for a in (q_rows, blocks_kv, draft_k, draft_vt, tree_cols)]
     return pl.pallas_call(
         attend_kernel,
-        out_shape=jax.ShapeDtypeStruct((DH, rows), jnp.float32),
+        out_shape=jax.ShapeDtypeStruct((rows // heads, heads * DH), jnp.float32),
         in_specs=[pl.BlockSpec(memory_space=pltpu.SMEM)] + [vmem] * 5,
         out_specs=vmem,
         scratch_shapes=[pltpu.VMEM((blocks, DH, rows), jnp.float32), pltpu.VMEM((blocks, rows), jnp.float32)],
@@ -151,14 +154,17 @@
     draft_k = jnp.concatenate([first[1], second[1]], 1)
     draft_vt = jnp.concatenate([first[2], second[2]], 1)
     tree_cols = jnp.tile(jnp.transpose(tree_keep), (1, heads_here))
-    give = attend(context_length, other_q.reshape(heads_here * rows, DH), blocks, draft_k, draft_vt, tree_cols)
+    give = attend(context_length, other_q.reshape(heads_here * rows, DH), blocks, draft_k, draft_vt, tree_cols,
+                  heads_here)
     got = lax.ppermute(give, "ctx", swap)
-    keep = attend(context_length, own_q.reshape(heads_here * rows, DH), blocks, draft_k, draft_vt, tree_cols)
-    keep = jnp.transpose(keep.reshape(DH, heads_here, rows), (2, 1, 0)).reshape(1, rows, heads_here * DH)
-    got = jnp.transpose(got.reshape(DH, heads_here, rows), (2, 1, 0)).reshape(1, rows, heads_here * DH)
+    keep = attend(context_length, own_q.reshape(heads_here * rows, DH), blocks, draft_k, draft_vt, tree_cols,
+                  heads_here)
+    keep = keep[None]
+    got = got[None]
     result = jnp.zeros((layers, rows, heads_here * DH), jnp.float32)
     result = lax.dynamic_update_slice(result, keep, (own, 0, 0))
     return lax.dynamic_update_slice(result, got, (other, 0, 0))
+
 
 def solution(mesh):
     placed = (

time: 78.9 us -> 78.3 us (level)
  Pallas kernels: 4.28 us -> 2.16 us
  waiting for transfers between devices: 39.2 us -> 40.6 us
    pallas_call x2 -> x1, Pallas kernels: 4.28 us -> 2.16 us  [attend(): pl.pallas_call(attend_kernel, out_shape=jax.ShapeDtypeStruct((rows // hea...]
    ppermute x1, waiting for transfers between devices: 0.42 us -> 1.76 us  [body(): got = lax.ppermute(give, 'ctx', swap)]
  transfers between devices with their start and end apart: 5 -> 5, of which waited for: 5 -> 5; matrix products, arithmetic and copies ran while one was open for 2% -> 3% of each run, Pallas kernels for 3% -> 0%
where the time goes in v12:
time: 78.3 us; the launch traced here: 77.8 us
  waiting for transfers between devices  40.6 us (52%)
  starting transfers between devices  28.3 us (36%)
  local copies, waits for them, and re-layouts  4.61 us (6%)
  Pallas kernels  2.16 us (3%)
  other arithmetic  1.26 us (2%)
  between operations  0.86 us (1%)
    ppermute x3, waiting for transfers between devices, body(): lax.ppermute(lax.dynamic_index_in_dim(a, other, 0, keepdims=False), 'ctx'...  37.2 us
    all_to_all x1, starting transfers between devices, body(): blocks = lax.all_to_all(kv, 'ctx', 0, 0, tiled=True)  15.3 us
    ppermute x3, starting transfers between devices, body(): lax.ppermute(lax.dynamic_index_in_dim(a, other, 0, keepdims=False), 'ctx'...  9.66 us
    ppermute x1, starting transfers between devices, body(): got = lax.ppermute(give, 'ctx', swap)  3.34 us
    pallas_call x1, Pallas kernels, attend(): pl.pallas_call(attend_kernel, out_shape=jax.ShapeDtypeStruct((rows // hea...  2.16 us
    unnamed x15, local copies, waits for them, and re-layouts  1.87 us
    ppermute x1, waiting for transfers between devices, body(): got = lax.ppermute(give, 'ctx', swap)  1.76 us
    all_to_all x1, waiting for transfers between devices, body(): blocks = lax.all_to_all(kv, 'ctx', 0, 0, tiled=True)  1.64 us
  transfers between devices with their start and end apart: 5, of which 5 were waited for; matrix products, arithmetic and copies ran while one was open for 3% of the time, Pallas kernels for 0%

profile of v12, /device:TPU:6, one launch (start us, length us, event | category | flops | bytes accessed | tf_op | source)
XLA Modules:
  0.0 77.8 jit_solution(7704346638415715557)
XLA Ops:
  0.0 1.0 %copy-done = bf16[2,128,1024]{2,1,0:T(8,128)(2,1)S(1)} copy-done((bf16[2,128,1024]{2,1,0:T(8,128)(2,1)S(1)}, bf16[2,128,1024]{2,1,0:T(8,128)(2,1)}, u32[]{:S(2)}) %copy-start) | copy-done | bytes 524312
  1.0 0.1 copy_bitcast_fusion.1
  1.2 0.0 copy-done.1
  1.2 0.1 copy_bitcast_fusion
  1.3 1.1 %pad_maximum_fusion = bf16[16,2,128,128]{3,2,1,0:T(8,128)(2,1)} fusion(bf16[16,1,128,128]{3,2,1,0:T(8,128)(2,1)S(1)} %bitcast.41, bf16[16,1,128,128]{3,2,1,0:T(8,128)(2,1)S(1)} %bitcast.40), kind=kLoop, calls=%fused_computation | loop fusion | flops 524288 | bytes 2097152 | tf_op jit(solution)/shard_map/stack | solution.py:146
  2.4 15.3 %all-to-all-start = ((bf16[16,2,128,128]{3,2,1,0:T(8,128)(2,1)}), bf16[16,2,128,128]{3,2,1,0:T(8,128)(2,1)S(1)}, u32[]{:S(2)}, u32[]{:S(2)}) async-start(bf16[16,2,128,128]{3,2,1,0:T(8,128)(2,1)} %pad_maximum_fusion), calls=%async_computation | async-start | bytes 2097152 | tf_op jit(solution)/shard_map/all_to_all | solution.py:147
  17.8 0.7 copy-done.5
  18.5 3.8 %collective-permute-start = (bf16[48,64]{1,0:T(8,128)(2,1)S(1)}, bf16[48,64]{1,0:T(8,128)(2,1)S(1)}, u32[]{:S(2)}, u32[]{:S(2)}) collective-permute-start(bf16[48,64]{1,0:T(8,128)(2,1)S(1)} %dynamic-slice_bitcast_fusion.2), channel_id=1, source_target_pairs={{0,1},{1,0},{2,3},{3,2},{4,5},{5,4},{6,7},{7,6},{8,9},{9,8},{10,11... | collective-permute-start | bytes 18440 | tf_op jit(solution)/shard_map/ppermute | solution.py:137
  22.3 2.0 %collective-permute-start.1 = (bf16[48,64]{1,0:T(8,128)(2,1)S(1)}, bf16[48,64]{1,0:T(8,128)(2,1)S(1)}, u32[]{:S(2)}, u32[]{:S(2)}) collective-permute-start(bf16[48,64]{1,0:T(8,128)(2,1)S(1)} %dynamic-slice_bitcast_fusion.1), channel_id=1, source_target_pairs={{0,1},{1,0},{2,3},{3,2},{4,5},{5,4},{6,7},{7,6},{8,9},{9,8},{10,11... | collective-permute-start | bytes 18440 | tf_op jit(solution)/shard_map/ppermute | solution.py:137
  24.4 3.8 %collective-permute-start.2 = (bf16[48,512]{1,0:T(8,128)(2,1)S(1)}, bf16[48,512]{1,0:T(8,128)(2,1)S(1)}, u32[]{:S(2)}, u32[]{:S(2)}) collective-permute-start(bf16[48,512]{1,0:T(8,128)(2,1)S(1)} %get-tuple-element.5), channel_id=1, source_target_pairs={{0,1},{1,0},{2,3},{3,2},{4,5},{5,4},{6,7},{7,6},{8,9},{9,8},{10,11... | collective-permute-start | bytes 147464 | tf_op jit(solution)/shard_map/ppermute | solution.py:137
  28.3 0.1 copy.14
  28.4 0.1 broadcast_multiply_fusion
  28.4 0.1 mul.20
  28.6 0.1 tile.10.tree_ref
  29.3 36.6 %collective-permute-done = bf16[48,64]{1,0:T(8,128)(2,1)S(1)} collective-permute-done((bf16[48,64]{1,0:T(8,128)(2,1)S(1)}, bf16[48,64]{1,0:T(8,128)(2,1)S(1)}, u32[]{:S(2)}, u32[]{:S(2)}) %collective-permute-start) | collective-permute-done | bytes 6176 | tf_op jit(solution)/shard_map/ppermute | solution.py:137
  66.0 0.2 collective-permute-done.1
  66.1 0.1 pad_maximum_fusion.1
  66.2 0.4 collective-permute-done.2
  66.7 1.6 %all-to-all-done.kv_ref = bf16[16,2,128,128]{3,2,1,0:T(8,128)(2,1)S(1)} async-done(((bf16[16,2,128,128]{3,2,1,0:T(8,128)(2,1)}), bf16[16,2,128,128]{3,2,1,0:T(8,128)(2,1)S(1)}, u32[]{:S(2)}, u32[]{:S(2)}) %all-to-all-start) | async-done | bytes 1048608 | tf_op jit(solution)/shard_map/all_to_all | solution.py:147
  68.3 2.2 %shard_map.73 = f32[48,512]{1,0:T(8,128)} custom-call(s32[1]{0:T(128)S(6)} %copy.22.len_ref, bf16[192,128]{1,0:T(8,128)(2,1)S(1)} %bitcast.39, bf16[16,2,128,128]{3,2,1,0:T(8,128)(2,1)S(1)} %all-to-all-done.kv_ref, bf16[48,128]{1,0:T(8,128)(2,1)S(1)} %get-tuple-element.11.dk_ref, bf16[48,128]{1,0:T(8,128)(2,1)S(1)} %get-tuple-element.12.dvt_ref, ...), custom_call_target="tpu_custom_call" | custom-call | tf_op jit(solution)/shard_map/pallas_call | solution.py:113
  70.5 3.3 %collective-permute-start.3 = (f32[48,512]{1,0:T(8,128)}, f32[48,512]{1,0:T(8,128)S(1)}, u32[]{:S(2)}, u32[]{:S(2)}) collective-permute-start(f32[48,512]{1,0:T(8,128)} %shard_map.73), channel_id=1, source_target_pairs={{0,1},{1,0},{2,3},{3,2},{4,5},{5,4},{6,7},{7,6},{8,9},{9,8},{10,11... | collective-permute-start | bytes 294920 | tf_op jit(solution)/shard_map/ppermute | solution.py:159
  73.9 1.5 %shard_map.74 = f32[2,48,512]{2,1,0:T(8,128)S(1)} fusion(f32[2,48,512]{2,1,0:T(8,128)S(1)} %broadcast_in_dim.11, s32[]{:T(128)S(6)} %select_n.42, s32[1]{0:T(128)S(6)} %copy.22.len_ref, bf16[192,128]{1,0:T(8,128)(2,1)S(1)} %bitcast.42, bf16[16,2,128,128]{3,2,1,0:T(8,128)(2,1)S(1)} %all-to-all-done.kv_ref, bf16[48,128]{1,0:T(8,128)(2,1)S(1)} %get-tuple-element.11.dk_ref, ...), kind=kCustom, calls=%fused_computation.4 | custom fusion | bytes 1269768 | tf_op jit(solution)/shard_map/pallas_call | solution.py:113
  75.4 1.8 %collective-permute-done.3 = f32[48,512]{1,0:T(8,128)S(1)} collective-permute-done((f32[48,512]{1,0:T(8,128)}, f32[48,512]{1,0:T(8,128)S(1)}, u32[]{:S(2)}, u32[]{:S(2)}) %collective-permute-start.3) | collective-permute-done | bytes 98336 | tf_op jit(solution)/shard_map/ppermute | solution.py:159
  77.2 0.6 bitcast_dynamic-update-slice_fusion
  (23 shorter events, 0.2 us)
Async XLA Ops:
  0.0 1.0 %copy-start = (bf16[2,128,1024]{2,1,0:T(8,128)(2,1)S(1)}, bf16[2,128,1024]{2,1,0:T(8,128)(2,1)}, u32[]{:S(2)}) copy-start(bf16[2,128,1024]{2,1,0:T(8,128)(2,1)} %param.8) | copy-start | bytes 1572868
  0.0 1.2 %copy-start.1 = (bf16[2,128,1024]{2,1,0:T(8,128)(2,1)S(1)}, bf16[2,128,1024]{2,1,0:T(8,128)(2,1)}, u32[]{:S(2)}) copy-start(bf16[2,128,1024]{2,1,0:T(8,128)(2,1)} %param.9) | copy-start | bytes 1572868
  2.4 22.0 %copy-start.3 = (bf16[2,48,512]{2,1,0:T(8,128)(2,1)S(1)}, bf16[2,48,512]{2,1,0:T(8,128)(2,1)}, u32[]{:S(2)}) copy-start(bf16[2,48,512]{2,1,0:T(8,128)(2,1)} %param.7) | copy-start | bytes 294916
  2.4 65.9 %all-to-all-start = ((bf16[16,2,128,128]{3,2,1,0:T(8,128)(2,1)}), bf16[16,2,128,128]{3,2,1,0:T(8,128)(2,1)S(1)}, u32[]{:S(2)}, u32[]{:S(2)}) async-start(bf16[16,2,128,128]{3,2,1,0:T(8,128)(2,1)} %pad_maximum_fusion), calls=%async_computation | async-start | bytes 2097152 | tf_op jit(solution)/shard_map/all_to_all | solution.py:147
  17.7 0.7 copy-start.5
  17.8 4.6 %copy-start.6 = (bf16[2,48,64]{2,1,0:T(8,128)(2,1)S(1)}, bf16[2,48,64]{2,1,0:T(8,128)(2,1)}, u32[]{:S(2)}) copy-start(bf16[2,48,64]{2,1,0:T(8,128)(2,1)} %param.11) | copy-start | bytes 36868
  18.5 47.5 %collective-permute-start = (bf16[48,64]{1,0:T(8,128)(2,1)S(1)}, bf16[48,64]{1,0:T(8,128)(2,1)S(1)}, u32[]{:S(2)}, u32[]{:S(2)}) collective-permute-start(bf16[48,64]{1,0:T(8,128)(2,1)S(1)} %dynamic-slice_bitcast_fusion.2), channel_id=1, source_target_pairs={{0,1},{1,0},{2,3},{3,2},{4,5},{5,4},{6,7},{7,6},{8,9},{9,8},{10,11... | collective-permute-start | bytes 18440 | tf_op jit(solution)/shard_map/ppermute | solution.py:137
  22.3 43.8 %collective-permute-start.1 = (bf16[48,64]{1,0:T(8,128)(2,1)S(1)}, bf16[48,64]{1,0:T(8,128)(2,1)S(1)}, u32[]{:S(2)}, u32[]{:S(2)}) collective-permute-start(bf16[48,64]{1,0:T(8,128)(2,1)S(1)} %dynamic-slice_bitcast_fusion.1), channel_id=1, source_target_pairs={{0,1},{1,0},{2,3},{3,2},{4,5},{5,4},{6,7},{7,6},{8,9},{9,8},{10,11... | collective-permute-start | bytes 18440 | tf_op jit(solution)/shard_map/ppermute | solution.py:137
  24.4 3.9 %copy-start.4 = (s32[2,24,24]{2,1,0:T(8,128)S(1)}, s32[2,24,24]{2,1,0:T(8,128)}, u32[]{:S(2)}) copy-start(s32[2,24,24]{2,1,0:T(8,128)} %param.12) | copy-start | bytes 13828
  24.4 42.2 %collective-permute-start.2 = (bf16[48,512]{1,0:T(8,128)(2,1)S(1)}, bf16[48,512]{1,0:T(8,128)(2,1)S(1)}, u32[]{:S(2)}, u32[]{:S(2)}) collective-permute-start(bf16[48,512]{1,0:T(8,128)(2,1)S(1)} %get-tuple-element.5), channel_id=1, source_target_pairs={{0,1},{1,0},{2,3},{3,2},{4,5},{5,4},{6,7},{7,6},{8,9},{9,8},{10,11... | collective-permute-start | bytes 147464 | tf_op jit(solution)/shard_map/ppermute | solution.py:137
  70.5 6.7 %collective-permute-start.3 = (f32[48,512]{1,0:T(8,128)}, f32[48,512]{1,0:T(8,128)S(1)}, u32[]{:S(2)}, u32[]{:S(2)}) collective-permute-start(f32[48,512]{1,0:T(8,128)} %shard_map.73), channel_id=1, source_target_pairs={{0,1},{1,0},{2,3},{3,2},{4,5},{5,4},{6,7},{7,6},{8,9},{9,8},{10,11... | collective-permute-start | bytes 294920 | tf_op jit(solution)/shard_map/ppermute | solution.py:159
  75.4 1.8 %copy-start.2 = (f32[2,48,512]{2,1,0:T(8,128)}, f32[2,48,512]{2,1,0:T(8,128)S(1)}, u32[]{:S(2)}) copy-start(f32[2,48,512]{2,1,0:T(8,128)S(1)} %shard_map.74) | copy-start | bytes 589828

commit v13 on v12

--- a/solution.py
+++ b/solution.py
@@ -119,6 +119,34 @@
     )(context_length, *operands)
 
 
+def pack_kernel(k_ref, v_ref, o_ref, sem):
+    layers, _, width = k_ref.shape
+    copies = []
+    for k in range(width // DH):
+        for l in range(layers):
+            for c, src in enumerate((k_ref, v_ref)):
+                copy = pltpu.make_async_copy(
+                    src.at[l, :, pl.ds(k * DH, DH)], o_ref.at[k * layers + l, c], sem.at[len(copies)]
+                )
+                copy.start()
+                copies.append(copy)
+    for copy in copies:
+        copy.wait()
+
+
+def pack(key_cache, value_cache):
+    layers, local_len, width = key_cache.shape
+    n = layers * (width // DH)
+    anywhere = pl.BlockSpec(memory_space=pl.ANY)
+    return pl.pallas_call(
+        pack_kernel,
+        out_shape=jax.ShapeDtypeStruct((n, 2, local_len, DH), key_cache.dtype),
+        in_specs=[anywhere, anywhere],
+        out_specs=anywhere,
+        scratch_shapes=[pltpu.SemaphoreType.DMA((2 * n,))],
+    )(key_cache, value_cache)
+
+
 def body(queries, key_cache, value_cache, draft_keys, draft_values, ancestors, context_length):
     n = lax.axis_size("ctx")
     d = lax.axis_index("ctx")
@@ -141,9 +169,7 @@
     first = [jnp.where(own == 0, a, b) for a, b in zip(mine_now, swapped)]
     second = [jnp.where(own == 0, b, a) for a, b in zip(mine_now, swapped)]
 
-    keys_out = jnp.transpose(key_cache.reshape(layers, local_len, KVH, DH), (2, 0, 1, 3))
-    values_out = jnp.transpose(value_cache.reshape(layers, local_len, KVH, DH), (2, 0, 1, 3))
-    kv = jnp.stack([keys_out, values_out], 2).reshape(n, 2, local_len, DH)
+    kv = pack(key_cache, value_cache)
     blocks = lax.all_to_all(kv, "ctx", 0, 0, tiled=True)
 
     tree_keep = (

time: 78.3 us -> 109 us (1.39)
  Pallas kernels: 2.16 us -> 35.3 us
  local copies, waits for them, and re-layouts: 4.61 us -> 3.3 us
    pallas_call x0 -> x1, Pallas kernels: none -> 33.1 us  [pack(): pl.pallas_call(pack_kernel, out_shape=jax.ShapeDtypeStruct((n, 2, local_l...]
  transfers between devices with their start and end apart: 5 -> 5, of which waited for: 5 -> 5; matrix products, arithmetic and copies ran while one was open for 3% -> 2% of each run, Pallas kernels for 0% -> 0%
where the time goes in v13:
time: 109 us
  waiting for transfers between devices  40.6 us (37%)
  Pallas kernels  35.3 us (32%)
  starting transfers between devices  28.3 us (26%)
  local copies, waits for them, and re-layouts  3.3 us (3%)
    ppermute x3, waiting for transfers between devices, body(): lax.ppermute(lax.dynamic_index_in_dim(a, other, 0, keepdims=False), 'ctx'...  37.2 us
    pallas_call x1, Pallas kernels, pack(): pl.pallas_call(pack_kernel, out_shape=jax.ShapeDtypeStruct((n, 2, local_l...  33.1 us
    all_to_all x1, starting transfers between devices, body(): blocks = lax.all_to_all(kv, 'ctx', 0, 0, tiled=True)  15.3 us
    ppermute x3, starting transfers between devices, body(): lax.ppermute(lax.dynamic_index_in_dim(a, other, 0, keepdims=False), 'ctx'...  9.66 us
    ppermute x1, starting transfers between devices, body(): got = lax.ppermute(give, 'ctx', swap)  3.34 us
  transfers between devices with their start and end apart: 5, of which 5 were waited for; matrix products, arithmetic and copies ran while one was open for 2% of the time, Pallas kernels for 0%

profile of v13, /device:TPU:6, one launch (start us, length us, event | category | flops | bytes accessed | tf_op | source)
XLA Modules:
  0.0 108.6 jit_solution(11648628213041483118)
XLA Ops:
  0.0 33.1 %shard_map.73 = bf16[16,2,128,128]{3,2,1,0:T(8,128)(2,1)} custom-call(bf16[2,128,1024]{2,1,0:T(8,128)(2,1)} %k_ref.1, bf16[2,128,1024]{2,1,0:T(8,128)(2,1)} %v_ref.1), custom_call_target="tpu_custom_call" | custom-call | tf_op jit(solution)/shard_map/pallas_call | solution.py:141
  33.2 0.0 copy-start.1
  33.2 15.3 %all-to-all-start = ((bf16[16,2,128,128]{3,2,1,0:T(8,128)(2,1)}), bf16[16,2,128,128]{3,2,1,0:T(8,128)(2,1)S(1)}, u32[]{:S(2)}, u32[]{:S(2)}) async-start(bf16[16,2,128,128]{3,2,1,0:T(8,128)(2,1)} %shard_map.73), calls=%async_computation | async-start | bytes 2097152 | tf_op jit(solution)/shard_map/all_to_all | solution.py:173
  48.5 0.0 copy-start.3
  48.6 0.7 copy-done.3
  49.3 3.8 %collective-permute-start = (bf16[48,64]{1,0:T(8,128)(2,1)S(1)}, bf16[48,64]{1,0:T(8,128)(2,1)S(1)}, u32[]{:S(2)}, u32[]{:S(2)}) collective-permute-start(bf16[48,64]{1,0:T(8,128)(2,1)S(1)} %dynamic-slice_bitcast_fusion.2), channel_id=1, source_target_pairs={{0,1},{1,0},{2,3},{3,2},{4,5},{5,4},{6,7},{7,6},{8,9},{9,8},{10,11... | collective-permute-start | bytes 18440 | tf_op jit(solution)/shard_map/ppermute | solution.py:165
  53.1 2.0 %collective-permute-start.1 = (bf16[48,64]{1,0:T(8,128)(2,1)S(1)}, bf16[48,64]{1,0:T(8,128)(2,1)S(1)}, u32[]{:S(2)}, u32[]{:S(2)}) collective-permute-start(bf16[48,64]{1,0:T(8,128)(2,1)S(1)} %dynamic-slice_bitcast_fusion.1), channel_id=1, source_target_pairs={{0,1},{1,0},{2,3},{3,2},{4,5},{5,4},{6,7},{7,6},{8,9},{9,8},{10,11... | collective-permute-start | bytes 18440 | tf_op jit(solution)/shard_map/ppermute | solution.py:165
  55.2 0.0 copy-start.2
  55.2 3.8 %collective-permute-start.2 = (bf16[48,512]{1,0:T(8,128)(2,1)S(1)}, bf16[48,512]{1,0:T(8,128)(2,1)S(1)}, u32[]{:S(2)}, u32[]{:S(2)}) collective-permute-start(bf16[48,512]{1,0:T(8,128)(2,1)S(1)} %get-tuple-element.5), channel_id=1, source_target_pairs={{0,1},{1,0},{2,3},{3,2},{4,5},{5,4},{6,7},{7,6},{8,9},{9,8},{10,11... | collective-permute-start | bytes 147464 | tf_op jit(solution)/shard_map/ppermute | solution.py:165
  59.0 0.1 copy.10
  59.1 0.1 broadcast_multiply_fusion
  59.2 0.1 mul.20
  59.3 0.1 tile.10.tree_ref
  60.1 36.6 %collective-permute-done = bf16[48,64]{1,0:T(8,128)(2,1)S(1)} collective-permute-done((bf16[48,64]{1,0:T(8,128)(2,1)S(1)}, bf16[48,64]{1,0:T(8,128)(2,1)S(1)}, u32[]{:S(2)}, u32[]{:S(2)}) %collective-permute-start) | collective-permute-done | bytes 6176 | tf_op jit(solution)/shard_map/ppermute | solution.py:165
  96.7 0.2 collective-permute-done.1
  96.9 0.1 pad_maximum_fusion
  97.0 0.4 collective-permute-done.2
  97.5 1.6 %all-to-all-done.kv_ref = bf16[16,2,128,128]{3,2,1,0:T(8,128)(2,1)S(1)} async-done(((bf16[16,2,128,128]{3,2,1,0:T(8,128)(2,1)}), bf16[16,2,128,128]{3,2,1,0:T(8,128)(2,1)S(1)}, u32[]{:S(2)}, u32[]{:S(2)}) %all-to-all-start) | async-done | bytes 1048608 | tf_op jit(solution)/shard_map/all_to_all | solution.py:173
  99.1 2.1 %shard_map.74 = f32[48,512]{1,0:T(8,128)} custom-call(s32[1]{0:T(128)S(6)} %copy.14.len_ref, bf16[192,128]{1,0:T(8,128)(2,1)S(1)} %bitcast.23, bf16[16,2,128,128]{3,2,1,0:T(8,128)(2,1)S(1)} %all-to-all-done.kv_ref, bf16[48,128]{1,0:T(8,128)(2,1)S(1)} %get-tuple-element.11.dk_ref, bf16[48,128]{1,0:T(8,128)(2,1)S(1)} %get-tuple-element.12.dvt_ref, ...), custom_call_target="tpu_custom_call" | custom-call | tf_op jit(solution)/shard_map/pallas_call | solution.py:113
  101.2 3.3 %collective-permute-start.3 = (f32[48,512]{1,0:T(8,128)}, f32[48,512]{1,0:T(8,128)S(1)}, u32[]{:S(2)}, u32[]{:S(2)}) collective-permute-start(f32[48,512]{1,0:T(8,128)} %shard_map.74), channel_id=1, source_target_pairs={{0,1},{1,0},{2,3},{3,2},{4,5},{5,4},{6,7},{7,6},{8,9},{9,8},{10,11... | collective-permute-start | bytes 294920 | tf_op jit(solution)/shard_map/ppermute | solution.py:185
  104.7 1.5 %shard_map.75 = f32[2,48,512]{2,1,0:T(8,128)S(1)} fusion(f32[2,48,512]{2,1,0:T(8,128)S(1)} %broadcast_in_dim.11, s32[]{:T(128)S(6)} %select_n.42, s32[1]{0:T(128)S(6)} %copy.14.len_ref, bf16[192,128]{1,0:T(8,128)(2,1)S(1)} %bitcast.24, bf16[16,2,128,128]{3,2,1,0:T(8,128)(2,1)S(1)} %all-to-all-done.kv_ref, bf16[48,128]{1,0:T(8,128)(2,1)S(1)} %get-tuple-element.11.dk_ref, ...), kind=kCustom, calls=%fused_computation.1 | custom fusion | bytes 1269768 | tf_op jit(solution)/shard_map/pallas_call | solution.py:113
  106.2 0.0 copy-start
  106.2 1.8 %collective-permute-done.3 = f32[48,512]{1,0:T(8,128)S(1)} collective-permute-done((f32[48,512]{1,0:T(8,128)}, f32[48,512]{1,0:T(8,128)S(1)}, u32[]{:S(2)}, u32[]{:S(2)}) %collective-permute-start.3) | collective-permute-done | bytes 98336 | tf_op jit(solution)/shard_map/ppermute | solution.py:185
  108.0 0.6 bitcast_dynamic-update-slice_fusion
  (17 shorter events, 0.2 us)
Async XLA Ops:
  33.2 22.0 %copy-start.1 = (bf16[2,48,512]{2,1,0:T(8,128)(2,1)S(1)}, bf16[2,48,512]{2,1,0:T(8,128)(2,1)}, u32[]{:S(2)}) copy-start(bf16[2,48,512]{2,1,0:T(8,128)(2,1)} %param.7) | copy-start | bytes 294916
  33.2 65.9 %all-to-all-start = ((bf16[16,2,128,128]{3,2,1,0:T(8,128)(2,1)}), bf16[16,2,128,128]{3,2,1,0:T(8,128)(2,1)S(1)}, u32[]{:S(2)}, u32[]{:S(2)}) async-start(bf16[16,2,128,128]{3,2,1,0:T(8,128)(2,1)} %shard_map.73), calls=%async_computation | async-start | bytes 2097152 | tf_op jit(solution)/shard_map/all_to_all | solution.py:173
  48.5 0.7 copy-start.3
  48.5 4.6 %copy-start.4 = (bf16[2,48,64]{2,1,0:T(8,128)(2,1)S(1)}, bf16[2,48,64]{2,1,0:T(8,128)(2,1)}, u32[]{:S(2)}) copy-start(bf16[2,48,64]{2,1,0:T(8,128)(2,1)} %param.11) | copy-start | bytes 36868
  49.3 47.5 %collective-permute-start = (bf16[48,64]{1,0:T(8,128)(2,1)S(1)}, bf16[48,64]{1,0:T(8,128)(2,1)S(1)}, u32[]{:S(2)}, u32[]{:S(2)}) collective-permute-start(bf16[48,64]{1,0:T(8,128)(2,1)S(1)} %dynamic-slice_bitcast_fusion.2), channel_id=1, source_target_pairs={{0,1},{1,0},{2,3},{3,2},{4,5},{5,4},{6,7},{7,6},{8,9},{9,8},{10,11... | collective-permute-start | bytes 18440 | tf_op jit(solution)/shard_map/ppermute | solution.py:165
  53.1 43.8 %collective-permute-start.1 = (bf16[48,64]{1,0:T(8,128)(2,1)S(1)}, bf16[48,64]{1,0:T(8,128)(2,1)S(1)}, u32[]{:S(2)}, u32[]{:S(2)}) collective-permute-start(bf16[48,64]{1,0:T(8,128)(2,1)S(1)} %dynamic-slice_bitcast_fusion.1), channel_id=1, source_target_pairs={{0,1},{1,0},{2,3},{3,2},{4,5},{5,4},{6,7},{7,6},{8,9},{9,8},{10,11... | collective-permute-start | bytes 18440 | tf_op jit(solution)/shard_map/ppermute | solution.py:165
  55.2 3.9 %copy-start.2 = (s32[2,24,24]{2,1,0:T(8,128)S(1)}, s32[2,24,24]{2,1,0:T(8,128)}, u32[]{:S(2)}) copy-start(s32[2,24,24]{2,1,0:T(8,128)} %param.12) | copy-start | bytes 13828
  55.2 42.2 %collective-permute-start.2 = (bf16[48,512]{1,0:T(8,128)(2,1)S(1)}, bf16[48,512]{1,0:T(8,128)(2,1)S(1)}, u32[]{:S(2)}, u32[]{:S(2)}) collective-permute-start(bf16[48,512]{1,0:T(8,128)(2,1)S(1)} %get-tuple-element.5), channel_id=1, source_target_pairs={{0,1},{1,0},{2,3},{3,2},{4,5},{5,4},{6,7},{7,6},{8,9},{9,8},{10,11... | collective-permute-start | bytes 147464 | tf_op jit(solution)/shard_map/ppermute | solution.py:165
  101.2 6.7 %collective-permute-start.3 = (f32[48,512]{1,0:T(8,128)}, f32[48,512]{1,0:T(8,128)S(1)}, u32[]{:S(2)}, u32[]{:S(2)}) collective-permute-start(f32[48,512]{1,0:T(8,128)} %shard_map.74), channel_id=1, source_target_pairs={{0,1},{1,0},{2,3},{3,2},{4,5},{5,4},{6,7},{7,6},{8,9},{9,8},{10,11... | collective-permute-start | bytes 294920 | tf_op jit(solution)/shard_map/ppermute | solution.py:185
  106.2 1.8 %copy-start = (f32[2,48,512]{2,1,0:T(8,128)}, f32[2,48,512]{2,1,0:T(8,128)S(1)}, u32[]{:S(2)}) copy-start(f32[2,48,512]{2,1,0:T(8,128)S(1)} %shard_map.75) | copy-start | bytes 589828

commit v14 on v13

--- a/solution.py
+++ b/solution.py
@@ -119,31 +119,23 @@
     )(context_length, *operands)
 
 
-def pack_kernel(k_ref, v_ref, o_ref, sem):
+def pack_kernel(k_ref, v_ref, o_ref):
     layers, _, width = k_ref.shape
-    copies = []
     for k in range(width // DH):
         for l in range(layers):
-            for c, src in enumerate((k_ref, v_ref)):
-                copy = pltpu.make_async_copy(
-                    src.at[l, :, pl.ds(k * DH, DH)], o_ref.at[k * layers + l, c], sem.at[len(copies)]
-                )
-                copy.start()
-                copies.append(copy)
-    for copy in copies:
-        copy.wait()
+            o_ref[k * layers + l, 0] = k_ref[l, :, k * DH:(k + 1) * DH]
+            o_ref[k * layers + l, 1] = v_ref[l, :, k * DH:(k + 1) * DH]
 
 
 def pack(key_cache, value_cache):
     layers, local_len, width = key_cache.shape
     n = layers * (width // DH)
-    anywhere = pl.BlockSpec(memory_space=pl.ANY)
+    vmem = pl.BlockSpec(memory_space=pltpu.VMEM)
     return pl.pallas_call(
         pack_kernel,
         out_shape=jax.ShapeDtypeStruct((n, 2, local_len, DH), key_cache.dtype),
-        in_specs=[anywhere, anywhere],
-        out_specs=anywhere,
-        scratch_shapes=[pltpu.SemaphoreType.DMA((2 * n,))],
+        in_specs=[vmem, vmem],
+        out_specs=vmem,
     )(key_cache, value_cache)
 
 

time: 109 us -> 78.2 us (0.72)
  Pallas kernels: 35.3 us -> 4.52 us
    pallas_call x1, Pallas kernels: 33.1 us -> 2.37 us  [pack(): pl.pallas_call(pack_kernel, out_shape=jax.ShapeDtypeStruct((n, 2, local_l...]
  transfers between devices with their start and end apart: 5 -> 5, of which waited for: 5 -> 5; matrix products, arithmetic and copies ran while one was open for 2% -> 3% of each run, Pallas kernels for 0% -> 0%
where the time goes in v14:
time: 78.2 us; the launch traced here: 77.8 us
  waiting for transfers between devices  40.6 us (52%)
  starting transfers between devices  28.3 us (36%)
  Pallas kernels  4.52 us (6%)
  local copies, waits for them, and re-layouts  3.3 us (4%)
  between operations  0.84 us (1%)
    ppermute x3, waiting for transfers between devices, body(): lax.ppermute(lax.dynamic_index_in_dim(a, other, 0, keepdims=False), 'ctx'...  37.2 us
    all_to_all x1, starting transfers between devices, body(): blocks = lax.all_to_all(kv, 'ctx', 0, 0, tiled=True)  15.3 us
    ppermute x3, starting transfers between devices, body(): lax.ppermute(lax.dynamic_index_in_dim(a, other, 0, keepdims=False), 'ctx'...  9.66 us
    ppermute x1, starting transfers between devices, body(): got = lax.ppermute(give, 'ctx', swap)  3.34 us
    pallas_call x1, Pallas kernels, pack(): pl.pallas_call(pack_kernel, out_shape=jax.ShapeDtypeStruct((n, 2, local_l...  2.37 us
    pallas_call x1, Pallas kernels, attend(): pl.pallas_call(attend_kernel, out_shape=jax.ShapeDtypeStruct((rows // hea...  2.15 us
    ppermute x1, waiting for transfers between devices, body(): got = lax.ppermute(give, 'ctx', swap)  1.76 us
    all_to_all x1, waiting for transfers between devices, body(): blocks = lax.all_to_all(kv, 'ctx', 0, 0, tiled=True)  1.64 us
  transfers between devices with their start and end apart: 5, of which 5 were waited for; matrix products, arithmetic and copies ran while one was open for 3% of the time, Pallas kernels for 0%

profile of v14, /device:TPU:6, one launch (start us, length us, event | category | flops | bytes accessed | tf_op | source)
XLA Modules:
  0.0 77.8 jit_solution(3587141467795900971)
XLA Ops:
  0.0 2.4 %shard_map.73 = bf16[16,2,128,128]{3,2,1,0:T(8,128)(2,1)} custom-call(bf16[2,128,1024]{2,1,0:T(8,128)(2,1)} %k_ref.1, bf16[2,128,1024]{2,1,0:T(8,128)(2,1)} %v_ref.1), custom_call_target="tpu_custom_call" | custom-call | tf_op jit(solution)/shard_map/pallas_call | solution.py:134
  2.4 15.3 %all-to-all-start = ((bf16[16,2,128,128]{3,2,1,0:T(8,128)(2,1)}), bf16[16,2,128,128]{3,2,1,0:T(8,128)(2,1)S(1)}, u32[]{:S(2)}, u32[]{:S(2)}) async-start(bf16[16,2,128,128]{3,2,1,0:T(8,128)(2,1)} %shard_map.73), calls=%async_computation | async-start | bytes 2097152 | tf_op jit(solution)/shard_map/all_to_all | solution.py:165
  17.7 0.0 copy-start.3
  17.7 0.0 copy-start.4
  17.7 0.7 copy-done.3
  18.4 3.8 %collective-permute-start = (bf16[48,64]{1,0:T(8,128)(2,1)S(1)}, bf16[48,64]{1,0:T(8,128)(2,1)S(1)}, u32[]{:S(2)}, u32[]{:S(2)}) collective-permute-start(bf16[48,64]{1,0:T(8,128)(2,1)S(1)} %dynamic-slice_bitcast_fusion.2), channel_id=1, source_target_pairs={{0,1},{1,0},{2,3},{3,2},{4,5},{5,4},{6,7},{7,6},{8,9},{9,8},{10,11... | collective-permute-start | bytes 18440 | tf_op jit(solution)/shard_map/ppermute | solution.py:157
  22.3 2.0 %collective-permute-start.1 = (bf16[48,64]{1,0:T(8,128)(2,1)S(1)}, bf16[48,64]{1,0:T(8,128)(2,1)S(1)}, u32[]{:S(2)}, u32[]{:S(2)}) collective-permute-start(bf16[48,64]{1,0:T(8,128)(2,1)S(1)} %dynamic-slice_bitcast_fusion.1), channel_id=1, source_target_pairs={{0,1},{1,0},{2,3},{3,2},{4,5},{5,4},{6,7},{7,6},{8,9},{9,8},{10,11... | collective-permute-start | bytes 18440 | tf_op jit(solution)/shard_map/ppermute | solution.py:157
  24.3 0.0 copy-start.2
  24.4 3.8 %collective-permute-start.2 = (bf16[48,512]{1,0:T(8,128)(2,1)S(1)}, bf16[48,512]{1,0:T(8,128)(2,1)S(1)}, u32[]{:S(2)}, u32[]{:S(2)}) collective-permute-start(bf16[48,512]{1,0:T(8,128)(2,1)S(1)} %get-tuple-element.5), channel_id=1, source_target_pairs={{0,1},{1,0},{2,3},{3,2},{4,5},{5,4},{6,7},{7,6},{8,9},{9,8},{10,11... | collective-permute-start | bytes 147464 | tf_op jit(solution)/shard_map/ppermute | solution.py:157
  28.2 0.1 copy.10
  28.3 0.1 broadcast_multiply_fusion
  28.4 0.1 mul.20
  28.5 0.1 tile.10.tree_ref
  29.3 36.6 %collective-permute-done = bf16[48,64]{1,0:T(8,128)(2,1)S(1)} collective-permute-done((bf16[48,64]{1,0:T(8,128)(2,1)S(1)}, bf16[48,64]{1,0:T(8,128)(2,1)S(1)}, u32[]{:S(2)}, u32[]{:S(2)}) %collective-permute-start) | collective-permute-done | bytes 6176 | tf_op jit(solution)/shard_map/ppermute | solution.py:157
  65.9 0.2 collective-permute-done.1
  66.1 0.1 pad_maximum_fusion
  66.2 0.4 collective-permute-done.2
  66.7 1.6 %all-to-all-done.kv_ref = bf16[16,2,128,128]{3,2,1,0:T(8,128)(2,1)S(1)} async-done(((bf16[16,2,128,128]{3,2,1,0:T(8,128)(2,1)}), bf16[16,2,128,128]{3,2,1,0:T(8,128)(2,1)S(1)}, u32[]{:S(2)}, u32[]{:S(2)}) %all-to-all-start) | async-done | bytes 1048608 | tf_op jit(solution)/shard_map/all_to_all | solution.py:165
  68.3 2.1 %shard_map.74 = f32[48,512]{1,0:T(8,128)} custom-call(s32[1]{0:T(128)S(6)} %copy.14.len_ref, bf16[192,128]{1,0:T(8,128)(2,1)S(1)} %bitcast.23, bf16[16,2,128,128]{3,2,1,0:T(8,128)(2,1)S(1)} %all-to-all-done.kv_ref, bf16[48,128]{1,0:T(8,128)(2,1)S(1)} %get-tuple-element.11.dk_ref, bf16[48,128]{1,0:T(8,128)(2,1)S(1)} %get-tuple-element.12.dvt_ref, ...), custom_call_target="tpu_custom_call" | custom-call | tf_op jit(solution)/shard_map/pallas_call | solution.py:113
  70.4 3.3 %collective-permute-start.3 = (f32[48,512]{1,0:T(8,128)}, f32[48,512]{1,0:T(8,128)S(1)}, u32[]{:S(2)}, u32[]{:S(2)}) collective-permute-start(f32[48,512]{1,0:T(8,128)} %shard_map.74), channel_id=1, source_target_pairs={{0,1},{1,0},{2,3},{3,2},{4,5},{5,4},{6,7},{7,6},{8,9},{9,8},{10,11... | collective-permute-start | bytes 294920 | tf_op jit(solution)/shard_map/ppermute | solution.py:177
  73.9 1.5 %shard_map.75 = f32[2,48,512]{2,1,0:T(8,128)S(1)} fusion(f32[2,48,512]{2,1,0:T(8,128)S(1)} %broadcast_in_dim.11, s32[]{:T(128)S(6)} %select_n.42, s32[1]{0:T(128)S(6)} %copy.14.len_ref, bf16[192,128]{1,0:T(8,128)(2,1)S(1)} %bitcast.24, bf16[16,2,128,128]{3,2,1,0:T(8,128)(2,1)S(1)} %all-to-all-done.kv_ref, bf16[48,128]{1,0:T(8,128)(2,1)S(1)} %get-tuple-element.11.dk_ref, ...), kind=kCustom, calls=%fused_computation.1 | custom fusion | bytes 1269768 | tf_op jit(solution)/shard_map/pallas_call | solution.py:113
  75.4 0.0 copy-start
  75.4 1.8 %collective-permute-done.3 = f32[48,512]{1,0:T(8,128)S(1)} collective-permute-done((f32[48,512]{1,0:T(8,128)}, f32[48,512]{1,0:T(8,128)S(1)}, u32[]{:S(2)}, u32[]{:S(2)}) %collective-permute-start.3) | collective-permute-done | bytes 98336 | tf_op jit(solution)/shard_map/ppermute | solution.py:177
  77.2 0.6 bitcast_dynamic-update-slice_fusion
  (17 shorter events, 0.2 us)
Async XLA Ops:
  2.4 22.0 %copy-start.1 = (bf16[2,48,512]{2,1,0:T(8,128)(2,1)S(1)}, bf16[2,48,512]{2,1,0:T(8,128)(2,1)}, u32[]{:S(2)}) copy-start(bf16[2,48,512]{2,1,0:T(8,128)(2,1)} %param.7) | copy-start | bytes 294916
  2.4 65.9 %all-to-all-start = ((bf16[16,2,128,128]{3,2,1,0:T(8,128)(2,1)}), bf16[16,2,128,128]{3,2,1,0:T(8,128)(2,1)S(1)}, u32[]{:S(2)}, u32[]{:S(2)}) async-start(bf16[16,2,128,128]{3,2,1,0:T(8,128)(2,1)} %shard_map.73), calls=%async_computation | async-start | bytes 2097152 | tf_op jit(solution)/shard_map/all_to_all | solution.py:165
  17.7 0.7 copy-start.3
  17.7 4.6 %copy-start.4 = (bf16[2,48,64]{2,1,0:T(8,128)(2,1)S(1)}, bf16[2,48,64]{2,1,0:T(8,128)(2,1)}, u32[]{:S(2)}) copy-start(bf16[2,48,64]{2,1,0:T(8,128)(2,1)} %param.11) | copy-start | bytes 36868
  18.4 47.5 %collective-permute-start = (bf16[48,64]{1,0:T(8,128)(2,1)S(1)}, bf16[48,64]{1,0:T(8,128)(2,1)S(1)}, u32[]{:S(2)}, u32[]{:S(2)}) collective-permute-start(bf16[48,64]{1,0:T(8,128)(2,1)S(1)} %dynamic-slice_bitcast_fusion.2), channel_id=1, source_target_pairs={{0,1},{1,0},{2,3},{3,2},{4,5},{5,4},{6,7},{7,6},{8,9},{9,8},{10,11... | collective-permute-start | bytes 18440 | tf_op jit(solution)/shard_map/ppermute | solution.py:157
  22.3 43.8 %collective-permute-start.1 = (bf16[48,64]{1,0:T(8,128)(2,1)S(1)}, bf16[48,64]{1,0:T(8,128)(2,1)S(1)}, u32[]{:S(2)}, u32[]{:S(2)}) collective-permute-start(bf16[48,64]{1,0:T(8,128)(2,1)S(1)} %dynamic-slice_bitcast_fusion.1), channel_id=1, source_target_pairs={{0,1},{1,0},{2,3},{3,2},{4,5},{5,4},{6,7},{7,6},{8,9},{9,8},{10,11... | collective-permute-start | bytes 18440 | tf_op jit(solution)/shard_map/ppermute | solution.py:157
  24.3 3.9 %copy-start.2 = (s32[2,24,24]{2,1,0:T(8,128)S(1)}, s32[2,24,24]{2,1,0:T(8,128)}, u32[]{:S(2)}) copy-start(s32[2,24,24]{2,1,0:T(8,128)} %param.12) | copy-start | bytes 13828
  24.4 42.2 %collective-permute-start.2 = (bf16[48,512]{1,0:T(8,128)(2,1)S(1)}, bf16[48,512]{1,0:T(8,128)(2,1)S(1)}, u32[]{:S(2)}, u32[]{:S(2)}) collective-permute-start(bf16[48,512]{1,0:T(8,128)(2,1)S(1)} %get-tuple-element.5), channel_id=1, source_target_pairs={{0,1},{1,0},{2,3},{3,2},{4,5},{5,4},{6,7},{7,6},{8,9},{9,8},{10,11... | collective-permute-start | bytes 147464 | tf_op jit(solution)/shard_map/ppermute | solution.py:157
  70.4 6.7 %collective-permute-start.3 = (f32[48,512]{1,0:T(8,128)}, f32[48,512]{1,0:T(8,128)S(1)}, u32[]{:S(2)}, u32[]{:S(2)}) collective-permute-start(f32[48,512]{1,0:T(8,128)} %shard_map.74), channel_id=1, source_target_pairs={{0,1},{1,0},{2,3},{3,2},{4,5},{5,4},{6,7},{7,6},{8,9},{9,8},{10,11... | collective-permute-start | bytes 294920 | tf_op jit(solution)/shard_map/ppermute | solution.py:177
  75.4 1.8 %copy-start = (f32[2,48,512]{2,1,0:T(8,128)}, f32[2,48,512]{2,1,0:T(8,128)S(1)}, u32[]{:S(2)}) copy-start(f32[2,48,512]{2,1,0:T(8,128)S(1)} %shard_map.75) | copy-start | bytes 589828

commit v15 on v12

--- a/solution.py
+++ b/solution.py
@@ -62,7 +62,7 @@
     return lax.dot_general(a, b, dims, preferred_element_type=jnp.float32)
 
 
-def attend_kernel(len_ref, q_ref, kv_ref, dk_ref, dvt_ref, tree_ref, o_ref, out_sc, lse_sc):
+def attend_kernel(len_ref, q_ref, kv_ref, dk_ref, dvt_ref, tree_ref, give_ref, keep_ref, out_sc, lse_sc):
     blocks, _, block_len, _ = kv_ref.shape
     score_scale = 1.0 / math.sqrt(DH)
     nt = (((1,), (1,)), ((), ()))
@@ -99,9 +99,11 @@
     for j in range(1, blocks):
         weighted = weighted + factor[j:j + 1] * out_sc[j]
     final = jnp.transpose(weighted / jnp.sum(factor, axis=0, keepdims=True))
-    rows = o_ref.shape[0]
-    for i in range(o_ref.shape[1] // DH):
-        o_ref[:, i * DH:(i + 1) * DH] = final[i * rows:(i + 1) * rows, :]
+    rows = give_ref.shape[0]
+    heads = give_ref.shape[1] // DH
+    for h, o_ref in enumerate((give_ref, keep_ref)):
+        for i in range(heads):
+            o_ref[:, i * DH:(i + 1) * DH] = final[(h * heads + i) * rows:(h * heads + i + 1) * rows, :]
 
 
 def attend(context_length, q_rows, blocks_kv, draft_k, draft_vt, tree_cols, heads):
@@ -112,9 +114,9 @@
                 for a in (q_rows, blocks_kv, draft_k, draft_vt, tree_cols)]
     return pl.pallas_call(
         attend_kernel,
-        out_shape=jax.ShapeDtypeStruct((rows // heads, heads * DH), jnp.float32),
+        out_shape=[jax.ShapeDtypeStruct((rows // heads, heads * DH // 2), jnp.float32)] * 2,
         in_specs=[pl.BlockSpec(memory_space=pltpu.SMEM)] + [vmem] * 5,
-        out_specs=vmem,
+        out_specs=[vmem, vmem],
         scratch_shapes=[pltpu.VMEM((blocks, DH, rows), jnp.float32), pltpu.VMEM((blocks, rows), jnp.float32)],
     )(context_length, *operands)
 
@@ -154,11 +156,9 @@
     draft_k = jnp.concatenate([first[1], second[1]], 1)
     draft_vt = jnp.concatenate([first[2], second[2]], 1)
     tree_cols = jnp.tile(jnp.transpose(tree_keep), (1, heads_here))
-    give = attend(context_length, other_q.reshape(heads_here * rows, DH), blocks, draft_k, draft_vt, tree_cols,
-                  heads_here)
+    both_q = jnp.concatenate([other_q, own_q], 0).reshape(2 * heads_here * rows, DH)
+    give, keep = attend(context_length, both_q, blocks, draft_k, draft_vt, jnp.tile(tree_cols, (1, 2)), 2 * heads_here)
     got = lax.ppermute(give, "ctx", swap)
-    keep = attend(context_length, own_q.reshape(heads_here * rows, DH), blocks, draft_k, draft_vt, tree_cols,
-                  heads_here)
     keep = keep[None]
     got = got[None]
     result = jnp.zeros((layers, rows, heads_here * DH), jnp.float32)

time: 78.3 us -> 78.1 us (level)
  Pallas kernels: 2.16 us -> 0 us
  waiting for transfers between devices: 40.6 us -> 41.7 us
    pallas_call x1 -> x0, Pallas kernels: 2.16 us -> none  [attend(): pl.pallas_call(attend_kernel, out_shape=jax.ShapeDtypeStruct((rows // hea...]
    ppermute x1, waiting for transfers between devices: 1.76 us -> 3.15 us  [body(): got = lax.ppermute(give, 'ctx', swap)]
  transfers between devices with their start and end apart: 5 -> 5, of which waited for: 5 -> 5; matrix products, arithmetic and copies ran while one was open for 3% -> 1% of each run, Pallas kernels for 0% -> 0%
where the time goes in v15:
time: 78.1 us; the launch traced here: 77.6 us
  waiting for transfers between devices  41.7 us (53%)
  starting transfers between devices  28.3 us (36%)
  local copies, waits for them, and re-layouts  5.31 us (7%)
  other arithmetic  1.33 us (2%)
  between operations  0.88 us (1%)
    ppermute x3, waiting for transfers between devices, body(): lax.ppermute(lax.dynamic_index_in_dim(a, other, 0, keepdims=False), 'ctx'...  37 us
    all_to_all x1, starting transfers between devices, body(): blocks = lax.all_to_all(kv, 'ctx', 0, 0, tiled=True)  15.3 us
    ppermute x3, starting transfers between devices, body(): lax.ppermute(lax.dynamic_index_in_dim(a, other, 0, keepdims=False), 'ctx'...  9.66 us
    ppermute x1, starting transfers between devices, body(): got = lax.ppermute(give, 'ctx', swap)  3.36 us
    ppermute x1, waiting for transfers between devices, body(): got = lax.ppermute(give, 'ctx', swap)  3.15 us
    pallas_call x1, local copies, waits for them, and re-layouts, attend(): pl.pallas_call(attend_kernel, out_shape=[jax.ShapeDtypeStruct((rows // he...  2.08 us
    unnamed x15, local copies, waits for them, and re-layouts  1.87 us
    all_to_all x1, waiting for transfers between devices, body(): blocks = lax.all_to_all(kv, 'ctx', 0, 0, tiled=True)  1.57 us
  transfers between devices with their start and end apart: 5, of which 5 were waited for; matrix products, arithmetic and copies ran while one was open for 1% of the time, Pallas kernels for 0%

profile of v15, /device:TPU:6, one launch (start us, length us, event | category | flops | bytes accessed | tf_op | source)
XLA Modules:
  0.0 77.6 jit_solution(6936260873195306774)
XLA Ops:
  0.0 1.0 %copy-done = bf16[2,128,1024]{2,1,0:T(8,128)(2,1)S(1)} copy-done((bf16[2,128,1024]{2,1,0:T(8,128)(2,1)S(1)}, bf16[2,128,1024]{2,1,0:T(8,128)(2,1)}, u32[]{:S(2)}) %copy-start) | copy-done | bytes 524312
  1.0 0.1 copy_bitcast_fusion.1
  1.2 0.1 copy_bitcast_fusion
  1.3 1.1 %pad_maximum_fusion = bf16[16,2,128,128]{3,2,1,0:T(8,128)(2,1)} fusion(bf16[16,1,128,128]{3,2,1,0:T(8,128)(2,1)S(1)} %bitcast.39, bf16[16,1,128,128]{3,2,1,0:T(8,128)(2,1)S(1)} %bitcast.38), kind=kLoop, calls=%fused_computation | loop fusion | flops 524288 | bytes 2097152 | tf_op jit(solution)/shard_map/stack | solution.py:148
  2.4 15.3 %all-to-all-start = ((bf16[16,2,128,128]{3,2,1,0:T(8,128)(2,1)}), bf16[16,2,128,128]{3,2,1,0:T(8,128)(2,1)S(1)}, u32[]{:S(2)}, u32[]{:S(2)}) async-start(bf16[16,2,128,128]{3,2,1,0:T(8,128)(2,1)} %pad_maximum_fusion), calls=%async_computation | async-start | bytes 2097152 | tf_op jit(solution)/shard_map/all_to_all | solution.py:149
  17.8 0.7 copy-done.5
  18.5 3.8 %collective-permute-start.2 = (bf16[48,64]{1,0:T(8,128)(2,1)S(1)}, bf16[48,64]{1,0:T(8,128)(2,1)S(1)}, u32[]{:S(2)}, u32[]{:S(2)}) collective-permute-start(bf16[48,64]{1,0:T(8,128)(2,1)S(1)} %dynamic-slice_bitcast_fusion.1), channel_id=1, source_target_pairs={{0,1},{1,0},{2,3},{3,2},{4,5},{5,4},{6,7},{7,6},{8,9},{9,8},{10,11... | collective-permute-start | bytes 18440 | tf_op jit(solution)/shard_map/ppermute | solution.py:139
  22.4 2.0 %collective-permute-start.1 = (bf16[48,64]{1,0:T(8,128)(2,1)S(1)}, bf16[48,64]{1,0:T(8,128)(2,1)S(1)}, u32[]{:S(2)}, u32[]{:S(2)}) collective-permute-start(bf16[48,64]{1,0:T(8,128)(2,1)S(1)} %dynamic-slice_bitcast_fusion.2), channel_id=1, source_target_pairs={{0,1},{1,0},{2,3},{3,2},{4,5},{5,4},{6,7},{7,6},{8,9},{9,8},{10,11... | collective-permute-start | bytes 18440 | tf_op jit(solution)/shard_map/ppermute | solution.py:139
  24.4 3.8 %collective-permute-start = (bf16[48,512]{1,0:T(8,128)(2,1)S(1)}, bf16[48,512]{1,0:T(8,128)(2,1)S(1)}, u32[]{:S(2)}, u32[]{:S(2)}) collective-permute-start(bf16[48,512]{1,0:T(8,128)(2,1)S(1)} %get-tuple-element.13), channel_id=1, source_target_pairs={{0,1},{1,0},{2,3},{3,2},{4,5},{5,4},{6,7},{7,6},{8,9},{9,8},{10,11... | collective-permute-start | bytes 147464 | tf_op jit(solution)/shard_map/ppermute | solution.py:139
  28.3 0.1 copy.14
  28.4 0.1 broadcast_multiply_fusion
  28.5 0.1 mul.20
  28.6 0.1 tile.17
  28.8 0.1 tile.19
  29.5 36.4 %collective-permute-done.2 = bf16[48,64]{1,0:T(8,128)(2,1)S(1)} collective-permute-done((bf16[48,64]{1,0:T(8,128)(2,1)S(1)}, bf16[48,64]{1,0:T(8,128)(2,1)S(1)}, u32[]{:S(2)}, u32[]{:S(2)}) %collective-permute-start.2) | collective-permute-done | bytes 6176 | tf_op jit(solution)/shard_map/ppermute | solution.py:139
  66.0 0.2 collective-permute-done.1
  66.1 0.1 pad_maximum_fusion.2
  66.2 0.4 collective-permute-done
  66.7 0.1 pad_maximum_fusion.1
  66.8 1.6 %all-to-all-done = bf16[16,2,128,128]{3,2,1,0:T(8,128)(2,1)S(1)} async-done(((bf16[16,2,128,128]{3,2,1,0:T(8,128)(2,1)}), bf16[16,2,128,128]{3,2,1,0:T(8,128)(2,1)S(1)}, u32[]{:S(2)}, u32[]{:S(2)}) %all-to-all-start) | async-done | bytes 1048608 | tf_op jit(solution)/shard_map/all_to_all | solution.py:149
  68.4 2.1 %shard_map.73 = (f32[2,48,512]{2,1,0:T(8,128)S(1)}, f32[48,512]{1,0:T(8,128)S(1)}) fusion(f32[2,48,512]{2,1,0:T(8,128)S(1)} %broadcast_in_dim.11, s32[]{:T(128)S(6)} %select_n.43, s32[1]{0:T(128)S(6)} %copy.21, bf16[384,128]{1,0:T(8,128)(2,1)S(1)} %bitcast.40, bf16[16,2,128,128]{3,2,1,0:T(8,128)(2,1)S(1)} %all-to-all-done, ...), kind=kCustom, calls=%fused_computation.5 | custom fusion | bytes 1441800 | tf_op jit(solution)/shard_map/pallas_call | solution.py:115
  70.5 3.4 %collective-permute-start.3 = (f32[48,512]{1,0:T(8,128)S(1)}, f32[48,512]{1,0:T(8,128)S(1)}, u32[]{:S(2)}, u32[]{:S(2)}) collective-permute-start(f32[48,512]{1,0:T(8,128)S(1)} %get-tuple-element.12), channel_id=1, source_target_pairs={{0,1},{1,0},{2,3},{3,2},{4,5},{5,4},{6,7},{7,6},{8,9},{9,8},{10,11... | collective-permute-start | bytes 294920 | tf_op jit(solution)/shard_map/ppermute | solution.py:161
  73.8 3.1 %collective-permute-done.3 = f32[48,512]{1,0:T(8,128)S(1)} collective-permute-done((f32[48,512]{1,0:T(8,128)S(1)}, f32[48,512]{1,0:T(8,128)S(1)}, u32[]{:S(2)}, u32[]{:S(2)}) %collective-permute-start.3) | collective-permute-done | bytes 98336 | tf_op jit(solution)/shard_map/ppermute | solution.py:161
  77.0 0.6 bitcast_dynamic-update-slice_fusion
  (24 shorter events, 0.2 us)
Async XLA Ops:
  0.0 1.0 %copy-start = (bf16[2,128,1024]{2,1,0:T(8,128)(2,1)S(1)}, bf16[2,128,1024]{2,1,0:T(8,128)(2,1)}, u32[]{:S(2)}) copy-start(bf16[2,128,1024]{2,1,0:T(8,128)(2,1)} %param.8) | copy-start | bytes 1572868
  0.0 1.2 %copy-start.1 = (bf16[2,128,1024]{2,1,0:T(8,128)(2,1)S(1)}, bf16[2,128,1024]{2,1,0:T(8,128)(2,1)}, u32[]{:S(2)}) copy-start(bf16[2,128,1024]{2,1,0:T(8,128)(2,1)} %param.9) | copy-start | bytes 1572868
  2.4 22.0 %copy-start.3 = (bf16[2,48,512]{2,1,0:T(8,128)(2,1)S(1)}, bf16[2,48,512]{2,1,0:T(8,128)(2,1)}, u32[]{:S(2)}) copy-start(bf16[2,48,512]{2,1,0:T(8,128)(2,1)} %param.7) | copy-start | bytes 294916
  2.4 65.9 %all-to-all-start = ((bf16[16,2,128,128]{3,2,1,0:T(8,128)(2,1)}), bf16[16,2,128,128]{3,2,1,0:T(8,128)(2,1)S(1)}, u32[]{:S(2)}, u32[]{:S(2)}) async-start(bf16[16,2,128,128]{3,2,1,0:T(8,128)(2,1)} %pad_maximum_fusion), calls=%async_computation | async-start | bytes 2097152 | tf_op jit(solution)/shard_map/all_to_all | solution.py:149
  17.8 0.7 copy-start.5
  17.8 4.6 %copy-start.6 = (bf16[2,48,64]{2,1,0:T(8,128)(2,1)S(1)}, bf16[2,48,64]{2,1,0:T(8,128)(2,1)}, u32[]{:S(2)}) copy-start(bf16[2,48,64]{2,1,0:T(8,128)(2,1)} %param.10) | copy-start | bytes 36868
  18.5 47.5 %collective-permute-start.2 = (bf16[48,64]{1,0:T(8,128)(2,1)S(1)}, bf16[48,64]{1,0:T(8,128)(2,1)S(1)}, u32[]{:S(2)}, u32[]{:S(2)}) collective-permute-start(bf16[48,64]{1,0:T(8,128)(2,1)S(1)} %dynamic-slice_bitcast_fusion.1), channel_id=1, source_target_pairs={{0,1},{1,0},{2,3},{3,2},{4,5},{5,4},{6,7},{7,6},{8,9},{9,8},{10,11... | collective-permute-start | bytes 18440 | tf_op jit(solution)/shard_map/ppermute | solution.py:139
  22.4 43.8 %collective-permute-start.1 = (bf16[48,64]{1,0:T(8,128)(2,1)S(1)}, bf16[48,64]{1,0:T(8,128)(2,1)S(1)}, u32[]{:S(2)}, u32[]{:S(2)}) collective-permute-start(bf16[48,64]{1,0:T(8,128)(2,1)S(1)} %dynamic-slice_bitcast_fusion.2), channel_id=1, source_target_pairs={{0,1},{1,0},{2,3},{3,2},{4,5},{5,4},{6,7},{7,6},{8,9},{9,8},{10,11... | collective-permute-start | bytes 18440 | tf_op jit(solution)/shard_map/ppermute | solution.py:139
  24.4 3.9 %copy-start.4 = (s32[2,24,24]{2,1,0:T(8,128)S(1)}, s32[2,24,24]{2,1,0:T(8,128)}, u32[]{:S(2)}) copy-start(s32[2,24,24]{2,1,0:T(8,128)} %param.12) | copy-start | bytes 13828
  24.4 42.2 %collective-permute-start = (bf16[48,512]{1,0:T(8,128)(2,1)S(1)}, bf16[48,512]{1,0:T(8,128)(2,1)S(1)}, u32[]{:S(2)}, u32[]{:S(2)}) collective-permute-start(bf16[48,512]{1,0:T(8,128)(2,1)S(1)} %get-tuple-element.13), channel_id=1, source_target_pairs={{0,1},{1,0},{2,3},{3,2},{4,5},{5,4},{6,7},{7,6},{8,9},{9,8},{10,11... | collective-permute-start | bytes 147464 | tf_op jit(solution)/shard_map/ppermute | solution.py:139
  70.4 6.5 %copy-start.2 = (f32[2,48,512]{2,1,0:T(8,128)}, f32[2,48,512]{2,1,0:T(8,128)S(1)}, u32[]{:S(2)}) copy-start(f32[2,48,512]{2,1,0:T(8,128)S(1)} %get-tuple-element.11) | copy-start | bytes 589828
  70.5 6.5 %collective-permute-start.3 = (f32[48,512]{1,0:T(8,128)S(1)}, f32[48,512]{1,0:T(8,128)S(1)}, u32[]{:S(2)}, u32[]{:S(2)}) collective-permute-start(f32[48,512]{1,0:T(8,128)S(1)} %get-tuple-element.12), channel_id=1, source_target_pairs={{0,1},{1,0},{2,3},{3,2},{4,5},{5,4},{6,7},{7,6},{8,9},{9,8},{10,11... | collective-permute-start | bytes 294920 | tf_op jit(solution)/shard_map/ppermute | solution.py:161

commit v16 on v15

--- a/solution.py
+++ b/solution.py
@@ -13,49 +13,6 @@
 
 
 masked_score = -1e30
-
-
-def send_target(s, j, n):
-    return (s + j) % n if (s + j) % 2 == 0 else (s - j) % n
-
-
-def blocks_partial(query_heads, block_keys, block_values, draft_k, draft_v, cache_keep, draft_keep, score_scale):
-    scores = (
-        jnp.einsum("qhd,jpd->hqjp", query_heads, block_keys, preferred_element_type=jnp.float32)
-        * score_scale
-    )
-    draft_scores = (
-        jnp.einsum("qhd,td->hqt", query_heads, draft_k, preferred_element_type=jnp.float32)
-        * score_scale
-    )
-    scores = jnp.where(cache_keep[None, None], scores, masked_score)
-    draft_scores = jnp.where(draft_keep[None], draft_scores[:, :, None, :], masked_score)
-    top_score = jnp.maximum(jnp.max(scores, -1), jnp.max(draft_scores, -1))
-    shift_by = jnp.where(top_score > -1e29, top_score, 0.0)
-    cache_weight = jnp.exp(scores - shift_by[..., None])
-    draft_weight = jnp.exp(draft_scores - shift_by[..., None])
-    total = jnp.sum(cache_weight, -1) + jnp.sum(draft_weight, -1)
-    weighted = jnp.einsum(
-        "hqjp,jpd->hqjd",
-        cache_weight.astype(jnp.bfloat16),
-        block_values,
-        preferred_element_type=jnp.float32,
-    )
-    weighted = weighted + jnp.einsum(
-        "hqjt,td->hqjd",
-        draft_weight.astype(jnp.bfloat16),
-        draft_v,
-        preferred_element_type=jnp.float32,
-    )
-    alive = total > 0.0
-    safe_total = jnp.where(alive, total, 1.0)
-    output = lax.reduce_precision(
-        jnp.where(alive[..., None], weighted / safe_total[..., None], 0.0), exponent_bits=8, mantissa_bits=7
-    )
-    lse = jnp.where(alive, top_score + jnp.log(safe_total), masked_score)
-    top = jnp.max(lse, -1)
-    factor = jnp.where(lse > -1e29, jnp.exp(lse - top[..., None]), 0.0)
-    return top, jnp.sum(factor, -1), jnp.sum(factor[..., None] * output, 2)
 
 
 def _dot(a, b, dims):
@@ -126,11 +83,9 @@
     d = lax.axis_index("ctx")
     layers, rows, q_cols = queries.shape
     assert n == KVH * layers
-    kv_cols = draft_keys.shape[2]
     local_len = key_cache.shape[1]
     trees = ancestors.shape[0]
     heads_here = H // n
-    score_scale = 1.0 / math.sqrt(DH)
     own = d % layers
     swap = [(s, s ^ 1) for s in range(n)]
 

time: 78.1 us -> 78.1 us (level)
  no operation moved by 1% of the time
where the time goes in v16:
time: 78.1 us; the launch traced here: 77.6 us
  waiting for transfers between devices  41.7 us (53%)
  starting transfers between devices  28.3 us (36%)
  local copies, waits for them, and re-layouts  5.31 us (7%)
  other arithmetic  1.33 us (2%)
  between operations  0.88 us (1%)
    ppermute x3, waiting for transfers between devices, body(): lax.ppermute(lax.dynamic_index_in_dim(a, other, 0, keepdims=False), 'ctx'...  37 us
    all_to_all x1, starting transfers between devices, body(): blocks = lax.all_to_all(kv, 'ctx', 0, 0, tiled=True)  15.3 us
    ppermute x3, starting transfers between devices, body(): lax.ppermute(lax.dynamic_index_in_dim(a, other, 0, keepdims=False), 'ctx'...  9.66 us
    ppermute x1, starting transfers between devices, body(): got = lax.ppermute(give, 'ctx', swap)  3.36 us
    ppermute x1, waiting for transfers between devices, body(): got = lax.ppermute(give, 'ctx', swap)  3.15 us
    pallas_call x1, local copies, waits for them, and re-layouts, attend(): pl.pallas_call(attend_kernel, out_shape=[jax.ShapeDtypeStruct((rows // he...  2.08 us
    unnamed x15, local copies, waits for them, and re-layouts  1.87 us
    all_to_all x1, waiting for transfers between devices, body(): blocks = lax.all_to_all(kv, 'ctx', 0, 0, tiled=True)  1.57 us
  transfers between devices with their start and end apart: 5, of which 5 were waited for; matrix products, arithmetic and copies ran while one was open for 1% of the time, Pallas kernels for 0%

profile of v16, /device:TPU:6, one launch (start us, length us, event | category | flops | bytes accessed | tf_op | source)
XLA Modules:
  0.0 77.6 jit_solution(6936260873195306774)
XLA Ops:
  0.0 1.0 %copy-done = bf16[2,128,1024]{2,1,0:T(8,128)(2,1)S(1)} copy-done((bf16[2,128,1024]{2,1,0:T(8,128)(2,1)S(1)}, bf16[2,128,1024]{2,1,0:T(8,128)(2,1)}, u32[]{:S(2)}) %copy-start) | copy-done | bytes 524312
  1.0 0.1 copy_bitcast_fusion.1
  1.2 0.1 copy_bitcast_fusion
  1.3 1.1 %pad_maximum_fusion = bf16[16,2,128,128]{3,2,1,0:T(8,128)(2,1)} fusion(bf16[16,1,128,128]{3,2,1,0:T(8,128)(2,1)S(1)} %bitcast.39, bf16[16,1,128,128]{3,2,1,0:T(8,128)(2,1)S(1)} %bitcast.38), kind=kLoop, calls=%fused_computation | loop fusion | flops 524288 | bytes 2097152 | tf_op jit(solution)/shard_map/stack | solution.py:103
  2.4 15.3 %all-to-all-start = ((bf16[16,2,128,128]{3,2,1,0:T(8,128)(2,1)}), bf16[16,2,128,128]{3,2,1,0:T(8,128)(2,1)S(1)}, u32[]{:S(2)}, u32[]{:S(2)}) async-start(bf16[16,2,128,128]{3,2,1,0:T(8,128)(2,1)} %pad_maximum_fusion), calls=%async_computation | async-start | bytes 2097152 | tf_op jit(solution)/shard_map/all_to_all | solution.py:104
  17.8 0.7 copy-done.5
  18.5 3.8 %collective-permute-start.2 = (bf16[48,64]{1,0:T(8,128)(2,1)S(1)}, bf16[48,64]{1,0:T(8,128)(2,1)S(1)}, u32[]{:S(2)}, u32[]{:S(2)}) collective-permute-start(bf16[48,64]{1,0:T(8,128)(2,1)S(1)} %dynamic-slice_bitcast_fusion.1), channel_id=1, source_target_pairs={{0,1},{1,0},{2,3},{3,2},{4,5},{5,4},{6,7},{7,6},{8,9},{9,8},{10,11... | collective-permute-start | bytes 18440 | tf_op jit(solution)/shard_map/ppermute | solution.py:94
  22.4 2.0 %collective-permute-start.1 = (bf16[48,64]{1,0:T(8,128)(2,1)S(1)}, bf16[48,64]{1,0:T(8,128)(2,1)S(1)}, u32[]{:S(2)}, u32[]{:S(2)}) collective-permute-start(bf16[48,64]{1,0:T(8,128)(2,1)S(1)} %dynamic-slice_bitcast_fusion.2), channel_id=1, source_target_pairs={{0,1},{1,0},{2,3},{3,2},{4,5},{5,4},{6,7},{7,6},{8,9},{9,8},{10,11... | collective-permute-start | bytes 18440 | tf_op jit(solution)/shard_map/ppermute | solution.py:94
  24.4 3.8 %collective-permute-start = (bf16[48,512]{1,0:T(8,128)(2,1)S(1)}, bf16[48,512]{1,0:T(8,128)(2,1)S(1)}, u32[]{:S(2)}, u32[]{:S(2)}) collective-permute-start(bf16[48,512]{1,0:T(8,128)(2,1)S(1)} %get-tuple-element.13), channel_id=1, source_target_pairs={{0,1},{1,0},{2,3},{3,2},{4,5},{5,4},{6,7},{7,6},{8,9},{9,8},{10,11... | collective-permute-start | bytes 147464 | tf_op jit(solution)/shard_map/ppermute | solution.py:94
  28.3 0.1 copy.14
  28.4 0.1 broadcast_multiply_fusion
  28.5 0.1 mul.20
  28.6 0.1 tile.17
  28.8 0.1 tile.19
  29.5 36.4 %collective-permute-done.2 = bf16[48,64]{1,0:T(8,128)(2,1)S(1)} collective-permute-done((bf16[48,64]{1,0:T(8,128)(2,1)S(1)}, bf16[48,64]{1,0:T(8,128)(2,1)S(1)}, u32[]{:S(2)}, u32[]{:S(2)}) %collective-permute-start.2) | collective-permute-done | bytes 6176 | tf_op jit(solution)/shard_map/ppermute | solution.py:94
  66.0 0.2 collective-permute-done.1
  66.1 0.1 pad_maximum_fusion.2
  66.2 0.4 collective-permute-done
  66.7 0.1 pad_maximum_fusion.1
  66.8 1.6 %all-to-all-done = bf16[16,2,128,128]{3,2,1,0:T(8,128)(2,1)S(1)} async-done(((bf16[16,2,128,128]{3,2,1,0:T(8,128)(2,1)}), bf16[16,2,128,128]{3,2,1,0:T(8,128)(2,1)S(1)}, u32[]{:S(2)}, u32[]{:S(2)}) %all-to-all-start) | async-done | bytes 1048608 | tf_op jit(solution)/shard_map/all_to_all | solution.py:104
  68.4 2.1 %shard_map.73 = (f32[2,48,512]{2,1,0:T(8,128)S(1)}, f32[48,512]{1,0:T(8,128)S(1)}) fusion(f32[2,48,512]{2,1,0:T(8,128)S(1)} %broadcast_in_dim.11, s32[]{:T(128)S(6)} %select_n.43, s32[1]{0:T(128)S(6)} %copy.21, bf16[384,128]{1,0:T(8,128)(2,1)S(1)} %bitcast.40, bf16[16,2,128,128]{3,2,1,0:T(8,128)(2,1)S(1)} %all-to-all-done, ...), kind=kCustom, calls=%fused_computation.5 | custom fusion | bytes 1441800 | tf_op jit(solution)/shard_map/pallas_call | solution.py:72
  70.5 3.4 %collective-permute-start.3 = (f32[48,512]{1,0:T(8,128)S(1)}, f32[48,512]{1,0:T(8,128)S(1)}, u32[]{:S(2)}, u32[]{:S(2)}) collective-permute-start(f32[48,512]{1,0:T(8,128)S(1)} %get-tuple-element.12), channel_id=1, source_target_pairs={{0,1},{1,0},{2,3},{3,2},{4,5},{5,4},{6,7},{7,6},{8,9},{9,8},{10,11... | collective-permute-start | bytes 294920 | tf_op jit(solution)/shard_map/ppermute | solution.py:116
  73.8 3.1 %collective-permute-done.3 = f32[48,512]{1,0:T(8,128)S(1)} collective-permute-done((f32[48,512]{1,0:T(8,128)S(1)}, f32[48,512]{1,0:T(8,128)S(1)}, u32[]{:S(2)}, u32[]{:S(2)}) %collective-permute-start.3) | collective-permute-done | bytes 98336 | tf_op jit(solution)/shard_map/ppermute | solution.py:116
  77.0 0.6 bitcast_dynamic-update-slice_fusion
  (24 shorter events, 0.2 us)
Async XLA Ops:
  0.0 1.0 %copy-start = (bf16[2,128,1024]{2,1,0:T(8,128)(2,1)S(1)}, bf16[2,128,1024]{2,1,0:T(8,128)(2,1)}, u32[]{:S(2)}) copy-start(bf16[2,128,1024]{2,1,0:T(8,128)(2,1)} %param.8) | copy-start | bytes 1572868
  0.0 1.2 %copy-start.1 = (bf16[2,128,1024]{2,1,0:T(8,128)(2,1)S(1)}, bf16[2,128,1024]{2,1,0:T(8,128)(2,1)}, u32[]{:S(2)}) copy-start(bf16[2,128,1024]{2,1,0:T(8,128)(2,1)} %param.9) | copy-start | bytes 1572868
  2.4 22.0 %copy-start.3 = (bf16[2,48,512]{2,1,0:T(8,128)(2,1)S(1)}, bf16[2,48,512]{2,1,0:T(8,128)(2,1)}, u32[]{:S(2)}) copy-start(bf16[2,48,512]{2,1,0:T(8,128)(2,1)} %param.7) | copy-start | bytes 294916
  2.4 65.9 %all-to-all-start = ((bf16[16,2,128,128]{3,2,1,0:T(8,128)(2,1)}), bf16[16,2,128,128]{3,2,1,0:T(8,128)(2,1)S(1)}, u32[]{:S(2)}, u32[]{:S(2)}) async-start(bf16[16,2,128,128]{3,2,1,0:T(8,128)(2,1)} %pad_maximum_fusion), calls=%async_computation | async-start | bytes 2097152 | tf_op jit(solution)/shard_map/all_to_all | solution.py:104
  17.8 0.7 copy-start.5
  17.8 4.6 %copy-start.6 = (bf16[2,48,64]{2,1,0:T(8,128)(2,1)S(1)}, bf16[2,48,64]{2,1,0:T(8,128)(2,1)}, u32[]{:S(2)}) copy-start(bf16[2,48,64]{2,1,0:T(8,128)(2,1)} %param.10) | copy-start | bytes 36868
  18.5 47.5 %collective-permute-start.2 = (bf16[48,64]{1,0:T(8,128)(2,1)S(1)}, bf16[48,64]{1,0:T(8,128)(2,1)S(1)}, u32[]{:S(2)}, u32[]{:S(2)}) collective-permute-start(bf16[48,64]{1,0:T(8,128)(2,1)S(1)} %dynamic-slice_bitcast_fusion.1), channel_id=1, source_target_pairs={{0,1},{1,0},{2,3},{3,2},{4,5},{5,4},{6,7},{7,6},{8,9},{9,8},{10,11... | collective-permute-start | bytes 18440 | tf_op jit(solution)/shard_map/ppermute | solution.py:94
  22.4 43.8 %collective-permute-start.1 = (bf16[48,64]{1,0:T(8,128)(2,1)S(1)}, bf16[48,64]{1,0:T(8,128)(2,1)S(1)}, u32[]{:S(2)}, u32[]{:S(2)}) collective-permute-start(bf16[48,64]{1,0:T(8,128)(2,1)S(1)} %dynamic-slice_bitcast_fusion.2), channel_id=1, source_target_pairs={{0,1},{1,0},{2,3},{3,2},{4,5},{5,4},{6,7},{7,6},{8,9},{9,8},{10,11... | collective-permute-start | bytes 18440 | tf_op jit(solution)/shard_map/ppermute | solution.py:94
  24.4 3.9 %copy-start.4 = (s32[2,24,24]{2,1,0:T(8,128)S(1)}, s32[2,24,24]{2,1,0:T(8,128)}, u32[]{:S(2)}) copy-start(s32[2,24,24]{2,1,0:T(8,128)} %param.12) | copy-start | bytes 13828
  24.4 42.2 %collective-permute-start = (bf16[48,512]{1,0:T(8,128)(2,1)S(1)}, bf16[48,512]{1,0:T(8,128)(2,1)S(1)}, u32[]{:S(2)}, u32[]{:S(2)}) collective-permute-start(bf16[48,512]{1,0:T(8,128)(2,1)S(1)} %get-tuple-element.13), channel_id=1, source_target_pairs={{0,1},{1,0},{2,3},{3,2},{4,5},{5,4},{6,7},{7,6},{8,9},{9,8},{10,11... | collective-permute-start | bytes 147464 | tf_op jit(solution)/shard_map/ppermute | solution.py:94
  70.4 6.5 %copy-start.2 = (f32[2,48,512]{2,1,0:T(8,128)}, f32[2,48,512]{2,1,0:T(8,128)S(1)}, u32[]{:S(2)}) copy-start(f32[2,48,512]{2,1,0:T(8,128)S(1)} %get-tuple-element.11) | copy-start | bytes 589828
  70.5 6.5 %collective-permute-start.3 = (f32[48,512]{1,0:T(8,128)S(1)}, f32[48,512]{1,0:T(8,128)S(1)}, u32[]{:S(2)}, u32[]{:S(2)}) collective-permute-start(f32[48,512]{1,0:T(8,128)S(1)} %get-tuple-element.12), channel_id=1, source_target_pairs={{0,1},{1,0},{2,3},{3,2},{4,5},{5,4},{6,7},{7,6},{8,9},{9,8},{10,11... | collective-permute-start | bytes 294920 | tf_op jit(solution)/shard_map/ppermute | solution.py:116

commit v17 on v16

--- a/solution.py
+++ b/solution.py
@@ -78,6 +78,28 @@
     )(context_length, *operands)
 
 
+def pack_kernel(k_ref, v_ref, o_ref):
+    layers = k_ref.shape[0]
+    for h in range(k_ref.shape[2] // DH):
+        for l in range(layers):
+            o_ref[h * layers + l, 0] = k_ref[l, :, h * DH:(h + 1) * DH]
+            o_ref[h * layers + l, 1] = v_ref[l, :, h * DH:(h + 1) * DH]
+
+
+def pack(key_cache, value_cache, heads_per_step=2):
+    layers, local_len, width = key_cache.shape
+    steps = width // DH // heads_per_step
+    n = layers * (width // DH)
+    cache_spec = pl.BlockSpec((layers, local_len, heads_per_step * DH), lambda g: (0, 0, g))
+    return pl.pallas_call(
+        pack_kernel,
+        grid=(steps,),
+        out_shape=jax.ShapeDtypeStruct((n, 2, local_len, DH), key_cache.dtype),
+        in_specs=[cache_spec, cache_spec],
+        out_specs=pl.BlockSpec((heads_per_step * layers, 2, local_len, DH), lambda g: (g, 0, 0, 0)),
+    )(key_cache, value_cache)
+
+
 def body(queries, key_cache, value_cache, draft_keys, draft_values, ancestors, context_length):
     n = lax.axis_size("ctx")
     d = lax.axis_index("ctx")
@@ -98,9 +120,7 @@
     first = [jnp.where(own == 0, a, b) for a, b in zip(mine_now, swapped)]
     second = [jnp.where(own == 0, b, a) for a, b in zip(mine_now, swapped)]
 
-    keys_out = jnp.transpose(key_cache.reshape(layers, local_len, KVH, DH), (2, 0, 1, 3))
-    values_out = jnp.transpose(value_cache.reshape(layers, local_len, KVH, DH), (2, 0, 1, 3))
-    kv = jnp.stack([keys_out, values_out], 2).reshape(n, 2, local_len, DH)
+    kv = pack(key_cache, value_cache)
     blocks = lax.all_to_all(kv, "ctx", 0, 0, tiled=True)
 
     tree_keep = (

time: 78.1 us -> 79.2 us (1.014)
  Pallas kernels: 0 us -> 3.48 us
  local copies, waits for them, and re-layouts: 5.31 us -> 4 us
  other arithmetic: 1.33 us -> 0.25 us
    pallas_call x0 -> x1, Pallas kernels: none -> 3.48 us  [pack(): pl.pallas_call(pack_kernel, grid=(steps,), out_shape=jax.ShapeDtypeStruct...]
    another operation x1 -> x0, other arithmetic: 1.08 us -> none  [body(): kv = jnp.stack([keys_out, values_out], 2).reshape(n, 2, local_len, DH)]
    unnamed x15 -> x11, local copies, waits for them, and re-layouts: 1.87 us -> 0.8 us
where the time goes in v17:
time: 79.2 us; the launch traced here: 78.7 us
  waiting for transfers between devices  41.7 us (53%)
  starting transfers between devices  28.3 us (36%)
  local copies, waits for them, and re-layouts  4 us (5%)
  Pallas kernels  3.48 us (4%)
  between operations  0.86 us (1%)
    ppermute x3, waiting for transfers between devices, body(): lax.ppermute(lax.dynamic_index_in_dim(a, other, 0, keepdims=False), 'ctx'...  37 us
    all_to_all x1, starting transfers between devices, body(): blocks = lax.all_to_all(kv, 'ctx', 0, 0, tiled=True)  15.3 us
    ppermute x3, starting transfers between devices, body(): lax.ppermute(lax.dynamic_index_in_dim(a, other, 0, keepdims=False), 'ctx'...  9.66 us
    pallas_call x1, Pallas kernels, pack(): pl.pallas_call(pack_kernel, grid=(steps,), out_shape=jax.ShapeDtypeStruct...  3.48 us
    ppermute x1, starting transfers between devices, body(): got = lax.ppermute(give, 'ctx', swap)  3.36 us
    ppermute x1, waiting for transfers between devices, body(): got = lax.ppermute(give, 'ctx', swap)  3.15 us
    pallas_call x1, local copies, waits for them, and re-layouts, attend(): pl.pallas_call(attend_kernel, out_shape=[jax.ShapeDtypeStruct((rows // he...  2.08 us
  transfers between devices with their start and end apart: 5, of which 5 were waited for; matrix products, arithmetic and copies ran while one was open for 1% of the time, Pallas kernels for 0%

profile of v17, /device:TPU:6, one launch (start us, length us, event | category | flops | bytes accessed | tf_op | source)
XLA Modules:
  0.0 78.7 jit_solution(14669994182117350427)
XLA Ops:
  0.0 3.5 %shard_map.73 = bf16[16,2,128,128]{3,2,1,0:T(8,128)(2,1)} custom-call(bf16[2,128,1024]{2,1,0:T(8,128)(2,1)} %k_ref.1, bf16[2,128,1024]{2,1,0:T(8,128)(2,1)} %v_ref.1), custom_call_target="tpu_custom_call" | custom-call | tf_op jit(solution)/shard_map/pallas_call | solution.py:94
  3.5 15.3 %all-to-all-start = ((bf16[16,2,128,128]{3,2,1,0:T(8,128)(2,1)}), bf16[16,2,128,128]{3,2,1,0:T(8,128)(2,1)S(1)}, u32[]{:S(2)}, u32[]{:S(2)}) async-start(bf16[16,2,128,128]{3,2,1,0:T(8,128)(2,1)} %shard_map.73), calls=%async_computation | async-start | bytes 2097152 | tf_op jit(solution)/shard_map/all_to_all | solution.py:124
  18.8 0.0 copy-start.3
  18.8 0.0 copy-start.4
  18.9 0.7 copy-done.3
  19.6 3.8 %collective-permute-start.2 = (bf16[48,64]{1,0:T(8,128)(2,1)S(1)}, bf16[48,64]{1,0:T(8,128)(2,1)S(1)}, u32[]{:S(2)}, u32[]{:S(2)}) collective-permute-start(bf16[48,64]{1,0:T(8,128)(2,1)S(1)} %dynamic-slice_bitcast_fusion.1), channel_id=1, source_target_pairs={{0,1},{1,0},{2,3},{3,2},{4,5},{5,4},{6,7},{7,6},{8,9},{9,8},{10,11... | collective-permute-start | bytes 18440 | tf_op jit(solution)/shard_map/ppermute | solution.py:116
  23.4 2.0 %collective-permute-start.1 = (bf16[48,64]{1,0:T(8,128)(2,1)S(1)}, bf16[48,64]{1,0:T(8,128)(2,1)S(1)}, u32[]{:S(2)}, u32[]{:S(2)}) collective-permute-start(bf16[48,64]{1,0:T(8,128)(2,1)S(1)} %dynamic-slice_bitcast_fusion.2), channel_id=1, source_target_pairs={{0,1},{1,0},{2,3},{3,2},{4,5},{5,4},{6,7},{7,6},{8,9},{9,8},{10,11... | collective-permute-start | bytes 18440 | tf_op jit(solution)/shard_map/ppermute | solution.py:116
  25.5 0.0 copy-start.2
  25.5 3.8 %collective-permute-start = (bf16[48,512]{1,0:T(8,128)(2,1)S(1)}, bf16[48,512]{1,0:T(8,128)(2,1)S(1)}, u32[]{:S(2)}, u32[]{:S(2)}) collective-permute-start(bf16[48,512]{1,0:T(8,128)(2,1)S(1)} %get-tuple-element.13), channel_id=1, source_target_pairs={{0,1},{1,0},{2,3},{3,2},{4,5},{5,4},{6,7},{7,6},{8,9},{9,8},{10,11... | collective-permute-start | bytes 147464 | tf_op jit(solution)/shard_map/ppermute | solution.py:116
  29.3 0.1 copy.10
  29.4 0.1 broadcast_multiply_fusion
  29.5 0.1 mul.20
  29.7 0.1 tile.17
  29.8 0.1 tile.19
  30.6 36.4 %collective-permute-done.2 = bf16[48,64]{1,0:T(8,128)(2,1)S(1)} collective-permute-done((bf16[48,64]{1,0:T(8,128)(2,1)S(1)}, bf16[48,64]{1,0:T(8,128)(2,1)S(1)}, u32[]{:S(2)}, u32[]{:S(2)}) %collective-permute-start.2) | collective-permute-done | bytes 6176 | tf_op jit(solution)/shard_map/ppermute | solution.py:116
  67.0 0.2 collective-permute-done.1
  67.2 0.1 pad_maximum_fusion.1
  67.3 0.4 collective-permute-done
  67.7 0.1 pad_maximum_fusion
  67.8 1.6 %all-to-all-done = bf16[16,2,128,128]{3,2,1,0:T(8,128)(2,1)S(1)} async-done(((bf16[16,2,128,128]{3,2,1,0:T(8,128)(2,1)}), bf16[16,2,128,128]{3,2,1,0:T(8,128)(2,1)S(1)}, u32[]{:S(2)}, u32[]{:S(2)}) %all-to-all-start) | async-done | bytes 1048608 | tf_op jit(solution)/shard_map/all_to_all | solution.py:124
  69.4 2.1 %shard_map.74 = (f32[2,48,512]{2,1,0:T(8,128)S(1)}, f32[48,512]{1,0:T(8,128)S(1)}) fusion(f32[2,48,512]{2,1,0:T(8,128)S(1)} %broadcast_in_dim.11, s32[]{:T(128)S(6)} %select_n.43, s32[1]{0:T(128)S(6)} %copy.13, bf16[384,128]{1,0:T(8,128)(2,1)S(1)} %bitcast.22, bf16[16,2,128,128]{3,2,1,0:T(8,128)(2,1)S(1)} %all-to-all-done, ...), kind=kCustom, calls=%fused_computation.2 | custom fusion | bytes 1441800 | tf_op jit(solution)/shard_map/pallas_call | solution.py:72
  71.5 3.4 %collective-permute-start.3 = (f32[48,512]{1,0:T(8,128)S(1)}, f32[48,512]{1,0:T(8,128)S(1)}, u32[]{:S(2)}, u32[]{:S(2)}) collective-permute-start(f32[48,512]{1,0:T(8,128)S(1)} %get-tuple-element.12), channel_id=1, source_target_pairs={{0,1},{1,0},{2,3},{3,2},{4,5},{5,4},{6,7},{7,6},{8,9},{9,8},{10,11... | collective-permute-start | bytes 294920 | tf_op jit(solution)/shard_map/ppermute | solution.py:136
  74.9 3.1 %collective-permute-done.3 = f32[48,512]{1,0:T(8,128)S(1)} collective-permute-done((f32[48,512]{1,0:T(8,128)S(1)}, f32[48,512]{1,0:T(8,128)S(1)}, u32[]{:S(2)}, u32[]{:S(2)}) %collective-permute-start.3) | collective-permute-done | bytes 98336 | tf_op jit(solution)/shard_map/ppermute | solution.py:136
  78.0 0.6 bitcast_dynamic-update-slice_fusion
  (18 shorter events, 0.2 us)
Async XLA Ops:
  3.5 22.0 %copy-start.1 = (bf16[2,48,512]{2,1,0:T(8,128)(2,1)S(1)}, bf16[2,48,512]{2,1,0:T(8,128)(2,1)}, u32[]{:S(2)}) copy-start(bf16[2,48,512]{2,1,0:T(8,128)(2,1)} %param.7) | copy-start | bytes 294916
  3.5 65.9 %all-to-all-start = ((bf16[16,2,128,128]{3,2,1,0:T(8,128)(2,1)}), bf16[16,2,128,128]{3,2,1,0:T(8,128)(2,1)S(1)}, u32[]{:S(2)}, u32[]{:S(2)}) async-start(bf16[16,2,128,128]{3,2,1,0:T(8,128)(2,1)} %shard_map.73), calls=%async_computation | async-start | bytes 2097152 | tf_op jit(solution)/shard_map/all_to_all | solution.py:124
  18.8 0.7 copy-start.3
  18.8 4.6 %copy-start.4 = (bf16[2,48,64]{2,1,0:T(8,128)(2,1)S(1)}, bf16[2,48,64]{2,1,0:T(8,128)(2,1)}, u32[]{:S(2)}) copy-start(bf16[2,48,64]{2,1,0:T(8,128)(2,1)} %param.10) | copy-start | bytes 36868
  19.6 47.5 %collective-permute-start.2 = (bf16[48,64]{1,0:T(8,128)(2,1)S(1)}, bf16[48,64]{1,0:T(8,128)(2,1)S(1)}, u32[]{:S(2)}, u32[]{:S(2)}) collective-permute-start(bf16[48,64]{1,0:T(8,128)(2,1)S(1)} %dynamic-slice_bitcast_fusion.1), channel_id=1, source_target_pairs={{0,1},{1,0},{2,3},{3,2},{4,5},{5,4},{6,7},{7,6},{8,9},{9,8},{10,11... | collective-permute-start | bytes 18440 | tf_op jit(solution)/shard_map/ppermute | solution.py:116
  23.4 43.8 %collective-permute-start.1 = (bf16[48,64]{1,0:T(8,128)(2,1)S(1)}, bf16[48,64]{1,0:T(8,128)(2,1)S(1)}, u32[]{:S(2)}, u32[]{:S(2)}) collective-permute-start(bf16[48,64]{1,0:T(8,128)(2,1)S(1)} %dynamic-slice_bitcast_fusion.2), channel_id=1, source_target_pairs={{0,1},{1,0},{2,3},{3,2},{4,5},{5,4},{6,7},{7,6},{8,9},{9,8},{10,11... | collective-permute-start | bytes 18440 | tf_op jit(solution)/shard_map/ppermute | solution.py:116
  25.5 3.9 %copy-start.2 = (s32[2,24,24]{2,1,0:T(8,128)S(1)}, s32[2,24,24]{2,1,0:T(8,128)}, u32[]{:S(2)}) copy-start(s32[2,24,24]{2,1,0:T(8,128)} %param.12) | copy-start | bytes 13828
  25.5 42.2 %collective-permute-start = (bf16[48,512]{1,0:T(8,128)(2,1)S(1)}, bf16[48,512]{1,0:T(8,128)(2,1)S(1)}, u32[]{:S(2)}, u32[]{:S(2)}) collective-permute-start(bf16[48,512]{1,0:T(8,128)(2,1)S(1)} %get-tuple-element.13), channel_id=1, source_target_pairs={{0,1},{1,0},{2,3},{3,2},{4,5},{5,4},{6,7},{7,6},{8,9},{9,8},{10,11... | collective-permute-start | bytes 147464 | tf_op jit(solution)/shard_map/ppermute | solution.py:116
  71.5 6.5 %copy-start = (f32[2,48,512]{2,1,0:T(8,128)}, f32[2,48,512]{2,1,0:T(8,128)S(1)}, u32[]{:S(2)}) copy-start(f32[2,48,512]{2,1,0:T(8,128)S(1)} %get-tuple-element.11) | copy-start | bytes 589828
  71.5 6.5 %collective-permute-start.3 = (f32[48,512]{1,0:T(8,128)S(1)}, f32[48,512]{1,0:T(8,128)S(1)}, u32[]{:S(2)}, u32[]{:S(2)}) collective-permute-start(f32[48,512]{1,0:T(8,128)S(1)} %get-tuple-element.12), channel_id=1, source_target_pairs={{0,1},{1,0},{2,3},{3,2},{4,5},{5,4},{6,7},{7,6},{8,9},{9,8},{10,11... | collective-permute-start | bytes 294920 | tf_op jit(solution)/shard_map/ppermute | solution.py:136
